TPU v7x, 512 devices: a whole 4x8x8 slice. The times are simulated.
512 devices in a mesh: dp: 128 (over y, z, core), owner: 4 (over x).
Axes of the slice: x: 4, y: 8, z: 8, core: 2. Of those that a mesh axis runs over, the one named last changes fastest.
Arguments:
- embeddings: bfloat16 [65536, 1024], P(('dp', 'owner')), may hold values from -120 to 120
- assignment: int32 [65536], P(('dp', 'owner')), may hold values from 0 to 8191, as said below
- pair_list: int32 [8192], replicated, may hold values from 0 to 8191, as said below
Outputs:
- best_similarity: float32 [65536], P(('dp', 'owner'))
Inputs may be any that keep to these rules, and one draw needn't show every extreme that they name: `assignment`: row r's cluster id is (t * n + o) * 16 + c, where n is the number of owner indices, o the owner index of the device holding row r, t an index of dp and c below 16. Among the rows of one device at most 2 share one t, and on every device exactly 2 rows share some t. pair_list[pair_list[k]] = k for every cluster k; cluster k = (t * n + o) * 16 + c and its partner have the same t and different owner indices o.
All inputs are finite; a program needn't handle non-finite values.
Results may differ from a plain program's by a relative error of at most 0.00053.
Values may be sent and summed in bfloat16 or wider, within the bound.
No kernel may reach another device: no remote copies, remote signals or barrier semaphores. Data moves between devices by JAX's collectives and lax.ppermute only.
A program may use at most 64 MiB of HBM per device.

v0:
```python
import jax
import jax.numpy as jnp
from jax import lax
from jax.sharding import PartitionSpec as P

CPD = 16


def shards(embeddings, assignment, pair_list):
    rows, width = embeddings.shape
    n_dp = lax.axis_size("dp")
    n_owner = lax.axis_size("owner")
    capacity = 2 * rows // n_dp
    slots = capacity * n_dp
    values = embeddings.astype(jnp.float32)
    unit = (values * lax.rsqrt(jnp.sum(values * values, axis=1, keepdims=True) + 1e-06)).astype(
        jnp.bfloat16
    )
    target = assignment // (n_owner * CPD)
    onehot = (target[:, None] == jnp.arange(n_dp, dtype=jnp.int32)[None, :]).astype(jnp.int32)
    slot = jnp.sum(jnp.cumsum(onehot, axis=0) * onehot, axis=1) - 1
    position = target * capacity + slot
    here_owner = lax.axis_index("owner")
    here_dp = lax.axis_index("dp")
    first_id = (here_dp * n_owner + here_owner) * CPD
    partners_mine = lax.dynamic_slice_in_dim(pair_list, first_id, CPD)
    start_best = jnp.full((slots,), -1.0, jnp.float32)
    send_rows = jnp.zeros((slots, width), jnp.bfloat16).at[position].set(unit)
    send_ids = jnp.full((slots,), -1, jnp.int32).at[position].set(assignment)
    got_rows, got_ids = (
        lax.all_to_all(
            send_rows.reshape(n_dp, capacity, width), "dp", split_axis=0, concat_axis=0, tiled=True
        ),
        lax.all_to_all(
            send_ids.reshape(n_dp, capacity), "dp", split_axis=0, concat_axis=0, tiled=True
        ),
    )
    mine = got_rows.reshape(slots, width)
    mine_ids = got_ids.reshape(slots)
    local = jnp.clip(mine_ids - first_id, 0, CPD - 1)
    picked = local[:, None] == jnp.arange(CPD, dtype=jnp.int32)[None, :]
    partner = jnp.sum(jnp.where(picked, partners_mine[None, :], 0), axis=1)
    rows_p = lax.all_gather(mine, "owner", axis=0, tiled=True)
    ids_p = lax.all_gather(mine_ids, "owner", axis=0, tiled=True)
    scores = lax.dot_general(
        mine, rows_p, (((1,), (1,)), ((), ())), preferred_element_type=jnp.float32
    )
    column = jnp.arange(ids_p.shape[0], dtype=jnp.int32)
    itself = here_owner * slots + jnp.arange(slots, dtype=jnp.int32)
    same = (
        (mine_ids[:, None] == ids_p[None, :])
        & (ids_p[None, :] >= 0)
        & (itself[:, None] != column[None, :])
    )
    related = same | (partner[:, None] == ids_p[None, :])
    best = jnp.maximum(start_best, jnp.max(jnp.where(related, scores, -1.0), axis=1))
    returned = lax.all_to_all(
        best.reshape(n_dp, capacity), "dp", split_axis=0, concat_axis=0, tiled=True
    )
    return returned.reshape(slots)[position]


def solution(mesh):
    placed = (P(("dp", "owner"), None), P(("dp", "owner")), P())
    return jax.shard_map(
        shards, mesh=mesh, in_specs=placed, out_specs=P(("dp", "owner")), check_vma=False
    )
```

profile of v0, /device:TPU:1, one launch (start us, length us, event | category | flops | bytes accessed | tf_op | source)
XLA Modules:
  0.0 119.6 jit_solution(16147763869348303755)
XLA Ops:
  6.5 0.0 all-gather.3.cloned.1.call-start
  6.5 0.7 and_select_fusion
  7.2 0.1 fusion.9
  7.3 0.2 reduce_window_sum.11
  7.5 0.2 select_reduce_fusion
  7.6 0.7 compare_select_fusion
  8.3 1.1 fusion.3
  9.4 1.8 %scatter_custom_fusion.1 = bf16[256,1024]{1,0:T(8,128)(2,1)S(1)} fusion(s32[128]{0:T(128)S(1)} %compare_select_fusion, bf16[128,1024]{1,0:T(8,128)(2,1)} %param.3, f32[128]{0:T(128)S(1)} %add_rsqrt_fusion, bf16[]{:T(256)} %constant.54.clone.1), kind=kCustom, calls=%fused_computation.12 | custom fusion | flops 393216 | bytes 786946 | tf_op jit(solution)/shard_map/scatter | solution.py:28
  11.2 0.2 reshape.57
  11.4 37.7 %all_to_all.20 = bf16[128,2,1024]{2,1,0:T(2,128)(2,1)S(1)} all-to-all(bf16[128,2,1024]{2,1,0:T(2,128)(2,1)S(1)} %reshape.57), channel_id=1, replica_groups=mesh['dp'=128,'owner'=4] {'dp'}, dimensions={0} | all-to-all | bytes 1048576 | tf_op jit(solution)/shard_map/all_to_all | solution.py:31
  49.1 1.0 reshape.58
  50.1 0.0 all-gather.3.cloned.1.call-update
  50.1 1.1 scatter_custom_fusion
  51.2 0.8 all_to_all.13
  52.0 7.2 %all-to-all-start = ((s32[128,1,2]{2,1,0:T(1,128)}), s32[128,1,2]{2,1,0:T(1,128)S(1)}, u32[]{:S(2)}, u32[]{:S(2)}) async-start(s32[128,1,2]{2,1,0:T(1,128)} %bitcast), calls=%async_computation | async-start | bytes 131072 | tf_op jit(solution)/shard_map/all_to_all | solution.py:34
  59.2 0.8 dynamic_slice.3
  59.9 10.9 %all-to-all-done = s32[128,1,2]{2,1,0:T(1,128)S(1)} async-done(((s32[128,1,2]{2,1,0:T(1,128)}), s32[128,1,2]{2,1,0:T(1,128)S(1)}, u32[]{:S(2)}, u32[]{:S(2)}) %all-to-all-start) | async-done | bytes 1056 | tf_op jit(solution)/shard_map/all_to_all | solution.py:34
  70.8 0.5 broadcast.76
  71.3 0.8 reduce.8
  72.1 0.1 eq.27
  72.3 0.1 reshape.87
  72.4 8.1 %all-gather = s32[4,1,256]{2,1,0:T(1,128)S(1)} all-gather(s32[1,1,256]{2,1,0:T(1,128)S(1)} %reshape.87), channel_id=1, replica_groups=mesh['dp'=128,'owner'=4] {'owner'}, dimensions={0}, use_global_device_ids=true | all-gather | bytes 5120 | tf_op jit(solution)/shard_map/all_gather | solution.py:44
  80.5 0.1 select_reduce_fusion.1
  80.6 0.0 all-gather.3.cloned.1.call-done
  80.7 2.8 %fusion = f32[256]{0:T(256)S(1)} fusion(bf16[256,1024]{1,0:T(8,128)(2,1)} %reshape.58, bf16[1024,1024]{1,0:T(8,128)(2,1)} %all-gather.3.cloned.1.call-done, s32[256]{0:T(256)S(1)} %iota_add_fusion, s32[1024]{0:T(1024)S(1)} %bitcast.8, s32[256]{0:T(256)S(1)} %select_reduce_fusion.1, s32[256]{0:T(256)S(1)} %eq.27, pred[1024]{0:T(1024)(128)(4,1)S(1)} %broadcast_compare_fusion), kind=kOutput, calls=%fused_computation.4 | convolution fusion | flops 538967808 | bytes 2630656 | tf_op jit(solution)/shard_map/dot_general | solution.py:45
  83.5 0.8 max_broadcast_in_dim.15
  84.3 13.7 %all-to-all-start.2 = ((f32[128,1,2]{2,1,0:T(1,128)}), f32[128,1,2]{2,1,0:T(1,128)S(1)}, u32[]{:S(2)}, u32[]{:S(2)}) async-start(f32[128,1,2]{2,1,0:T(1,128)} %bitcast.2), calls=%async_computation.2 | async-start | bytes 131072 | tf_op jit(solution)/shard_map/all_to_all | solution.py:57
  98.0 11.5 %all-to-all-done.2 = f32[128,1,2]{2,1,0:T(1,128)S(1)} async-done(((f32[128,1,2]{2,1,0:T(1,128)}), f32[128,1,2]{2,1,0:T(1,128)S(1)}, u32[]{:S(2)}, u32[]{:S(2)}) %all-to-all-start.2) | async-done | bytes 1056 | tf_op jit(solution)/shard_map/all_to_all | solution.py:57
  109.5 0.5 broadcast.77
  110.1 0.8 reduce.9
  110.9 0.1 reshape.59
  111.0 1.8 %gather_fusion = f32[128]{0:T(128)} fusion(f32[256]{0:T(256)S(1)} %reshape.59, s32[1024]{0:T(1024)S(1)} %pad_clamp_fusion), kind=kCustom, calls=%fused_computation | custom fusion | bytes 1536 | tf_op jit(solution)/shard_map/gather | solution.py:60
  (6 shorter events, 0.0 us)
Async XLA Ops:
  6.5 74.1 %all-gather.3.cloned.1.call-start = ((), (), s32[]{:S(2)}) async-start(), calls=%async_computation.3 | async-start | bytes 2621440 | tf_op jit(solution)/shard_map/all_gather | solution.py:43
  52.0 18.8 %all-to-all-start = ((s32[128,1,2]{2,1,0:T(1,128)}), s32[128,1,2]{2,1,0:T(1,128)S(1)}, u32[]{:S(2)}, u32[]{:S(2)}) async-start(s32[128,1,2]{2,1,0:T(1,128)} %bitcast), calls=%async_computation | async-start | bytes 131072 | tf_op jit(solution)/shard_map/all_to_all | solution.py:34
  84.3 25.3 %all-to-all-start.2 = ((f32[128,1,2]{2,1,0:T(1,128)}), f32[128,1,2]{2,1,0:T(1,128)S(1)}, u32[]{:S(2)}, u32[]{:S(2)}) async-start(f32[128,1,2]{2,1,0:T(1,128)} %bitcast.2), calls=%async_computation.2 | async-start | bytes 131072 | tf_op jit(solution)/shard_map/all_to_all | solution.py:57
Sparse Core Ops, SparseCore 0:
  50.2 29.8 all-gather.2
where the time goes:
time: 120 us
  blocking collectives  45.8 us (38%)
  waiting for transfers between devices  22.4 us (19%)
  starting transfers between devices  20.9 us (17%)
  between operations  13.5 us (11%)
  local copies, waits for them, and re-layouts  7.79 us (6%)
  other arithmetic  6.37 us (5%)
  matrix products  2.82 us (2%)
    all_to_all x1, blocking collectives, shards(): lax.all_to_all(send_rows.reshape(n_dp, capacity, width), 'dp', split_axis...  37.7 us
    all_to_all x1, starting transfers between devices, shards(): lax.all_to_all(best.reshape(n_dp, capacity), 'dp', split_axis=0, concat_a...  13.7 us
    all_to_all x1, waiting for transfers between devices, shards(): lax.all_to_all(best.reshape(n_dp, capacity), 'dp', split_axis=0, concat_a...  11.5 us
    all_to_all x1, waiting for transfers between devices, shards(): lax.all_to_all(send_ids.reshape(n_dp, capacity), 'dp', split_axis=0, conc...  10.9 us
    all_gather x1, blocking collectives, shards(): ids_p = lax.all_gather(mine_ids, 'owner', axis=0, tiled=True)  8.11 us
    all_to_all x1, starting transfers between devices, shards(): lax.all_to_all(send_ids.reshape(n_dp, capacity), 'dp', split_axis=0, conc...  7.16 us
    dot_general x1, matrix products, shards(): lax.dot_general(mine, rows_p, (((1,), (1,)), ((), ())), preferred_element...  2.82 us
  transfers between devices with their start and end apart: 3, of which 2 were waited for; matrix products, arithmetic and copies ran while one was open for 3% of the time, Pallas kernels for 0%

commit v1 on v0

v1 whole, which is shorter than its diff:
```python
import jax
import jax.numpy as jnp
from jax import lax
from jax.sharding import PartitionSpec as P

CPD = 16


def shards(embeddings, assignment, pair_list):
    rows, width = embeddings.shape
    n_dp = lax.axis_size("dp")
    n_owner = lax.axis_size("owner")
    capacity = 2 * rows // n_dp
    slots = capacity * n_dp
    here_owner = lax.axis_index("owner")
    here_dp = lax.axis_index("dp")

    all_ids = lax.all_gather(assignment, ("dp", "owner"), axis=0, tiled=False)
    all_ids = all_ids.reshape(n_dp, n_owner, rows)

    values = embeddings.astype(jnp.float32)
    unit = (values * lax.rsqrt(jnp.sum(values * values, axis=1, keepdims=True) + 1e-06)).astype(
        jnp.bfloat16
    )
    target = assignment // (n_owner * CPD)
    onehot = (target[:, None] == jnp.arange(n_dp, dtype=jnp.int32)[None, :]).astype(jnp.int32)
    slot = jnp.sum(jnp.cumsum(onehot, axis=0) * onehot, axis=1) - 1
    position = target * capacity + slot
    first_id = (here_dp * n_owner + here_owner) * CPD
    partners_mine = lax.dynamic_slice_in_dim(pair_list, first_id, CPD)
    send_rows = jnp.zeros((slots, width), jnp.bfloat16).at[position].set(unit)
    got_rows = lax.all_to_all(
        send_rows.reshape(n_dp, capacity, width), "dp", split_axis=0, concat_axis=0, tiled=True
    )
    mine = got_rows.reshape(slots, width)
    rows_p = lax.all_gather(mine, "owner", axis=0, tiled=True)

    hit = (all_ids // (n_owner * CPD)) == here_dp
    rank = jnp.cumsum(hit.astype(jnp.int32), axis=2) - 1
    which = hit[:, :, :, None] & (
        rank[:, :, :, None] == jnp.arange(capacity, dtype=jnp.int32)[None, None, None, :]
    )
    filled = jnp.any(which, axis=2)
    table = jnp.sum(jnp.where(which, all_ids[:, :, :, None], 0), axis=2)
    table = jnp.where(filled, table, -1)
    ids_p = jnp.transpose(table, (1, 0, 2)).reshape(n_owner * slots)
    mine_ids = lax.dynamic_slice_in_dim(ids_p, here_owner * slots, slots)

    local = jnp.clip(mine_ids - first_id, 0, CPD - 1)
    picked = local[:, None] == jnp.arange(CPD, dtype=jnp.int32)[None, :]
    partner = jnp.sum(jnp.where(picked, partners_mine[None, :], 0), axis=1)
    scores = lax.dot_general(
        mine, rows_p, (((1,), (1,)), ((), ())), preferred_element_type=jnp.float32
    )
    column = jnp.arange(ids_p.shape[0], dtype=jnp.int32)
    itself = here_owner * slots + jnp.arange(slots, dtype=jnp.int32)
    same = (
        (mine_ids[:, None] == ids_p[None, :])
        & (ids_p[None, :] >= 0)
        & (itself[:, None] != column[None, :])
    )
    related = same | (partner[:, None] == ids_p[None, :])
    best = jnp.maximum(-1.0, jnp.max(jnp.where(related, scores, -1.0), axis=1))
    every_best = lax.all_gather(best, "dp", axis=0, tiled=True)
    back = target * slots + here_dp * capacity + slot
    return jnp.take(every_best, back)


def solution(mesh):
    placed = (P(("dp", "owner"), None), P(("dp", "owner")), P())
    return jax.shard_map(
        shards, mesh=mesh, in_specs=placed, out_specs=P(("dp", "owner")), check_vma=False
    )
```

time: 120 us -> 211 us (1.76)
  blocking collectives: 45.8 us -> 184 us
  waiting for transfers between devices: 22.4 us -> 0.03 us
  starting transfers between devices: 20.9 us -> 0.01 us
  local copies, waits for them, and re-layouts: 7.79 us -> 3.92 us
    all_gather x1 -> x2, blocking collectives: 8.11 us -> 147 us  [the longest x1 96.7 us: shards(): all_ids = lax.all_gather(assignment, ('dp', 'owner'), axis=0, tiled=False)]
    all_to_all x2 -> x0, waiting for transfers between devices: 22.4 us -> none  [the longest x1 11.5 us: shards(): lax.all_to_all(best.reshape(n_dp, capacity), 'dp', split_axis=0, concat_a...]
    all_to_all x2 -> x0, starting transfers between devices: 20.9 us -> none  [the longest x1 13.7 us: shards(): lax.all_to_all(best.reshape(n_dp, capacity), 'dp', split_axis=0, concat_a...]
  transfers between devices with their start and end apart: 3 -> 1, of which waited for: 2 -> 0; matrix products, arithmetic and copies ran while one was open for 3% -> 1% of each run, Pallas kernels for 0% -> 0%
where the time goes in v1:
time: 211 us
  blocking collectives  184 us (87%)
  between operations  13.5 us (6%)
  other arithmetic  6.3 us (3%)
  local copies, waits for them, and re-layouts  3.92 us (2%)
  matrix products  2.64 us (1%)
    all_gather x1, blocking collectives, shards(): all_ids = lax.all_gather(assignment, ('dp', 'owner'), axis=0, tiled=False)  96.7 us
    all_gather x1, blocking collectives, shards(): every_best = lax.all_gather(best, 'dp', axis=0, tiled=True)  50.1 us
    all_to_all x1, blocking collectives, shards(): lax.all_to_all(send_rows.reshape(n_dp, capacity, width), 'dp', split_axis...  37.7 us
  transfers between devices with their start and end apart: 1, of which 0 were waited for; matrix products, arithmetic and copies ran while one was open for 1% of the time, Pallas kernels for 0%

profile of v1, /device:TPU:1, one launch (start us, length us, event | category | flops | bytes accessed | tf_op | source)
XLA Modules:
  0.0 210.9 jit_solution(3328990106305142735)
XLA Ops:
  6.5 0.0 all-gather.5.cloned.1.call-start
  6.5 0.7 and_select_fusion.1
  7.2 0.1 fusion.16
  7.3 0.2 reduce_window_sum.22
  7.5 0.2 select_reduce_fusion.1
  7.6 1.1 fusion.3
  8.7 0.7 compare_select_fusion.1
  9.4 0.0 copy-start.1
  9.4 1.8 scatter_custom_fusion
  11.2 0.2 reshape.108
  11.4 37.7 %all_to_all.5 = bf16[128,2,1024]{2,1,0:T(2,128)(2,1)S(1)} all-to-all(bf16[128,2,1024]{2,1,0:T(2,128)(2,1)S(1)} %reshape.108), channel_id=1, replica_groups=mesh['dp'=128,'owner'=4] {'dp'}, dimensions={0} | all-to-all | bytes 1048576 | tf_op jit(solution)/shard_map/all_to_all | solution.py:32
  49.1 1.0 reshape.109
  50.1 0.0 all-gather.5.cloned.1.call-update
  50.1 0.0 copy-start
  50.1 0.0 copy-done.1
  50.2 96.7 %all-gather.1 = s32[512,1,128]{2,1,0:T(1,128)S(1)} all-gather(s32[1,1,128]{2,1,0:T(1,128)S(1)} %bitcast.12), channel_id=2, replica_groups=mesh['dp'=128,'owner'=4] {'dp','owner'}, dimensions={0}, use_global_device_ids=true | all-gather | bytes 262656 | tf_op jit(solution)/shard_map/all_gather | solution.py:18
  146.8 0.2 copy.19
  147.0 0.4 fusion.8
  147.4 0.2 copy.23
  147.6 0.1 broadcast_add_fusion
  147.7 0.1 copy.24
  147.9 0.2 fusion.6
  148.1 0.2 select_reduce_fusion
  148.3 0.1 copy.26
  148.5 0.2 reshape.107
  148.7 0.8 dynamic_slice.7
  149.4 0.1 subtract_clamp_fusion
  149.5 0.1 select_reduce_fusion.2
  149.6 0.0 all-gather.5.cloned.1.call-done
  149.6 0.0 copy-done
  149.6 2.6 %fusion = f32[256]{0:T(256)S(1)} fusion(bf16[256,1024]{1,0:T(8,128)(2,1)S(1)} %copy-done, bf16[1024,1024]{1,0:T(8,128)(2,1)} %all-gather.5.cloned.1.call-done, s32[256]{0:T(256)S(1)} %get-tuple-element.9, s32[1024]{0:T(1024)S(1)} %reshape.107, s32[256]{0:T(256)S(1)} %select_reduce_fusion.2, s32[256]{0:T(256)S(1)} %get-tuple-element.6, ...), kind=kOutput, calls=%fused_computation.3 | convolution fusion | flops 538967808 | bytes 2630656 | tf_op jit(solution)/shard_map/dot_general | solution.py:52
  152.3 50.1 %all-gather.2 = f32[128,1,256]{2,1,0:T(1,128)S(1)} all-gather(f32[1,1,256]{2,1,0:T(1,128)S(1)} %bitcast.11), channel_id=1, replica_groups=mesh['dp'=128,'owner'=4] {'dp'}, dimensions={0}, use_global_device_ids=true | all-gather | bytes 132096 | tf_op jit(solution)/shard_map/all_gather | solution.py:64
  202.4 1.1 gather_fusion
  203.6 0.5 and_select_fusion
  (6 shorter events, 0.1 us)
Async XLA Ops:
  6.5 143.1 %all-gather.5.cloned.1.call-start = ((), (), s32[]{:S(2)}) async-start(), calls=%async_computation.1 | async-start | bytes 2621440 | tf_op jit(solution)/shard_map/all_gather | solution.py:36
  9.4 40.7 %copy-start.1 = (s32[128]{0:T(128)S(1)}, s32[128]{0:T(128)}, u32[]{:S(2)}) copy-start(s32[128]{0:T(128)} %param.4) | copy-start | bytes 1540
  50.1 99.5 %copy-start = (bf16[256,1024]{1,0:T(8,128)(2,1)S(1)}, bf16[256,1024]{1,0:T(8,128)(2,1)}, u32[]{:S(2)}) copy-start(bf16[256,1024]{1,0:T(8,128)(2,1)} %reshape.109) | copy-start | bytes 1572868
Sparse Core Ops, SparseCore 0:
  50.3 29.7 all-gather.4

commit v2 on v0

v2 whole, which is shorter than its diff:
```python
import jax
import jax.numpy as jnp
from jax import lax
from jax.sharding import PartitionSpec as P

CPD = 16
LANES = 128


def shards(embeddings, assignment, pair_list):
    rows, width = embeddings.shape
    n_dp = lax.axis_size("dp")
    n_owner = lax.axis_size("owner")
    capacity = 2 * rows // n_dp
    slots = capacity * n_dp
    here_owner = lax.axis_index("owner")
    here_dp = lax.axis_index("dp")
    values = embeddings.astype(jnp.float32)
    unit = (values * lax.rsqrt(jnp.sum(values * values, axis=1, keepdims=True) + 1e-06)).astype(
        jnp.bfloat16
    )
    target = assignment // (n_owner * CPD)
    onehot = (target[:, None] == jnp.arange(n_dp, dtype=jnp.int32)[None, :]).astype(jnp.int32)
    slot = jnp.sum(jnp.cumsum(onehot, axis=0) * onehot, axis=1) - 1
    position = target * capacity + slot
    first_id = (here_dp * n_owner + here_owner) * CPD
    partners_mine = lax.dynamic_slice_in_dim(pair_list, first_id, CPD)

    code = (assignment % CPD + 1).astype(jnp.bfloat16)
    lane = jnp.arange(LANES, dtype=jnp.int32)
    extra = jnp.where(lane[None, :] == 0, code[:, None], jnp.zeros((), jnp.bfloat16))
    packed = jnp.concatenate([unit, extra], axis=1)
    send = jnp.zeros((slots, width + LANES), jnp.bfloat16).at[position].set(packed)
    got = lax.all_to_all(
        send.reshape(n_dp, capacity, width + LANES), "dp", split_axis=0, concat_axis=0, tiled=True
    ).reshape(slots, width + LANES)

    blocks = [got]
    for k in range(1, n_owner):
        blocks.append(
            lax.ppermute(got, "owner", [(i, (i + k) % n_owner) for i in range(n_owner)])
        )

    def ids_of(block, k):
        c1 = block[:, width].astype(jnp.int32)
        owner_k = (here_owner - k) % n_owner
        return jnp.where(c1 > 0, (here_dp * n_owner + owner_k) * CPD + c1 - 1, -1)

    mine = got[:, :width]
    mine_ids = ids_of(got, 0)
    local = jnp.clip(mine_ids - first_id, 0, CPD - 1)
    picked = local[:, None] == jnp.arange(CPD, dtype=jnp.int32)[None, :]
    partner = jnp.sum(jnp.where(picked, partners_mine[None, :], 0), axis=1)
    itself = jnp.arange(slots, dtype=jnp.int32)
    best = jnp.full((slots,), -1.0, jnp.float32)
    for k, block in enumerate(blocks):
        ids_k = ids_of(block, k)
        scores = lax.dot_general(
            mine, block[:, :width], (((1,), (1,)), ((), ())), preferred_element_type=jnp.float32
        )
        same = (mine_ids[:, None] == ids_k[None, :]) & (ids_k[None, :] >= 0)
        if k == 0:
            same = same & (itself[:, None] != itself[None, :])
        related = same | (partner[:, None] == ids_k[None, :])
        best = jnp.maximum(best, jnp.max(jnp.where(related, scores, -1.0), axis=1))
    returned = lax.all_to_all(
        best.reshape(n_dp, capacity), "dp", split_axis=0, concat_axis=0, tiled=True
    )
    return returned.reshape(slots)[position]


def solution(mesh):
    placed = (P(("dp", "owner"), None), P(("dp", "owner")), P())
    return jax.shard_map(
        shards, mesh=mesh, in_specs=placed, out_specs=P(("dp", "owner")), check_vma=False
    )
```

time: 120 us -> 103 us (0.86)
  blocking collectives: 45.8 us -> 0 us
  waiting for transfers between devices: 22.4 us -> 57.1 us
  starting transfers between devices: 20.9 us -> 34.2 us
  between operations: 13.5 us -> 0.24 us
  other arithmetic: 6.37 us -> 3.56 us
  local copies, waits for them, and re-layouts: 7.79 us -> 5.84 us
  matrix products: 2.82 us -> 1.44 us
    all_to_all x1 -> x0, blocking collectives: 37.7 us -> none  [shards(): lax.all_to_all(send_rows.reshape(n_dp, capacity, width), 'dp', split_axis...]
    ppermute x0 -> x3, waiting for transfers between devices: none -> 25.4 us  [shards(): lax.ppermute(got, 'owner', [(i, (i + k) % n_owner) for i in range(n_owner)])]
    all_to_all x1, starting transfers between devices: 7.16 us -> 18.4 us  [shards(): lax.all_to_all(send.reshape(n_dp, capacity, width + LANES), 'dp', split_a...]
    ppermute x0 -> x3, starting transfers between devices: none -> 9.33 us  [shards(): lax.ppermute(got, 'owner', [(i, (i + k) % n_owner) for i in range(n_owner)])]
    all_to_all x1, waiting for transfers between devices: 10.9 us -> 20.1 us  [shards(): lax.all_to_all(send.reshape(n_dp, capacity, width + LANES), 'dp', split_a...]
    all_gather x1 -> x0, blocking collectives: 8.11 us -> none  [shards(): ids_p = lax.all_gather(mine_ids, 'owner', axis=0, tiled=True)]
    all_to_all x1, starting transfers between devices: 13.7 us -> 6.43 us  [shards(): lax.all_to_all(best.reshape(n_dp, capacity), 'dp', split_axis=0, concat_a...]
    dot_general x1 -> x4, matrix products: 2.82 us -> 1.44 us  [shards(): lax.dot_general(mine, block[:, :width], (((1,), (1,)), ((), ())), preferr...]
  transfers between devices with their start and end apart: 3 -> 5, of which waited for: 2 -> 5; matrix products, arithmetic and copies ran while one was open for 3% -> 2% of each run, Pallas kernels for 0% -> 0%
where the time goes in v2:
time: 103 us; the launch traced here: 102 us
  waiting for transfers between devices  57.1 us (55%)
  starting transfers between devices  34.2 us (33%)
  local copies, waits for them, and re-layouts  5.84 us (6%)
  other arithmetic  3.56 us (3%)
  matrix products  1.44 us (1%)
    ppermute x3, waiting for transfers between devices, shards(): lax.ppermute(got, 'owner', [(i, (i + k) % n_owner) for i in range(n_owner)])  25.4 us
    all_to_all x1, waiting for transfers between devices, shards(): lax.all_to_all(send.reshape(n_dp, capacity, width + LANES), 'dp', split_a...  20.1 us
    all_to_all x1, starting transfers between devices, shards(): lax.all_to_all(send.reshape(n_dp, capacity, width + LANES), 'dp', split_a...  18.4 us
    all_to_all x1, waiting for transfers between devices, shards(): lax.all_to_all(best.reshape(n_dp, capacity), 'dp', split_axis=0, concat_a...  11.5 us
    ppermute x3, starting transfers between devices, shards(): lax.ppermute(got, 'owner', [(i, (i + k) % n_owner) for i in range(n_owner)])  9.33 us
    all_to_all x1, starting transfers between devices, shards(): lax.all_to_all(best.reshape(n_dp, capacity), 'dp', split_axis=0, concat_a...  6.43 us
  transfers between devices with their start and end apart: 5, of which 5 were waited for; matrix products, arithmetic and copies ran while one was open for 2% of the time, Pallas kernels for 0%

profile of v2, /device:TPU:1, one launch (start us, length us, event | category | flops | bytes accessed | tf_op | source)
XLA Modules:
  0.0 102.3 jit_solution(14655646186655151228)
XLA Ops:
  0.0 0.0 copy-start.1
  0.0 0.0 copy-start
  0.0 0.6 copy-done.1
  0.7 0.1 fusion.32
  0.8 0.2 reduce_window_sum.11
  0.9 0.2 select_reduce_fusion
  1.1 0.0 copy-done
  1.1 0.1 fusion.4
  1.3 0.1 fusion.5
  1.4 0.1 broadcast_select_fusion
  1.5 1.3 %scatter_custom_fusion = bf16[256,1152]{1,0:T(8,128)(2,1)S(1)} fusion(s32[128]{0:T(128)S(1)} %compare_select_fusion, bf16[128,128]{1,0:T(8,128)(2,1)S(1)} %broadcast_select_fusion, bf16[]{:T(256)} %constant.118, bf16[128,1024]{1,0:T(8,128)(2,1)S(1)} %fusion.5, bf16[]{:T(256)} %constant.87.clone.1), kind=kCustom, calls=%fused_computation.21 | custom fusion | flops 589824 | bytes 884740 | tf_op jit(solution)/shard_map/scatter | solution.py:33
  2.8 1.0 %reshape.169 = bf16[128,2,1152]{2,1,0:T(2,128)(2,1)} reshape(bf16[256,1152]{1,0:T(8,128)(2,1)S(1)} %scatter_custom_fusion) | data formatting | bytes 1179648 | tf_op jit(solution)/shard_map/reshape | solution.py:35
  3.9 18.4 %all-to-all-start = ((bf16[128,2,1152]{2,1,0:T(2,128)(2,1)}), bf16[128,2,1152]{2,1,0:T(2,128)(2,1)S(1)}, u32[]{:S(2)}, u32[]{:S(2)}) async-start(bf16[128,2,1152]{2,1,0:T(2,128)(2,1)} %reshape.169), calls=%async_computation | async-start | bytes 1179648 | tf_op jit(solution)/shard_map/all_to_all | solution.py:34
  22.4 0.8 dynamic_slice.3
  23.1 20.1 %all-to-all-done = bf16[128,2,1152]{2,1,0:T(2,128)(2,1)S(1)} async-done(((bf16[128,2,1152]{2,1,0:T(2,128)(2,1)}), bf16[128,2,1152]{2,1,0:T(2,128)(2,1)S(1)}, u32[]{:S(2)}, u32[]{:S(2)}) %all-to-all-start) | async-done | bytes 589856 | tf_op jit(solution)/shard_map/all_to_all | solution.py:34
  43.2 0.2 reshape.170
  43.4 4.4 %collective-permute-start.2 = (bf16[256,1152]{1,0:T(8,128)(2,1)S(1)}, bf16[256,1152]{1,0:T(8,128)(2,1)S(1)}, u32[]{:S(2)}, u32[]{:S(2)}) collective-permute-start(bf16[256,1152]{1,0:T(8,128)(2,1)S(1)} %reshape.170), channel_id=1, source_target_pairs={{0,3},{1,0},{2,1},{3,2},{4,7},{5,4},{6,5},{7,6},{8,11},{9,8},{10,9... | collective-permute-start | bytes 1769480 | tf_op jit(solution)/shard_map/ppermute | solution.py:41
  47.8 2.4 %collective-permute-start.1 = (bf16[256,1152]{1,0:T(8,128)(2,1)S(1)}, bf16[256,1152]{1,0:T(8,128)(2,1)S(1)}, u32[]{:S(2)}, u32[]{:S(2)}) collective-permute-start(bf16[256,1152]{1,0:T(8,128)(2,1)S(1)} %reshape.170), channel_id=1, source_target_pairs={{0,2},{1,3},{2,0},{3,1},{4,6},{5,7},{6,4},{7,5},{8,10},{9,11},{10,... | collective-permute-start | bytes 1769480 | tf_op jit(solution)/shard_map/ppermute | solution.py:41
  50.3 2.5 %collective-permute-start = (bf16[256,1152]{1,0:T(8,128)(2,1)S(1)}, bf16[256,1152]{1,0:T(8,128)(2,1)S(1)}, u32[]{:S(2)}, u32[]{:S(2)}) collective-permute-start(bf16[256,1152]{1,0:T(8,128)(2,1)S(1)} %reshape.170), channel_id=1, source_target_pairs={{0,1},{1,2},{2,3},{3,0},{4,5},{5,6},{6,7},{7,4},{8,9},{9,10},{10,1... | collective-permute-start | bytes 1769480 | tf_op jit(solution)/shard_map/ppermute | solution.py:41
  52.8 0.2 fusion.31
  52.9 0.1 select_reduce_fusion.1
  53.0 0.4 fusion
  53.4 5.8 %collective-permute-done.2 = bf16[256,1152]{1,0:T(8,128)(2,1)S(1)} collective-permute-done((bf16[256,1152]{1,0:T(8,128)(2,1)S(1)}, bf16[256,1152]{1,0:T(8,128)(2,1)S(1)}, u32[]{:S(2)}, u32[]{:S(2)}) %collective-permute-start.2) | collective-permute-done | bytes 589856 | tf_op jit(solution)/shard_map/ppermute | solution.py:41
  59.2 0.1 fusion.30
  59.3 4.5 %collective-permute-done.1 = bf16[256,1152]{1,0:T(8,128)(2,1)S(1)} collective-permute-done((bf16[256,1152]{1,0:T(8,128)(2,1)S(1)}, bf16[256,1152]{1,0:T(8,128)(2,1)S(1)}, u32[]{:S(2)}, u32[]{:S(2)}) %collective-permute-start.1) | collective-permute-done | bytes 589856 | tf_op jit(solution)/shard_map/ppermute | solution.py:41
  63.8 0.1 fusion.27
  63.9 15.2 %collective-permute-done = bf16[256,1152]{1,0:T(8,128)(2,1)S(1)} collective-permute-done((bf16[256,1152]{1,0:T(8,128)(2,1)S(1)}, bf16[256,1152]{1,0:T(8,128)(2,1)S(1)}, u32[]{:S(2)}, u32[]{:S(2)}) %collective-permute-start) | collective-permute-done | bytes 589856 | tf_op jit(solution)/shard_map/ppermute | solution.py:41
  79.1 0.1 fusion.24
  79.2 0.4 fusion.3
  79.6 0.3 fusion.2
  80.0 0.4 fusion.1
  80.3 0.8 max.45
  81.1 6.4 %all-to-all-start.1 = ((f32[128,1,2]{2,1,0:T(1,128)}), f32[128,1,2]{2,1,0:T(1,128)S(1)}, u32[]{:S(2)}, u32[]{:S(2)}) async-start(f32[128,1,2]{2,1,0:T(1,128)} %bitcast), calls=%async_computation.1 | async-start | bytes 131072 | tf_op jit(solution)/shard_map/all_to_all | solution.py:66
  87.5 11.5 %all-to-all-done.1 = f32[128,1,2]{2,1,0:T(1,128)S(1)} async-done(((f32[128,1,2]{2,1,0:T(1,128)}), f32[128,1,2]{2,1,0:T(1,128)S(1)}, u32[]{:S(2)}, u32[]{:S(2)}) %all-to-all-start.1) | async-done | bytes 1056 | tf_op jit(solution)/shard_map/all_to_all | solution.py:66
  99.1 0.5 broadcast.270
  99.6 0.8 reduce.13
  100.4 0.1 reshape.171
  100.5 1.8 %gather_fusion = f32[128]{0:T(128)} fusion(f32[256]{0:T(256)S(1)} %reshape.171, s32[1024]{0:T(1024)S(1)} %pad_clamp_fusion), kind=kCustom, calls=%fused_computation | custom fusion | bytes 1536 | tf_op jit(solution)/shard_map/gather | solution.py:69
  (10 shorter events, 0.1 us)
Async XLA Ops:
  0.0 0.7 copy-start.1
  0.0 1.1 %copy-start = (bf16[128,1024]{1,0:T(8,128)(2,1)S(1)}, bf16[128,1024]{1,0:T(8,128)(2,1)}, u32[]{:S(2)}) copy-start(bf16[128,1024]{1,0:T(8,128)(2,1)} %param.3) | copy-start | bytes 786436
  3.9 39.3 %all-to-all-start = ((bf16[128,2,1152]{2,1,0:T(2,128)(2,1)}), bf16[128,2,1152]{2,1,0:T(2,128)(2,1)S(1)}, u32[]{:S(2)}, u32[]{:S(2)}) async-start(bf16[128,2,1152]{2,1,0:T(2,128)(2,1)} %reshape.169), calls=%async_computation | async-start | bytes 1179648 | tf_op jit(solution)/shard_map/all_to_all | solution.py:34
  43.4 15.8 %collective-permute-start.2 = (bf16[256,1152]{1,0:T(8,128)(2,1)S(1)}, bf16[256,1152]{1,0:T(8,128)(2,1)S(1)}, u32[]{:S(2)}, u32[]{:S(2)}) collective-permute-start(bf16[256,1152]{1,0:T(8,128)(2,1)S(1)} %reshape.170), channel_id=1, source_target_pairs={{0,3},{1,0},{2,1},{3,2},{4,7},{5,4},{6,5},{7,6},{8,11},{9,8},{10,9... | collective-permute-start | bytes 1769480 | tf_op jit(solution)/shard_map/ppermute | solution.py:41
  47.8 15.9 %collective-permute-start.1 = (bf16[256,1152]{1,0:T(8,128)(2,1)S(1)}, bf16[256,1152]{1,0:T(8,128)(2,1)S(1)}, u32[]{:S(2)}, u32[]{:S(2)}) collective-permute-start(bf16[256,1152]{1,0:T(8,128)(2,1)S(1)} %reshape.170), channel_id=1, source_target_pairs={{0,2},{1,3},{2,0},{3,1},{4,6},{5,7},{6,4},{7,5},{8,10},{9,11},{10,... | collective-permute-start | bytes 1769480 | tf_op jit(solution)/shard_map/ppermute | solution.py:41
  50.3 28.9 %collective-permute-start = (bf16[256,1152]{1,0:T(8,128)(2,1)S(1)}, bf16[256,1152]{1,0:T(8,128)(2,1)S(1)}, u32[]{:S(2)}, u32[]{:S(2)}) collective-permute-start(bf16[256,1152]{1,0:T(8,128)(2,1)S(1)} %reshape.170), channel_id=1, source_target_pairs={{0,1},{1,2},{2,3},{3,0},{4,5},{5,6},{6,7},{7,4},{8,9},{9,10},{10,1... | collective-permute-start | bytes 1769480 | tf_op jit(solution)/shard_map/ppermute | solution.py:41
  81.1 18.0 %all-to-all-start.1 = ((f32[128,1,2]{2,1,0:T(1,128)}), f32[128,1,2]{2,1,0:T(1,128)S(1)}, u32[]{:S(2)}, u32[]{:S(2)}) async-start(f32[128,1,2]{2,1,0:T(1,128)} %bitcast), calls=%async_computation.1 | async-start | bytes 131072 | tf_op jit(solution)/shard_map/all_to_all | solution.py:66

commit v3 on v2

v3 whole, which is shorter than its diff:
```python
import jax
import jax.numpy as jnp
from jax import lax
from jax.sharding import PartitionSpec as P

CPD = 16
LANES = 128


def shards(embeddings, assignment, pair_list):
    rows, width = embeddings.shape
    n_dp = lax.axis_size("dp")
    n_owner = lax.axis_size("owner")
    assert n_owner == 4
    capacity = 2 * rows // n_dp
    slots = capacity * n_dp
    here_owner = lax.axis_index("owner")
    here_dp = lax.axis_index("dp")
    values = embeddings.astype(jnp.float32)
    unit = (values * lax.rsqrt(jnp.sum(values * values, axis=1, keepdims=True) + 1e-06)).astype(
        jnp.bfloat16
    )
    target = assignment // (n_owner * CPD)
    onehot = (target[:, None] == jnp.arange(n_dp, dtype=jnp.int32)[None, :]).astype(jnp.int32)
    slot = jnp.sum(jnp.cumsum(onehot, axis=0) * onehot, axis=1) - 1
    position = target * capacity + slot
    first_id = (here_dp * n_owner + here_owner) * CPD

    code = (assignment % CPD + 1).astype(jnp.bfloat16)
    lane = jnp.arange(LANES, dtype=jnp.int32)
    extra = jnp.where(lane[None, :] == 0, code[:, None], jnp.zeros((), jnp.bfloat16))
    packed = jnp.concatenate([unit, extra], axis=1)
    send = jnp.zeros((slots, width + LANES), jnp.bfloat16).at[position].set(packed)
    got = lax.all_to_all(
        send.reshape(n_dp, capacity, width + LANES), "dp", split_axis=0, concat_axis=0, tiled=True
    ).reshape(slots, width + LANES)

    mine = got[:, :width]
    c1 = got[:, width].astype(jnp.int32)
    mine_ids = jnp.where(c1 > 0, first_id + c1 - 1, -1)

    to_next = [(i, (i + 1) % n_owner) for i in range(n_owner)]
    to_prev = [(i, (i - 1) % n_owner) for i in range(n_owner)]
    rows_l = lax.ppermute(mine, "owner", to_next)
    ids_l = lax.ppermute(mine_ids, "owner", to_next)
    rows_r = lax.ppermute(mine, "owner", to_prev)
    ids_r = lax.ppermute(mine_ids, "owner", to_prev)

    def partner_of(ids, owner_index):
        base = (here_dp * n_owner + owner_index) * CPD
        partners = lax.dynamic_slice_in_dim(pair_list, base, CPD)
        local = jnp.clip(ids - base, 0, CPD - 1)
        picked = local[:, None] == jnp.arange(CPD, dtype=jnp.int32)[None, :]
        return jnp.sum(jnp.where(picked, partners[None, :], 0), axis=1)

    def best_against(rows_a, ids_a, partner_a, rows_b, ids_b, itself):
        scores = lax.dot_general(
            rows_a, rows_b, (((1,), (1,)), ((), ())), preferred_element_type=jnp.float32
        )
        same = (ids_a[:, None] == ids_b[None, :]) & (ids_b[None, :] >= 0)
        if itself:
            column = jnp.arange(slots, dtype=jnp.int32)
            same = same & (column[:, None] != column[None, :])
        related = same | (partner_a[:, None] == ids_b[None, :])
        return jnp.max(jnp.where(related, scores, -1.0), axis=1)

    partner = partner_of(mine_ids, here_owner)
    partner_l = partner_of(ids_l, (here_owner - 1) % n_owner)
    far = best_against(rows_l, ids_l, partner_l, rows_r, ids_r, False)
    far_back = lax.ppermute(far, "owner", to_prev)
    best = jnp.maximum(
        jnp.maximum(-1.0, best_against(mine, mine_ids, partner, mine, mine_ids, True)),
        jnp.maximum(
            best_against(mine, mine_ids, partner, rows_l, ids_l, False),
            best_against(mine, mine_ids, partner, rows_r, ids_r, False),
        ),
    )
    best = jnp.maximum(best, far_back)
    returned = lax.all_to_all(
        best.reshape(n_dp, capacity), "dp", split_axis=0, concat_axis=0, tiled=True
    )
    return returned.reshape(slots)[position]


def solution(mesh):
    placed = (P(("dp", "owner"), None), P(("dp", "owner")), P())
    return jax.shard_map(
        shards, mesh=mesh, in_specs=placed, out_specs=P(("dp", "owner")), check_vma=False
    )
```

time: 103 us -> 98 us (0.951)
  waiting for transfers between devices: 57.1 us -> 39.3 us
  starting transfers between devices: 34.2 us -> 47.3 us
    ppermute x3 -> x5, waiting for transfers between devices: 25.4 us -> 7.73 us  [the longest x1 6.82 us: shards(): rows_l = lax.ppermute(mine, 'owner', to_next)]
    ppermute x3 -> x5, starting transfers between devices: 9.33 us -> 18.3 us  [the longest x1 5.32 us: shards(): far_back = lax.ppermute(far, 'owner', to_prev)]
    all_to_all x1, starting transfers between devices: 6.43 us -> 10.6 us  [shards(): lax.all_to_all(best.reshape(n_dp, capacity), 'dp', split_axis=0, concat_a...]
  transfers between devices with their start and end apart: 5 -> 7, of which waited for: 5 -> 4; matrix products, arithmetic and copies ran while one was open for 2% -> 2% of each run, Pallas kernels for 0% -> 0%
where the time goes in v3:
time: 98 us; the launch traced here: 97.6 us
  starting transfers between devices  47.3 us (48%)
  waiting for transfers between devices  39.3 us (40%)
  local copies, waits for them, and re-layouts  5.97 us (6%)
  other arithmetic  3.31 us (3%)
  matrix products  1.43 us (1%)
    all_to_all x1, waiting for transfers between devices, shards(): lax.all_to_all(send.reshape(n_dp, capacity, width + LANES), 'dp', split_a...  20 us
    all_to_all x1, starting transfers between devices, shards(): lax.all_to_all(send.reshape(n_dp, capacity, width + LANES), 'dp', split_a...  18.4 us
    all_to_all x1, waiting for transfers between devices, shards(): lax.all_to_all(best.reshape(n_dp, capacity), 'dp', split_axis=0, concat_a...  11.5 us
    all_to_all x1, starting transfers between devices, shards(): lax.all_to_all(best.reshape(n_dp, capacity), 'dp', split_axis=0, concat_a...  10.6 us
    ppermute x1, waiting for transfers between devices, shards(): rows_l = lax.ppermute(mine, 'owner', to_next)  6.82 us
    ppermute x1, starting transfers between devices, shards(): far_back = lax.ppermute(far, 'owner', to_prev)  5.32 us
    ppermute x1, starting transfers between devices, shards(): rows_r = lax.ppermute(mine, 'owner', to_prev)  4.57 us
    ppermute x1, starting transfers between devices, shards(): ids_r = lax.ppermute(mine_ids, 'owner', to_prev)  3.37 us
  transfers between devices with their start and end apart: 7, of which 4 were waited for; matrix products, arithmetic and copies ran while one was open for 2% of the time, Pallas kernels for 0%

profile of v3, /device:TPU:1, one launch (start us, length us, event | category | flops | bytes accessed | tf_op | source)
XLA Modules:
  0.0 97.6 jit_solution(2457652010713929327)
XLA Ops:
  0.0 0.0 copy-start.1
  0.0 0.0 copy-start
  0.0 0.6 copy-done.1
  0.7 0.1 fusion.13
  0.8 0.2 reduce_window_sum.11
  0.9 0.2 select_reduce_fusion.3
  1.1 0.0 copy-done
  1.1 0.1 fusion.1
  1.3 0.1 fusion.2
  1.4 0.1 broadcast_select_fusion
  1.5 1.3 %scatter_custom_fusion = bf16[256,1152]{1,0:T(8,128)(2,1)S(1)} fusion(s32[128]{0:T(128)S(1)} %compare_select_fusion, bf16[128,128]{1,0:T(8,128)(2,1)S(1)} %broadcast_select_fusion, bf16[]{:T(256)} %constant.92, bf16[128,1024]{1,0:T(8,128)(2,1)S(1)} %fusion.2, bf16[]{:T(256)} %constant.38.clone.1), kind=kCustom, calls=%fused_computation.8 | custom fusion | flops 589824 | bytes 884740 | tf_op jit(solution)/shard_map/scatter | solution.py:33
  2.8 1.0 %reshape.62 = bf16[128,2,1152]{2,1,0:T(2,128)(2,1)} reshape(bf16[256,1152]{1,0:T(8,128)(2,1)S(1)} %scatter_custom_fusion) | data formatting | bytes 1179648 | tf_op jit(solution)/shard_map/reshape | solution.py:35
  3.9 18.4 %all-to-all-start = ((bf16[128,2,1152]{2,1,0:T(2,128)(2,1)}), bf16[128,2,1152]{2,1,0:T(2,128)(2,1)S(1)}, u32[]{:S(2)}, u32[]{:S(2)}) async-start(bf16[128,2,1152]{2,1,0:T(2,128)(2,1)} %reshape.62), calls=%async_computation | async-start | bytes 1179648 | tf_op jit(solution)/shard_map/all_to_all | solution.py:34
  22.3 0.8 fusion.25
  23.2 20.0 %all-to-all-done = bf16[128,2,1152]{2,1,0:T(2,128)(2,1)S(1)} async-done(((bf16[128,2,1152]{2,1,0:T(2,128)(2,1)}), bf16[128,2,1152]{2,1,0:T(2,128)(2,1)S(1)}, u32[]{:S(2)}, u32[]{:S(2)}) %all-to-all-start) | async-done | bytes 589856 | tf_op jit(solution)/shard_map/all_to_all | solution.py:34
  43.2 0.2 reshape.63
  43.4 0.2 clamp_reduce_fusion
  43.6 3.1 %collective-permute-start = (s32[256]{0:T(256)S(1)}, s32[256]{0:T(256)S(1)}, u32[]{:S(2)}, u32[]{:S(2)}) collective-permute-start(s32[256]{0:T(256)S(1)} %get-tuple-element.6), channel_id=1, source_target_pairs={{0,1},{1,2},{2,3},{3,0},{4,5},{5,6},{6,7},{7,4},{8,9},{9,10},{10,1... | collective-permute-start | bytes 3080 | tf_op jit(solution)/shard_map/ppermute | solution.py:45
  46.7 3.4 %collective-permute-start.2 = (s32[256]{0:T(256)S(1)}, s32[256]{0:T(256)S(1)}, u32[]{:S(2)}, u32[]{:S(2)}) collective-permute-start(s32[256]{0:T(256)S(1)} %get-tuple-element.6), channel_id=1, source_target_pairs={{0,3},{1,0},{2,1},{3,2},{4,7},{5,4},{6,5},{7,6},{8,11},{9,8},{10,9... | collective-permute-start | bytes 3080 | tf_op jit(solution)/shard_map/ppermute | solution.py:47
  50.1 0.1 slice.11
  50.2 1.9 %collective-permute-start.1 = (bf16[256,1024]{1,0:T(8,128)(2,1)S(1)}, bf16[256,1024]{1,0:T(8,128)(2,1)S(1)}, u32[]{:S(2)}, u32[]{:S(2)}) collective-permute-start(bf16[256,1024]{1,0:T(8,128)(2,1)S(1)} %slice.11), channel_id=1, source_target_pairs={{0,1},{1,2},{2,3},{3,0},{4,5},{5,6},{6,7},{7,4},{8,9},{9,10},{10,1... | collective-permute-start | bytes 1572872 | tf_op jit(solution)/shard_map/ppermute | solution.py:44
  52.1 4.6 %collective-permute-start.3 = (bf16[256,1024]{1,0:T(8,128)(2,1)S(1)}, bf16[256,1024]{1,0:T(8,128)(2,1)S(1)}, u32[]{:S(2)}, u32[]{:S(2)}) collective-permute-start(bf16[256,1024]{1,0:T(8,128)(2,1)S(1)} %slice.11), channel_id=1, source_target_pairs={{0,3},{1,0},{2,1},{3,2},{4,7},{5,4},{6,5},{7,6},{8,11},{9,8},{10,9... | collective-permute-start | bytes 1572872 | tf_op jit(solution)/shard_map/ppermute | solution.py:46
  56.7 0.1 select_reduce_fusion.5
  56.8 0.4 fusion
  57.2 0.0 collective-permute-done
  57.2 0.1 select_reduce_fusion.4
  57.3 0.0 collective-permute-done.2
  57.3 6.8 %collective-permute-done.1 = bf16[256,1024]{1,0:T(8,128)(2,1)S(1)} collective-permute-done((bf16[256,1024]{1,0:T(8,128)(2,1)S(1)}, bf16[256,1024]{1,0:T(8,128)(2,1)S(1)}, u32[]{:S(2)}, u32[]{:S(2)}) %collective-permute-start.1) | collective-permute-done | bytes 524320 | tf_op jit(solution)/shard_map/ppermute | solution.py:44
  64.1 0.9 collective-permute-done.3
  65.0 0.4 select_reduce_fusion
  65.4 5.3 %collective-permute-start.4 = (f32[256]{0:T(256)S(1)}, f32[256]{0:T(256)S(1)}, u32[]{:S(2)}, u32[]{:S(2)}) collective-permute-start(f32[256]{0:T(256)S(1)} %select_reduce_fusion), channel_id=1, source_target_pairs={{0,3},{1,0},{2,1},{3,2},{4,7},{5,4},{6,5},{7,6},{8,11},{9,8},{10,9... | collective-permute-start | bytes 3080 | tf_op jit(solution)/shard_map/ppermute | solution.py:70
  70.7 0.4 select_reduce_fusion.1
  71.0 0.4 select_reduce_fusion.2
  71.4 0.0 collective-permute-done.4
  71.4 0.8 all_to_all.10
  72.2 10.6 %all-to-all-start.1 = ((f32[128,1,2]{2,1,0:T(1,128)}), f32[128,1,2]{2,1,0:T(1,128)S(1)}, u32[]{:S(2)}, u32[]{:S(2)}) async-start(f32[128,1,2]{2,1,0:T(1,128)} %bitcast), calls=%async_computation.1 | async-start | bytes 131072 | tf_op jit(solution)/shard_map/all_to_all | solution.py:79
  82.8 11.5 %all-to-all-done.1 = f32[128,1,2]{2,1,0:T(1,128)S(1)} async-done(((f32[128,1,2]{2,1,0:T(1,128)}), f32[128,1,2]{2,1,0:T(1,128)S(1)}, u32[]{:S(2)}, u32[]{:S(2)}) %all-to-all-start.1) | async-done | bytes 1056 | tf_op jit(solution)/shard_map/all_to_all | solution.py:79
  94.3 0.5 broadcast.127
  94.8 0.8 reduce.7
  95.6 0.1 reshape.64
  95.8 1.8 %gather_fusion = f32[128]{0:T(128)} fusion(f32[256]{0:T(256)S(1)} %reshape.64, s32[1024]{0:T(1024)S(1)} %pad_clamp_fusion), kind=kCustom, calls=%fused_computation | custom fusion | bytes 1536 | tf_op jit(solution)/shard_map/gather | solution.py:82
  (10 shorter events, 0.1 us)
Async XLA Ops:
  0.0 0.7 copy-start.1
  0.0 1.1 %copy-start = (bf16[128,1024]{1,0:T(8,128)(2,1)S(1)}, bf16[128,1024]{1,0:T(8,128)(2,1)}, u32[]{:S(2)}) copy-start(bf16[128,1024]{1,0:T(8,128)(2,1)} %param.3) | copy-start | bytes 786436
  3.9 39.3 %all-to-all-start = ((bf16[128,2,1152]{2,1,0:T(2,128)(2,1)}), bf16[128,2,1152]{2,1,0:T(2,128)(2,1)S(1)}, u32[]{:S(2)}, u32[]{:S(2)}) async-start(bf16[128,2,1152]{2,1,0:T(2,128)(2,1)} %reshape.62), calls=%async_computation | async-start | bytes 1179648 | tf_op jit(solution)/shard_map/all_to_all | solution.py:34
  43.6 13.6 %collective-permute-start = (s32[256]{0:T(256)S(1)}, s32[256]{0:T(256)S(1)}, u32[]{:S(2)}, u32[]{:S(2)}) collective-permute-start(s32[256]{0:T(256)S(1)} %get-tuple-element.6), channel_id=1, source_target_pairs={{0,1},{1,2},{2,3},{3,0},{4,5},{5,6},{6,7},{7,4},{8,9},{9,10},{10,1... | collective-permute-start | bytes 3080 | tf_op jit(solution)/shard_map/ppermute | solution.py:45
  46.7 10.5 %collective-permute-start.2 = (s32[256]{0:T(256)S(1)}, s32[256]{0:T(256)S(1)}, u32[]{:S(2)}, u32[]{:S(2)}) collective-permute-start(s32[256]{0:T(256)S(1)} %get-tuple-element.6), channel_id=1, source_target_pairs={{0,3},{1,0},{2,1},{3,2},{4,7},{5,4},{6,5},{7,6},{8,11},{9,8},{10,9... | collective-permute-start | bytes 3080 | tf_op jit(solution)/shard_map/ppermute | solution.py:47
  50.2 13.9 %collective-permute-start.1 = (bf16[256,1024]{1,0:T(8,128)(2,1)S(1)}, bf16[256,1024]{1,0:T(8,128)(2,1)S(1)}, u32[]{:S(2)}, u32[]{:S(2)}) collective-permute-start(bf16[256,1024]{1,0:T(8,128)(2,1)S(1)} %slice.11), channel_id=1, source_target_pairs={{0,1},{1,2},{2,3},{3,0},{4,5},{5,6},{6,7},{7,4},{8,9},{9,10},{10,1... | collective-permute-start | bytes 1572872 | tf_op jit(solution)/shard_map/ppermute | solution.py:44
  52.1 12.9 %collective-permute-start.3 = (bf16[256,1024]{1,0:T(8,128)(2,1)S(1)}, bf16[256,1024]{1,0:T(8,128)(2,1)S(1)}, u32[]{:S(2)}, u32[]{:S(2)}) collective-permute-start(bf16[256,1024]{1,0:T(8,128)(2,1)S(1)} %slice.11), channel_id=1, source_target_pairs={{0,3},{1,0},{2,1},{3,2},{4,7},{5,4},{6,5},{7,6},{8,11},{9,8},{10,9... | collective-permute-start | bytes 1572872 | tf_op jit(solution)/shard_map/ppermute | solution.py:46
  65.4 6.0 %collective-permute-start.4 = (f32[256]{0:T(256)S(1)}, f32[256]{0:T(256)S(1)}, u32[]{:S(2)}, u32[]{:S(2)}) collective-permute-start(f32[256]{0:T(256)S(1)} %select_reduce_fusion), channel_id=1, source_target_pairs={{0,3},{1,0},{2,1},{3,2},{4,7},{5,4},{6,5},{7,6},{8,11},{9,8},{10,9... | collective-permute-start | bytes 3080 | tf_op jit(solution)/shard_map/ppermute | solution.py:70
  72.2 22.1 %all-to-all-start.1 = ((f32[128,1,2]{2,1,0:T(1,128)}), f32[128,1,2]{2,1,0:T(1,128)S(1)}, u32[]{:S(2)}, u32[]{:S(2)}) async-start(f32[128,1,2]{2,1,0:T(1,128)} %bitcast), calls=%async_computation.1 | async-start | bytes 131072 | tf_op jit(solution)/shard_map/all_to_all | solution.py:79

commit v4 on v3

--- a/solution.py
+++ b/solution.py
@@ -30,10 +30,10 @@
     lane = jnp.arange(LANES, dtype=jnp.int32)
     extra = jnp.where(lane[None, :] == 0, code[:, None], jnp.zeros((), jnp.bfloat16))
     packed = jnp.concatenate([unit, extra], axis=1)
-    send = jnp.zeros((slots, width + LANES), jnp.bfloat16).at[position].set(packed)
-    got = lax.all_to_all(
-        send.reshape(n_dp, capacity, width + LANES), "dp", split_axis=0, concat_axis=0, tiled=True
-    ).reshape(slots, width + LANES)
+    send = jnp.zeros((n_dp, capacity, width + LANES), jnp.bfloat16).at[target, slot].set(packed)
+    got = lax.all_to_all(send, "dp", split_axis=0, concat_axis=0, tiled=True).reshape(
+        slots, width + LANES
+    )
 
     mine = got[:, :width]
     c1 = got[:, width].astype(jnp.int32)
@@ -41,10 +41,17 @@
 
     to_next = [(i, (i + 1) % n_owner) for i in range(n_owner)]
     to_prev = [(i, (i - 1) % n_owner) for i in range(n_owner)]
-    rows_l = lax.ppermute(mine, "owner", to_next)
-    ids_l = lax.ppermute(mine_ids, "owner", to_next)
-    rows_r = lax.ppermute(mine, "owner", to_prev)
-    ids_r = lax.ppermute(mine_ids, "owner", to_prev)
+    got_l = lax.ppermute(got, "owner", to_next)
+    got_r = lax.ppermute(got, "owner", to_prev)
+
+    def ids_of(block, owner_index):
+        c1 = block[:, width].astype(jnp.int32)
+        return jnp.where(c1 > 0, (here_dp * n_owner + owner_index) * CPD + c1 - 1, -1)
+
+    rows_l = got_l[:, :width]
+    ids_l = ids_of(got_l, (here_owner - 1) % n_owner)
+    rows_r = got_r[:, :width]
+    ids_r = ids_of(got_r, (here_owner + 1) % n_owner)
 
     def partner_of(ids, owner_index):
         base = (here_dp * n_owner + owner_index) * CPD
@@ -79,7 +86,8 @@
     returned = lax.all_to_all(
         best.reshape(n_dp, capacity), "dp", split_axis=0, concat_axis=0, tiled=True
     )
-    return returned.reshape(slots)[position]
+    pick = position[:, None] == jnp.arange(slots, dtype=jnp.int32)[None, :]
+    return jnp.sum(jnp.where(pick, returned.reshape(slots)[None, :], 0.0), axis=1)
 
 
 def solution(mesh):

time: 98 us -> 111 us (1.13)
  local copies, waits for them, and re-layouts: 5.97 us -> 22.9 us
  starting transfers between devices: 47.3 us -> 37 us
  waiting for transfers between devices: 39.3 us -> 46.4 us
    scatter x0 -> x1, local copies, waits for them, and re-layouts: none -> 18.4 us  [shards(): jnp.zeros((n_dp, capacity, width + LANES), jnp.bfloat16).at[target, slot]]
    ppermute x4 -> x2, starting transfers between devices: 13 us -> 6.32 us  [the longest x1 4.4 us: shards(): got_r = lax.ppermute(got, 'owner', to_prev)]
    ppermute x4 -> x2, waiting for transfers between devices: 7.72 us -> 13.2 us  [the longest x1 8.17 us: shards(): got_r = lax.ppermute(got, 'owner', to_prev)]
    ppermute x1, starting transfers between devices: 5.32 us -> 1.92 us  [shards(): far_back = lax.ppermute(far, 'owner', to_prev)]
    gather x1 -> x0, local copies, waits for them, and re-layouts: 1.77 us -> none  [shards(): return returned.reshape(slots)[position]]
    ppermute x1, waiting for transfers between devices: 0.01 us -> 1.61 us  [shards(): far_back = lax.ppermute(far, 'owner', to_prev)]
    scatter x1 -> x0, other arithmetic: 1.33 us -> none  [shards(): jnp.zeros((slots, width + LANES), jnp.bfloat16).at[position].set(packed)]
    broadcast_in_dim x0 -> x2, local copies, waits for them, and re-layouts: none -> 1.25 us  [the longest x1 1.11 us: shards(): jnp.zeros((n_dp, capacity, width + LANES), jnp.bfloat16).at[target, slot]]
  transfers between devices with their start and end apart: 7 -> 5, of which waited for: 4 -> 5; matrix products, arithmetic and copies ran while one was open for 2% -> 2% of each run, Pallas kernels for 0% -> 0%
where the time goes in v4:
time: 111 us
  waiting for transfers between devices  46.4 us (42%)
  starting transfers between devices  37 us (33%)
  local copies, waits for them, and re-layouts  22.9 us (21%)
  other arithmetic  2.56 us (2%)
  matrix products  1.51 us (1%)
    all_to_all x1, waiting for transfers between devices, shards(): lax.all_to_all(send, 'dp', split_axis=0, concat_axis=0, tiled=True)  20 us
    all_to_all x1, starting transfers between devices, shards(): lax.all_to_all(send, 'dp', split_axis=0, concat_axis=0, tiled=True)  18.4 us
    scatter x1, local copies, waits for them, and re-layouts, shards(): jnp.zeros((n_dp, capacity, width + LANES), jnp.bfloat16).at[target, slot]  18.4 us
    all_to_all x1, waiting for transfers between devices, shards(): lax.all_to_all(best.reshape(n_dp, capacity), 'dp', split_axis=0, concat_a...  11.5 us
    all_to_all x1, starting transfers between devices, shards(): lax.all_to_all(best.reshape(n_dp, capacity), 'dp', split_axis=0, concat_a...  10.3 us
    ppermute x1, waiting for transfers between devices, shards(): got_r = lax.ppermute(got, 'owner', to_prev)  8.17 us
    ppermute x1, waiting for transfers between devices, shards(): got_l = lax.ppermute(got, 'owner', to_next)  5.02 us
    ppermute x1, starting transfers between devices, shards(): got_r = lax.ppermute(got, 'owner', to_prev)  4.4 us
  transfers between devices with their start and end apart: 5, of which 5 were waited for; matrix products, arithmetic and copies ran while one was open for 2% of the time, Pallas kernels for 0%

profile of v4, /device:TPU:1, one launch (start us, length us, event | category | flops | bytes accessed | tf_op | source)
XLA Modules:
  0.0 110.6 jit_solution(11754288470971100015)
XLA Ops:
  0.0 0.0 copy-start.1
  0.0 0.0 copy-start
  0.0 0.6 copy-done.1
  0.7 0.1 fusion.15
  0.8 0.2 reduce_window_sum.11
  0.9 0.2 select_reduce_fusion.1
  1.1 0.0 copy-done
  1.1 0.1 fusion.4
  1.3 0.1 fusion.5
  1.4 0.1 broadcast_select_fusion
  1.5 1.1 %broadcast_in_dim.63 = bf16[128,2,1152]{2,1,0:T(2,128)(2,1)} broadcast(bf16[]{:T(256)} %constant.81.clone.1), dimensions={} | broadcast | bytes 589826 | tf_op jit(solution)/shard_map/broadcast_in_dim | solution.py:33
  2.6 18.4 %scatter_fusion = bf16[128,2,1152]{2,1,0:T(2,128)(2,1)} fusion(bf16[128,2,1152]{2,1,0:T(2,128)(2,1)} %broadcast_in_dim.63, s32[128]{0:T(128)S(1)} %fusion.20, bf16[128,1152]{1,0:T(8,128)(2,1)S(1)} %pad_maximum_fusion), kind=kCustom, calls=%fused_computation | custom fusion | bytes 885760 | tf_op jit(solution)/shard_map/scatter | solution.py:33
  21.1 18.4 %all-to-all-start = ((bf16[128,2,1152]{2,1,0:T(2,128)(2,1)}), bf16[128,2,1152]{2,1,0:T(2,128)(2,1)S(1)}, u32[]{:S(2)}, u32[]{:S(2)}) async-start(bf16[128,2,1152]{2,1,0:T(2,128)(2,1)} %scatter_fusion), calls=%async_computation | async-start | bytes 1179648 | tf_op jit(solution)/shard_map/all_to_all | solution.py:34
  39.6 0.8 fusion.21
  40.4 20.0 %all-to-all-done = bf16[128,2,1152]{2,1,0:T(2,128)(2,1)S(1)} async-done(((bf16[128,2,1152]{2,1,0:T(2,128)(2,1)}), bf16[128,2,1152]{2,1,0:T(2,128)(2,1)S(1)}, u32[]{:S(2)}, u32[]{:S(2)}) %all-to-all-start) | async-done | bytes 589856 | tf_op jit(solution)/shard_map/all_to_all | solution.py:34
  60.5 0.2 reshape.116
  60.7 0.2 copy.11
  60.9 4.4 %collective-permute-start.1 = (bf16[256,1152]{0,1:T(8,128)(2,1)S(1)}, bf16[256,1152]{0,1:T(8,128)(2,1)S(1)}, u32[]{:S(2)}, u32[]{:S(2)}) collective-permute-start(bf16[256,1152]{0,1:T(8,128)(2,1)S(1)} %copy.11), channel_id=1, source_target_pairs={{0,3},{1,0},{2,1},{3,2},{4,7},{5,4},{6,5},{7,6},{8,11},{9,8},{10,9... | collective-permute-start | bytes 1769480 | tf_op jit(solution)/shard_map/ppermute | solution.py:45
  65.3 1.9 %collective-permute-start = (bf16[256,1152]{0,1:T(8,128)(2,1)S(1)}, bf16[256,1152]{0,1:T(8,128)(2,1)S(1)}, u32[]{:S(2)}, u32[]{:S(2)}) collective-permute-start(bf16[256,1152]{0,1:T(8,128)(2,1)S(1)} %copy.11), channel_id=1, source_target_pairs={{0,1},{1,2},{2,3},{3,0},{4,5},{5,6},{6,7},{7,4},{8,9},{9,10},{10,1... | collective-permute-start | bytes 1769480 | tf_op jit(solution)/shard_map/ppermute | solution.py:44
  67.3 0.1 select_reduce_fusion.3
  67.4 0.4 fusion
  67.7 8.2 %collective-permute-done.1 = bf16[256,1152]{0,1:T(8,128)(2,1)S(1)} collective-permute-done((bf16[256,1152]{0,1:T(8,128)(2,1)S(1)}, bf16[256,1152]{0,1:T(8,128)(2,1)S(1)}, u32[]{:S(2)}, u32[]{:S(2)}) %collective-permute-start.1) | collective-permute-done | bytes 589856 | tf_op jit(solution)/shard_map/ppermute | solution.py:45
  75.9 5.0 %collective-permute-done = bf16[256,1152]{0,1:T(8,128)(2,1)S(1)} collective-permute-done((bf16[256,1152]{0,1:T(8,128)(2,1)S(1)}, bf16[256,1152]{0,1:T(8,128)(2,1)S(1)}, u32[]{:S(2)}, u32[]{:S(2)}) %collective-permute-start) | collective-permute-done | bytes 589856 | tf_op jit(solution)/shard_map/ppermute | solution.py:44
  81.0 0.1 select_reduce_fusion.2
  81.1 0.4 fusion.3
  81.4 1.9 %collective-permute-start.2 = (f32[256]{0:T(256)S(1)}, f32[256]{0:T(256)S(1)}, u32[]{:S(2)}, u32[]{:S(2)}) collective-permute-start(f32[256]{0:T(256)S(1)} %fusion.3), channel_id=1, source_target_pairs={{0,3},{1,0},{2,1},{3,2},{4,7},{5,4},{6,5},{7,6},{8,11},{9,8},{10,9... | collective-permute-start | bytes 3080 | tf_op jit(solution)/shard_map/ppermute | solution.py:77
  83.4 0.4 fusion.2
  83.7 0.4 fusion.1
  84.1 1.6 %collective-permute-done.2 = f32[256]{0:T(256)S(1)} collective-permute-done((f32[256]{0:T(256)S(1)}, f32[256]{0:T(256)S(1)}, u32[]{:S(2)}, u32[]{:S(2)}) %collective-permute-start.2) | collective-permute-done | bytes 1056 | tf_op jit(solution)/shard_map/ppermute | solution.py:77
  85.7 0.8 all_to_all.10
  86.5 10.3 %all-to-all-start.1 = ((f32[128,1,2]{2,1,0:T(1,128)}), f32[128,1,2]{2,1,0:T(1,128)S(1)}, u32[]{:S(2)}, u32[]{:S(2)}) async-start(f32[128,1,2]{2,1,0:T(1,128)} %bitcast.9), calls=%async_computation.1 | async-start | bytes 131072 | tf_op jit(solution)/shard_map/all_to_all | solution.py:86
  96.9 11.5 %all-to-all-done.1 = f32[128,1,2]{2,1,0:T(1,128)S(1)} async-done(((f32[128,1,2]{2,1,0:T(1,128)}), f32[128,1,2]{2,1,0:T(1,128)S(1)}, u32[]{:S(2)}, u32[]{:S(2)}) %all-to-all-start.1) | async-done | bytes 1056 | tf_op jit(solution)/shard_map/all_to_all | solution.py:86
  108.4 0.5 broadcast.269
  108.9 0.8 reduce.3
  109.7 0.1 broadcast_in_dim.114
  109.9 0.7 select_reduce_fusion
  (13 shorter events, 0.1 us)
Async XLA Ops:
  0.0 0.7 copy-start.1
  0.0 1.1 %copy-start = (bf16[128,1024]{1,0:T(8,128)(2,1)S(1)}, bf16[128,1024]{1,0:T(8,128)(2,1)}, u32[]{:S(2)}) copy-start(bf16[128,1024]{1,0:T(8,128)(2,1)} %param.3) | copy-start | bytes 786436
  21.1 39.4 %all-to-all-start = ((bf16[128,2,1152]{2,1,0:T(2,128)(2,1)}), bf16[128,2,1152]{2,1,0:T(2,128)(2,1)S(1)}, u32[]{:S(2)}, u32[]{:S(2)}) async-start(bf16[128,2,1152]{2,1,0:T(2,128)(2,1)} %scatter_fusion), calls=%async_computation | async-start | bytes 1179648 | tf_op jit(solution)/shard_map/all_to_all | solution.py:34
  60.9 15.0 %collective-permute-start.1 = (bf16[256,1152]{0,1:T(8,128)(2,1)S(1)}, bf16[256,1152]{0,1:T(8,128)(2,1)S(1)}, u32[]{:S(2)}, u32[]{:S(2)}) collective-permute-start(bf16[256,1152]{0,1:T(8,128)(2,1)S(1)} %copy.11), channel_id=1, source_target_pairs={{0,3},{1,0},{2,1},{3,2},{4,7},{5,4},{6,5},{7,6},{8,11},{9,8},{10,9... | collective-permute-start | bytes 1769480 | tf_op jit(solution)/shard_map/ppermute | solution.py:45
  65.3 15.6 %collective-permute-start = (bf16[256,1152]{0,1:T(8,128)(2,1)S(1)}, bf16[256,1152]{0,1:T(8,128)(2,1)S(1)}, u32[]{:S(2)}, u32[]{:S(2)}) collective-permute-start(bf16[256,1152]{0,1:T(8,128)(2,1)S(1)} %copy.11), channel_id=1, source_target_pairs={{0,1},{1,2},{2,3},{3,0},{4,5},{5,6},{6,7},{7,4},{8,9},{9,10},{10,1... | collective-permute-start | bytes 1769480 | tf_op jit(solution)/shard_map/ppermute | solution.py:44
  81.4 4.3 %collective-permute-start.2 = (f32[256]{0:T(256)S(1)}, f32[256]{0:T(256)S(1)}, u32[]{:S(2)}, u32[]{:S(2)}) collective-permute-start(f32[256]{0:T(256)S(1)} %fusion.3), channel_id=1, source_target_pairs={{0,3},{1,0},{2,1},{3,2},{4,7},{5,4},{6,5},{7,6},{8,11},{9,8},{10,9... | collective-permute-start | bytes 3080 | tf_op jit(solution)/shard_map/ppermute | solution.py:77
  86.5 21.9 %all-to-all-start.1 = ((f32[128,1,2]{2,1,0:T(1,128)}), f32[128,1,2]{2,1,0:T(1,128)S(1)}, u32[]{:S(2)}, u32[]{:S(2)}) async-start(f32[128,1,2]{2,1,0:T(1,128)} %bitcast.9), calls=%async_computation.1 | async-start | bytes 131072 | tf_op jit(solution)/shard_map/all_to_all | solution.py:86

commit v5 on v4

--- a/solution.py
+++ b/solution.py
@@ -30,7 +30,12 @@
     lane = jnp.arange(LANES, dtype=jnp.int32)
     extra = jnp.where(lane[None, :] == 0, code[:, None], jnp.zeros((), jnp.bfloat16))
     packed = jnp.concatenate([unit, extra], axis=1)
-    send = jnp.zeros((n_dp, capacity, width + LANES), jnp.bfloat16).at[target, slot].set(packed)
+    place = (target[None, None, :] == jnp.arange(n_dp, dtype=jnp.int32)[:, None, None]) & (
+        slot[None, None, :] == jnp.arange(capacity, dtype=jnp.int32)[None, :, None]
+    )
+    send = jnp.einsum(
+        "tkr,rw->tkw", place.astype(jnp.bfloat16), packed, preferred_element_type=jnp.float32
+    ).astype(jnp.bfloat16)
     got = lax.all_to_all(send, "dp", split_axis=0, concat_axis=0, tiled=True).reshape(
         slots, width + LANES
     )
@@ -83,11 +88,11 @@
         ),
     )
     best = jnp.maximum(best, far_back)
-    returned = lax.all_to_all(
-        best.reshape(n_dp, capacity), "dp", split_axis=0, concat_axis=0, tiled=True
-    )
+    wide = jnp.pad(best.reshape(n_dp, capacity), ((0, 0), (0, LANES - capacity)))
+    returned = lax.all_to_all(wide, "dp", split_axis=0, concat_axis=0, tiled=True)
+    returned = returned[:, :capacity].reshape(slots)
     pick = position[:, None] == jnp.arange(slots, dtype=jnp.int32)[None, :]
-    return jnp.sum(jnp.where(pick, returned.reshape(slots)[None, :], 0.0), axis=1)
+    return jnp.sum(jnp.where(pick, returned[None, :], 0.0), axis=1)
 
 
 def solution(mesh):

time: 111 us -> 92.7 us (0.84)
  blocking collectives: 0 us -> 21.7 us
  local copies, waits for them, and re-layouts: 22.9 us -> 2.76 us
  waiting for transfers between devices: 46.4 us -> 34.6 us
  starting transfers between devices: 37 us -> 26.7 us
  other arithmetic: 2.56 us -> 4.67 us
    all_to_all x0 -> x1, blocking collectives: none -> 21.7 us  [shards(): lax.all_to_all(wide, 'dp', split_axis=0, concat_axis=0, tiled=True)]
    scatter x1 -> x0, local copies, waits for them, and re-layouts: 18.4 us -> none  [shards(): jnp.zeros((n_dp, capacity, width + LANES), jnp.bfloat16).at[target, slot]]
    all_to_all x1 -> x0, waiting for transfers between devices: 11.5 us -> none  [shards(): lax.all_to_all(best.reshape(n_dp, capacity), 'dp', split_axis=0, concat_a...]
    all_to_all x1 -> x0, starting transfers between devices: 10.3 us -> none  [shards(): lax.all_to_all(best.reshape(n_dp, capacity), 'dp', split_axis=0, concat_a...]
    convert_element_type x0 -> x1, local copies, waits for them, and re-layouts: none -> 1.41 us  [shards(): send = jnp.einsum('tkr,rw->tkw', place.astype(jnp.bfloat16), packed, pref...]
    all_to_all x2 -> x0, local copies, waits for them, and re-layouts: 1.27 us -> none  [shards(): lax.all_to_all(best.reshape(n_dp, capacity), 'dp', split_axis=0, concat_a...]
    broadcast_in_dim x2 -> x1, local copies, waits for them, and re-layouts: 1.25 us -> 0.14 us  [shards(): return jnp.sum(jnp.where(pick, returned[None, :], 0.0), axis=1)]
  transfers between devices with their start and end apart: 5 -> 4, of which waited for: 5 -> 4; matrix products, arithmetic and copies ran while one was open for 2% -> 2% of each run, Pallas kernels for 0% -> 0%
where the time goes in v5:
time: 92.7 us; the launch traced here: 92.3 us
  waiting for transfers between devices  34.6 us (37%)
  starting transfers between devices  26.7 us (29%)
  blocking collectives  21.7 us (23%)
  other arithmetic  4.67 us (5%)
  local copies, waits for them, and re-layouts  2.76 us (3%)
  matrix products  1.72 us (2%)
    all_to_all x1, blocking collectives, shards(): lax.all_to_all(wide, 'dp', split_axis=0, concat_axis=0, tiled=True)  21.7 us
    all_to_all x1, waiting for transfers between devices, shards(): lax.all_to_all(send, 'dp', split_axis=0, concat_axis=0, tiled=True)  20 us
    all_to_all x1, starting transfers between devices, shards(): lax.all_to_all(send, 'dp', split_axis=0, concat_axis=0, tiled=True)  18.4 us
    ppermute x1, waiting for transfers between devices, shards(): got_r = lax.ppermute(got, 'owner', to_prev)  8.02 us
    ppermute x1, waiting for transfers between devices, shards(): got_l = lax.ppermute(got, 'owner', to_next)  4.91 us
    ppermute x1, starting transfers between devices, shards(): got_r = lax.ppermute(got, 'owner', to_prev)  4.39 us
    ppermute x1, starting transfers between devices, shards(): got_l = lax.ppermute(got, 'owner', to_next)  1.92 us
    ppermute x1, starting transfers between devices, shards(): far_back = lax.ppermute(far, 'owner', to_prev)  1.92 us
  transfers between devices with their start and end apart: 4, of which 4 were waited for; matrix products, arithmetic and copies ran while one was open for 2% of the time, Pallas kernels for 0%

profile of v5, /device:TPU:1, one launch (start us, length us, event | category | flops | bytes accessed | tf_op | source)
XLA Modules:
  0.0 92.3 jit_solution(12265806595319589795)
XLA Ops:
  0.0 0.7 and_select_fusion.1
  0.7 1.1 %fusion.4 = f32[128]{0:T(128)S(1)} fusion(bf16[128,1024]{1,0:T(8,128)(2,1)} %param.3), kind=kLoop, calls=%fused_computation.11 | loop fusion | flops 393088 | bytes 262656 | tf_op jit(solution)/shard_map/reduce_sum | solution.py:20
  1.8 1.1 %fusion.5 = bf16[128,1024]{1,0:T(8,128)(2,1)S(1)} fusion(bf16[128,1024]{1,0:T(8,128)(2,1)} %param.3, f32[128]{0:T(128)S(1)} %add_rsqrt_fusion), kind=kLoop, calls=%fused_computation.12 | loop fusion | flops 393216 | bytes 524800 | tf_op jit(solution)/shard_map/convert_element_type | solution.py:20
  2.8 0.1 iota_compare_fusion.2
  2.9 0.2 reduce_window_sum.11
  3.1 0.2 select_reduce_fusion.1
  3.3 0.1 broadcast_select_fusion
  3.4 0.3 convolution_convert_fusion
  3.7 1.4 %copy.7 = bf16[128,2,1152]{2,1,0:T(2,128)(2,1)} copy(bf16[128,2,1152]{2,0,1:T(8,128)(2,1)S(1)} %convolution_convert_fusion) | data formatting | bytes 1179648 | tf_op jit(solution)/shard_map/convert_element_type | solution.py:38
  5.1 18.4 %all-to-all-start = ((bf16[128,2,1152]{2,1,0:T(2,128)(2,1)}), bf16[128,2,1152]{2,1,0:T(2,128)(2,1)S(1)}, u32[]{:S(2)}, u32[]{:S(2)}) async-start(bf16[128,2,1152]{2,1,0:T(2,128)(2,1)} %copy.7), calls=%async_computation | async-start | bytes 1179648 | tf_op jit(solution)/shard_map/all_to_all | solution.py:39
  23.6 0.8 fusion.33
  24.4 20.0 %all-to-all-done = bf16[128,2,1152]{2,1,0:T(2,128)(2,1)S(1)} async-done(((bf16[128,2,1152]{2,1,0:T(2,128)(2,1)}), bf16[128,2,1152]{2,1,0:T(2,128)(2,1)S(1)}, u32[]{:S(2)}, u32[]{:S(2)}) %all-to-all-start) | async-done | bytes 589856 | tf_op jit(solution)/shard_map/all_to_all | solution.py:39
  44.5 0.2 reshape.144
  44.7 4.4 %collective-permute-start.1 = (bf16[256,1152]{1,0:T(8,128)(2,1)S(1)}, bf16[256,1152]{1,0:T(8,128)(2,1)S(1)}, u32[]{:S(2)}, u32[]{:S(2)}) collective-permute-start(bf16[256,1152]{1,0:T(8,128)(2,1)S(1)} %reshape.144), channel_id=1, source_target_pairs={{0,3},{1,0},{2,1},{3,2},{4,7},{5,4},{6,5},{7,6},{8,11},{9,8},{10,9... | collective-permute-start | bytes 1769480 | tf_op jit(solution)/shard_map/ppermute | solution.py:50
  49.1 1.9 %collective-permute-start = (bf16[256,1152]{1,0:T(8,128)(2,1)S(1)}, bf16[256,1152]{1,0:T(8,128)(2,1)S(1)}, u32[]{:S(2)}, u32[]{:S(2)}) collective-permute-start(bf16[256,1152]{1,0:T(8,128)(2,1)S(1)} %reshape.144), channel_id=1, source_target_pairs={{0,1},{1,2},{2,3},{3,0},{4,5},{5,6},{6,7},{7,4},{8,9},{9,10},{10,1... | collective-permute-start | bytes 1769480 | tf_op jit(solution)/shard_map/ppermute | solution.py:49
  51.0 0.2 fusion.24
  51.2 0.1 select_reduce_fusion.3
  51.3 0.4 fusion
  51.6 8.0 %collective-permute-done.1 = bf16[256,1152]{1,0:T(8,128)(2,1)S(1)} collective-permute-done((bf16[256,1152]{1,0:T(8,128)(2,1)S(1)}, bf16[256,1152]{1,0:T(8,128)(2,1)S(1)}, u32[]{:S(2)}, u32[]{:S(2)}) %collective-permute-start.1) | collective-permute-done | bytes 589856 | tf_op jit(solution)/shard_map/ppermute | solution.py:50
  59.7 0.1 fusion.23
  59.8 4.9 %collective-permute-done = bf16[256,1152]{1,0:T(8,128)(2,1)S(1)} collective-permute-done((bf16[256,1152]{1,0:T(8,128)(2,1)S(1)}, bf16[256,1152]{1,0:T(8,128)(2,1)S(1)}, u32[]{:S(2)}, u32[]{:S(2)}) %collective-permute-start) | collective-permute-done | bytes 589856 | tf_op jit(solution)/shard_map/ppermute | solution.py:49
  64.7 0.2 fusion.25
  64.9 0.1 select_reduce_fusion.2
  65.0 0.3 fusion.3
  65.3 1.9 %collective-permute-start.2 = (f32[256]{0:T(256)S(1)}, f32[256]{0:T(256)S(1)}, u32[]{:S(2)}, u32[]{:S(2)}) collective-permute-start(f32[256]{0:T(256)S(1)} %fusion.3), channel_id=1, source_target_pairs={{0,3},{1,0},{2,1},{3,2},{4,7},{5,4},{6,5},{7,6},{8,11},{9,8},{10,9... | collective-permute-start | bytes 3080 | tf_op jit(solution)/shard_map/ppermute | solution.py:82
  67.2 0.4 fusion.2
  67.6 0.4 fusion.1
  67.9 1.7 %collective-permute-done.2 = f32[256]{0:T(256)S(1)} collective-permute-done((f32[256]{0:T(256)S(1)}, f32[256]{0:T(256)S(1)}, u32[]{:S(2)}, u32[]{:S(2)}) %collective-permute-start.2) | collective-permute-done | bytes 1056 | tf_op jit(solution)/shard_map/ppermute | solution.py:82
  69.6 0.1 reshape.145
  69.8 21.7 %all_to_all.17 = f32[128,1,128]{2,1,0:T(1,128)S(1)} all-to-all(f32[128,1,128]{2,1,0:T(1,128)S(1)} %bitcast.8), channel_id=1, replica_groups=mesh['dp'=128,'owner'=4] {'dp'}, dimensions={0} | all-to-all | bytes 131072 | tf_op jit(solution)/shard_map/all_to_all | solution.py:92
  91.4 0.1 broadcast_in_dim.66
  91.6 0.7 select_reduce_fusion
  (9 shorter events, 0.1 us)
Async XLA Ops:
  5.1 39.3 %all-to-all-start = ((bf16[128,2,1152]{2,1,0:T(2,128)(2,1)}), bf16[128,2,1152]{2,1,0:T(2,128)(2,1)S(1)}, u32[]{:S(2)}, u32[]{:S(2)}) async-start(bf16[128,2,1152]{2,1,0:T(2,128)(2,1)} %copy.7), calls=%async_computation | async-start | bytes 1179648 | tf_op jit(solution)/shard_map/all_to_all | solution.py:39
  44.7 15.0 %collective-permute-start.1 = (bf16[256,1152]{1,0:T(8,128)(2,1)S(1)}, bf16[256,1152]{1,0:T(8,128)(2,1)S(1)}, u32[]{:S(2)}, u32[]{:S(2)}) collective-permute-start(bf16[256,1152]{1,0:T(8,128)(2,1)S(1)} %reshape.144), channel_id=1, source_target_pairs={{0,3},{1,0},{2,1},{3,2},{4,7},{5,4},{6,5},{7,6},{8,11},{9,8},{10,9... | collective-permute-start | bytes 1769480 | tf_op jit(solution)/shard_map/ppermute | solution.py:50
  49.1 15.6 %collective-permute-start = (bf16[256,1152]{1,0:T(8,128)(2,1)S(1)}, bf16[256,1152]{1,0:T(8,128)(2,1)S(1)}, u32[]{:S(2)}, u32[]{:S(2)}) collective-permute-start(bf16[256,1152]{1,0:T(8,128)(2,1)S(1)} %reshape.144), channel_id=1, source_target_pairs={{0,1},{1,2},{2,3},{3,0},{4,5},{5,6},{6,7},{7,4},{8,9},{9,10},{10,1... | collective-permute-start | bytes 1769480 | tf_op jit(solution)/shard_map/ppermute | solution.py:49
  65.3 4.3 %collective-permute-start.2 = (f32[256]{0:T(256)S(1)}, f32[256]{0:T(256)S(1)}, u32[]{:S(2)}, u32[]{:S(2)}) collective-permute-start(f32[256]{0:T(256)S(1)} %fusion.3), channel_id=1, source_target_pairs={{0,3},{1,0},{2,1},{3,2},{4,7},{5,4},{6,5},{7,6},{8,11},{9,8},{10,9... | collective-permute-start | bytes 3080 | tf_op jit(solution)/shard_map/ppermute | solution.py:82

commit v6 on v5

--- a/solution.py
+++ b/solution.py
@@ -17,24 +17,28 @@
     here_owner = lax.axis_index("owner")
     here_dp = lax.axis_index("dp")
     values = embeddings.astype(jnp.float32)
-    unit = (values * lax.rsqrt(jnp.sum(values * values, axis=1, keepdims=True) + 1e-06)).astype(
-        jnp.bfloat16
-    )
+    scale = lax.rsqrt(jnp.sum(values * values, axis=1) + 1e-06)
     target = assignment // (n_owner * CPD)
-    onehot = (target[:, None] == jnp.arange(n_dp, dtype=jnp.int32)[None, :]).astype(jnp.int32)
-    slot = jnp.sum(jnp.cumsum(onehot, axis=0) * onehot, axis=1) - 1
+    order = jnp.arange(rows, dtype=jnp.int32)
+    earlier = (target[:, None] == target[None, :]) & (order[None, :] < order[:, None])
+    slot = jnp.sum(earlier.astype(jnp.int32), axis=1)
     position = target * capacity + slot
     first_id = (here_dp * n_owner + here_owner) * CPD
 
     code = (assignment % CPD + 1).astype(jnp.bfloat16)
     lane = jnp.arange(LANES, dtype=jnp.int32)
     extra = jnp.where(lane[None, :] == 0, code[:, None], jnp.zeros((), jnp.bfloat16))
-    packed = jnp.concatenate([unit, extra], axis=1)
+    packed = jnp.concatenate([embeddings, extra], axis=1)
     place = (target[None, None, :] == jnp.arange(n_dp, dtype=jnp.int32)[:, None, None]) & (
         slot[None, None, :] == jnp.arange(capacity, dtype=jnp.int32)[None, :, None]
     )
-    send = jnp.einsum(
+    moved = jnp.einsum(
         "tkr,rw->tkw", place.astype(jnp.bfloat16), packed, preferred_element_type=jnp.float32
+    )
+    slot_scale = jnp.sum(jnp.where(place, scale[None, None, :], 0.0), axis=2)
+    lanes_all = jnp.arange(width + LANES, dtype=jnp.int32)
+    send = jnp.where(
+        lanes_all[None, None, :] < width, moved * slot_scale[:, :, None], moved
     ).astype(jnp.bfloat16)
     got = lax.all_to_all(send, "dp", split_axis=0, concat_axis=0, tiled=True).reshape(
         slots, width + LANES

time: 92.7 us -> 93.3 us (level)
  blocking collectives: 21.7 us -> 0 us
  waiting for transfers between devices: 34.6 us -> 46.2 us
  starting transfers between devices: 26.7 us -> 37 us
  other arithmetic: 4.67 us -> 3.49 us
  matrix products: 1.72 us -> 2.68 us
    all_to_all x1 -> x0, blocking collectives: 21.7 us -> none  [shards(): lax.all_to_all(wide, 'dp', split_axis=0, concat_axis=0, tiled=True)]
    all_to_all x0 -> x1, waiting for transfers between devices: none -> 11.5 us  [shards(): lax.all_to_all(wide, 'dp', split_axis=0, concat_axis=0, tiled=True)]
    all_to_all x0 -> x1, starting transfers between devices: none -> 10.3 us  [shards(): lax.all_to_all(wide, 'dp', split_axis=0, concat_axis=0, tiled=True)]
    dot_general x1, matrix products: 0.3 us -> 1.27 us  [shards(): jnp.einsum('tkr,rw->tkw', place.astype(jnp.bfloat16), packed, preferred_e...]
  transfers between devices with their start and end apart: 4 -> 5, of which waited for: 4 -> 5; matrix products, arithmetic and copies ran while one was open for 2% -> 2% of each run, Pallas kernels for 0% -> 0%
where the time goes in v6:
time: 93.3 us; the launch traced here: 92.9 us
  waiting for transfers between devices  46.2 us (50%)
  starting transfers between devices  37 us (40%)
  other arithmetic  3.49 us (4%)
  local copies, waits for them, and re-layouts  3.38 us (4%)
  matrix products  2.68 us (3%)
    all_to_all x1, waiting for transfers between devices, shards(): lax.all_to_all(send, 'dp', split_axis=0, concat_axis=0, tiled=True)  20 us
    all_to_all x1, starting transfers between devices, shards(): lax.all_to_all(send, 'dp', split_axis=0, concat_axis=0, tiled=True)  18.4 us
    all_to_all x1, waiting for transfers between devices, shards(): lax.all_to_all(wide, 'dp', split_axis=0, concat_axis=0, tiled=True)  11.5 us
    all_to_all x1, starting transfers between devices, shards(): lax.all_to_all(wide, 'dp', split_axis=0, concat_axis=0, tiled=True)  10.3 us
    ppermute x1, waiting for transfers between devices, shards(): got_r = lax.ppermute(got, 'owner', to_prev)  8.02 us
    ppermute x1, waiting for transfers between devices, shards(): got_l = lax.ppermute(got, 'owner', to_next)  4.91 us
    ppermute x1, starting transfers between devices, shards(): got_r = lax.ppermute(got, 'owner', to_prev)  4.39 us
    ppermute x1, starting transfers between devices, shards(): got_l = lax.ppermute(got, 'owner', to_next)  1.92 us
  transfers between devices with their start and end apart: 5, of which 5 were waited for; matrix products, arithmetic and copies ran while one was open for 2% of the time, Pallas kernels for 0%

profile of v6, /device:TPU:1, one launch (start us, length us, event | category | flops | bytes accessed | tf_op | source)
XLA Modules:
  0.0 92.9 jit_solution(11948714032070274655)
XLA Ops:
  0.0 0.7 fusion.31
  0.7 0.2 convert_reduce_fusion
  0.9 1.1 %multiply_reduce_fusion = f32[128]{0:T(128)S(1)} fusion(bf16[128,1024]{1,0:T(8,128)(2,1)} %param.3), kind=kLoop, calls=%fused_computation.10 | loop fusion | flops 393088 | bytes 262656 | tf_op jit(solution)/shard_map/reduce_sum | solution.py:20
  2.0 0.1 broadcast_select_fusion
  2.1 0.1 fusion.24
  2.2 1.3 %fusion = bf16[128,2,1152]{2,0,1:T(8,128)(2,1)S(1)} fusion(f32[128,2]{0,1:T(2,128)S(1)} %fusion.24, pred[1152]{0:T(1024)(128)(4,1)S(1)} %iota_compare_fusion.6, bf16[128,128]{1,0:T(8,128)(2,1)S(1)} %broadcast_select_fusion, bf16[128,1024]{1,0:T(8,128)(2,1)} %param.3, pred[2,128]{1,0:T(4,128)(4,1)S(1)} %iota_compare_fusion.7, ...), kind=kOutput, calls=%fused_computation.1 | convolution fusion | flops 77004800 | bytes 903552 | tf_op jit(solution)/shard_map/tkr,rw->tkw/dot_general | solution.py:35
  3.5 1.4 %copy.7 = bf16[128,2,1152]{2,1,0:T(2,128)(2,1)} copy(bf16[128,2,1152]{2,0,1:T(8,128)(2,1)S(1)} %fusion) | data formatting | bytes 1179648 | tf_op jit(solution)/shard_map/convert_element_type | solution.py:42
  4.9 18.4 %all-to-all-start = ((bf16[128,2,1152]{2,1,0:T(2,128)(2,1)}), bf16[128,2,1152]{2,1,0:T(2,128)(2,1)S(1)}, u32[]{:S(2)}, u32[]{:S(2)}) async-start(bf16[128,2,1152]{2,1,0:T(2,128)(2,1)} %copy.7), calls=%async_computation | async-start | bytes 1179648 | tf_op jit(solution)/shard_map/all_to_all | solution.py:43
  23.4 0.8 fusion.33
  24.2 20.0 %all-to-all-done = bf16[128,2,1152]{2,1,0:T(2,128)(2,1)S(1)} async-done(((bf16[128,2,1152]{2,1,0:T(2,128)(2,1)}), bf16[128,2,1152]{2,1,0:T(2,128)(2,1)S(1)}, u32[]{:S(2)}, u32[]{:S(2)}) %all-to-all-start) | async-done | bytes 589856 | tf_op jit(solution)/shard_map/all_to_all | solution.py:43
  44.2 0.2 reshape.147
  44.5 4.4 %collective-permute-start.1 = (bf16[256,1152]{1,0:T(8,128)(2,1)S(1)}, bf16[256,1152]{1,0:T(8,128)(2,1)S(1)}, u32[]{:S(2)}, u32[]{:S(2)}) collective-permute-start(bf16[256,1152]{1,0:T(8,128)(2,1)S(1)} %reshape.147), channel_id=1, source_target_pairs={{0,3},{1,0},{2,1},{3,2},{4,7},{5,4},{6,5},{7,6},{8,11},{9,8},{10,9... | collective-permute-start | bytes 1769480 | tf_op jit(solution)/shard_map/ppermute | solution.py:54
  48.9 1.9 %collective-permute-start = (bf16[256,1152]{1,0:T(8,128)(2,1)S(1)}, bf16[256,1152]{1,0:T(8,128)(2,1)S(1)}, u32[]{:S(2)}, u32[]{:S(2)}) collective-permute-start(bf16[256,1152]{1,0:T(8,128)(2,1)S(1)} %reshape.147), channel_id=1, source_target_pairs={{0,1},{1,2},{2,3},{3,0},{4,5},{5,6},{6,7},{7,4},{8,9},{9,10},{10,1... | collective-permute-start | bytes 1769480 | tf_op jit(solution)/shard_map/ppermute | solution.py:53
  50.8 0.2 fusion.25
  51.0 0.1 select_reduce_fusion.2
  51.1 0.4 fusion.1
  51.4 8.0 %collective-permute-done.1 = bf16[256,1152]{1,0:T(8,128)(2,1)S(1)} collective-permute-done((bf16[256,1152]{1,0:T(8,128)(2,1)S(1)}, bf16[256,1152]{1,0:T(8,128)(2,1)S(1)}, u32[]{:S(2)}, u32[]{:S(2)}) %collective-permute-start.1) | collective-permute-done | bytes 589856 | tf_op jit(solution)/shard_map/ppermute | solution.py:54
  59.4 0.1 fusion.23
  59.6 4.9 %collective-permute-done = bf16[256,1152]{1,0:T(8,128)(2,1)S(1)} collective-permute-done((bf16[256,1152]{1,0:T(8,128)(2,1)S(1)}, bf16[256,1152]{1,0:T(8,128)(2,1)S(1)}, u32[]{:S(2)}, u32[]{:S(2)}) %collective-permute-start) | collective-permute-done | bytes 589856 | tf_op jit(solution)/shard_map/ppermute | solution.py:53
  64.5 0.2 fusion.26
  64.6 0.1 select_reduce_fusion.1
  64.7 0.3 fusion.4
  65.1 1.9 %collective-permute-start.2 = (f32[256]{0:T(256)S(1)}, f32[256]{0:T(256)S(1)}, u32[]{:S(2)}, u32[]{:S(2)}) collective-permute-start(f32[256]{0:T(256)S(1)} %fusion.4), channel_id=1, source_target_pairs={{0,3},{1,0},{2,1},{3,2},{4,7},{5,4},{6,5},{7,6},{8,11},{9,8},{10,9... | collective-permute-start | bytes 3080 | tf_op jit(solution)/shard_map/ppermute | solution.py:86
  67.0 0.4 fusion.3
  67.4 0.3 fusion.2
  67.7 1.7 %collective-permute-done.2 = f32[256]{0:T(256)S(1)} collective-permute-done((f32[256]{0:T(256)S(1)}, f32[256]{0:T(256)S(1)}, u32[]{:S(2)}, u32[]{:S(2)}) %collective-permute-start.2) | collective-permute-done | bytes 1056 | tf_op jit(solution)/shard_map/ppermute | solution.py:86
  69.4 0.1 reshape.148
  69.5 0.6 pad.4
  70.2 10.3 %all-to-all-start.1 = ((f32[128,1,128]{2,1,0:T(1,128)}), f32[128,1,128]{2,1,0:T(1,128)S(1)}, u32[]{:S(2)}, u32[]{:S(2)}) async-start(f32[128,1,128]{2,1,0:T(1,128)} %bitcast.2), calls=%async_computation.1 | async-start | bytes 131072 | tf_op jit(solution)/shard_map/all_to_all | solution.py:96
  80.5 11.5 %all-to-all-done.1 = f32[128,1,128]{2,1,0:T(1,128)S(1)} async-done(((f32[128,1,128]{2,1,0:T(1,128)}), f32[128,1,128]{2,1,0:T(1,128)S(1)}, u32[]{:S(2)}, u32[]{:S(2)}) %all-to-all-start.1) | async-done | bytes 65568 | tf_op jit(solution)/shard_map/all_to_all | solution.py:96
  92.1 0.1 broadcast_in_dim.136
  92.2 0.7 select_reduce_fusion
  (10 shorter events, 0.1 us)
Async XLA Ops:
  4.9 39.3 %all-to-all-start = ((bf16[128,2,1152]{2,1,0:T(2,128)(2,1)}), bf16[128,2,1152]{2,1,0:T(2,128)(2,1)S(1)}, u32[]{:S(2)}, u32[]{:S(2)}) async-start(bf16[128,2,1152]{2,1,0:T(2,128)(2,1)} %copy.7), calls=%async_computation | async-start | bytes 1179648 | tf_op jit(solution)/shard_map/all_to_all | solution.py:43
  44.5 15.0 %collective-permute-start.1 = (bf16[256,1152]{1,0:T(8,128)(2,1)S(1)}, bf16[256,1152]{1,0:T(8,128)(2,1)S(1)}, u32[]{:S(2)}, u32[]{:S(2)}) collective-permute-start(bf16[256,1152]{1,0:T(8,128)(2,1)S(1)} %reshape.147), channel_id=1, source_target_pairs={{0,3},{1,0},{2,1},{3,2},{4,7},{5,4},{6,5},{7,6},{8,11},{9,8},{10,9... | collective-permute-start | bytes 1769480 | tf_op jit(solution)/shard_map/ppermute | solution.py:54
  48.9 15.6 %collective-permute-start = (bf16[256,1152]{1,0:T(8,128)(2,1)S(1)}, bf16[256,1152]{1,0:T(8,128)(2,1)S(1)}, u32[]{:S(2)}, u32[]{:S(2)}) collective-permute-start(bf16[256,1152]{1,0:T(8,128)(2,1)S(1)} %reshape.147), channel_id=1, source_target_pairs={{0,1},{1,2},{2,3},{3,0},{4,5},{5,6},{6,7},{7,4},{8,9},{9,10},{10,1... | collective-permute-start | bytes 1769480 | tf_op jit(solution)/shard_map/ppermute | solution.py:53
  65.1 4.3 %collective-permute-start.2 = (f32[256]{0:T(256)S(1)}, f32[256]{0:T(256)S(1)}, u32[]{:S(2)}, u32[]{:S(2)}) collective-permute-start(f32[256]{0:T(256)S(1)} %fusion.4), channel_id=1, source_target_pairs={{0,3},{1,0},{2,1},{3,2},{4,7},{5,4},{6,5},{7,6},{8,11},{9,8},{10,9... | collective-permute-start | bytes 3080 | tf_op jit(solution)/shard_map/ppermute | solution.py:86
  70.2 21.9 %all-to-all-start.1 = ((f32[128,1,128]{2,1,0:T(1,128)}), f32[128,1,128]{2,1,0:T(1,128)S(1)}, u32[]{:S(2)}, u32[]{:S(2)}) async-start(f32[128,1,128]{2,1,0:T(1,128)} %bitcast.2), calls=%async_computation.1 | async-start | bytes 131072 | tf_op jit(solution)/shard_map/all_to_all | solution.py:96

commit v7 on v5

--- a/solution.py
+++ b/solution.py
@@ -1,10 +1,22 @@
 import jax
 import jax.numpy as jnp
 from jax import lax
+from jax.experimental import pallas as pl
 from jax.sharding import PartitionSpec as P
 
 CPD = 16
+assert CPD & (CPD - 1) == 0
 LANES = 128
+
+
+def _pack_kernel(x_ref, a_ref, out_ref):
+    x = x_ref[...].astype(jnp.float32)
+    scale = lax.rsqrt(jnp.sum(x * x, axis=1, keepdims=True) + 1e-06)
+    width = x.shape[1]
+    out_ref[:, :width] = (x * scale).astype(out_ref.dtype)
+    code = (jnp.bitwise_and(a_ref[...], CPD - 1) + 1).astype(jnp.float32)
+    lane = lax.broadcasted_iota(jnp.int32, (x.shape[0], LANES), 1)
+    out_ref[:, width:] = jnp.where(lane == 0, code, 0.0).astype(out_ref.dtype)
 
 
 def shards(embeddings, assignment, pair_list):
@@ -16,20 +28,15 @@
     slots = capacity * n_dp
     here_owner = lax.axis_index("owner")
     here_dp = lax.axis_index("dp")
-    values = embeddings.astype(jnp.float32)
-    unit = (values * lax.rsqrt(jnp.sum(values * values, axis=1, keepdims=True) + 1e-06)).astype(
-        jnp.bfloat16
-    )
     target = assignment // (n_owner * CPD)
     onehot = (target[:, None] == jnp.arange(n_dp, dtype=jnp.int32)[None, :]).astype(jnp.int32)
     slot = jnp.sum(jnp.cumsum(onehot, axis=0) * onehot, axis=1) - 1
     position = target * capacity + slot
     first_id = (here_dp * n_owner + here_owner) * CPD
 
-    code = (assignment % CPD + 1).astype(jnp.bfloat16)
-    lane = jnp.arange(LANES, dtype=jnp.int32)
-    extra = jnp.where(lane[None, :] == 0, code[:, None], jnp.zeros((), jnp.bfloat16))
-    packed = jnp.concatenate([unit, extra], axis=1)
+    packed = pl.pallas_call(
+        _pack_kernel, out_shape=jax.ShapeDtypeStruct((rows, width + LANES), jnp.bfloat16)
+    )(embeddings, assignment.reshape(rows, 1))
     place = (target[None, None, :] == jnp.arange(n_dp, dtype=jnp.int32)[:, None, None]) & (
         slot[None, None, :] == jnp.arange(capacity, dtype=jnp.int32)[None, :, None]
     )

time: 92.7 us -> 95.2 us (1.027)
  Pallas kernels: 0 us -> 1.81 us
  other arithmetic: 4.67 us -> 3.09 us
  local copies, waits for them, and re-layouts: 2.76 us -> 4.15 us
  matrix products: 1.72 us -> 2.69 us
    pallas_call x0 -> x1, Pallas kernels: none -> 1.81 us  [shards(): pl.pallas_call(_pack_kernel, out_shape=jax.ShapeDtypeStruct((rows, width...]
    reshape x0 -> x1, local copies, waits for them, and re-layouts: none -> 1.39 us  [shards(): assignment.reshape(rows, 1)]
    reduce_sum x1 -> x0, other arithmetic: 1.08 us -> none  [shards(): jnp.sum(values * values, axis=1, keepdims=True) + 1e-06]
    convert_element_type x1 -> x0, other arithmetic: 1.07 us -> none  [shards(): (values * lax.rsqrt(jnp.sum(values * values, axis=1, keepdims=True) + 1e-...]
    dot_general x1, matrix products: 0.3 us -> 1.26 us  [shards(): jnp.einsum('tkr,rw->tkw', place.astype(jnp.bfloat16), packed, preferred_e...]
where the time goes in v7:
time: 95.2 us; the launch traced here: 94.8 us
  waiting for transfers between devices  34.6 us (36%)
  starting transfers between devices  26.6 us (28%)
  blocking collectives  21.7 us (23%)
  local copies, waits for them, and re-layouts  4.15 us (4%)
  other arithmetic  3.09 us (3%)
  matrix products  2.69 us (3%)
  Pallas kernels  1.81 us (2%)
    all_to_all x1, blocking collectives, shards(): lax.all_to_all(wide, 'dp', split_axis=0, concat_axis=0, tiled=True)  21.7 us
    all_to_all x1, waiting for transfers between devices, shards(): lax.all_to_all(send, 'dp', split_axis=0, concat_axis=0, tiled=True)  20 us
    all_to_all x1, starting transfers between devices, shards(): lax.all_to_all(send, 'dp', split_axis=0, concat_axis=0, tiled=True)  18.4 us
    ppermute x1, waiting for transfers between devices, shards(): got_r = lax.ppermute(got, 'owner', to_prev)  8.02 us
    ppermute x1, waiting for transfers between devices, shards(): got_l = lax.ppermute(got, 'owner', to_next)  4.91 us
    ppermute x1, starting transfers between devices, shards(): got_r = lax.ppermute(got, 'owner', to_prev)  4.39 us
    ppermute x1, starting transfers between devices, shards(): got_l = lax.ppermute(got, 'owner', to_next)  1.92 us
    ppermute x1, starting transfers between devices, shards(): far_back = lax.ppermute(far, 'owner', to_prev)  1.92 us
  transfers between devices with their start and end apart: 4, of which 4 were waited for; matrix products, arithmetic and copies ran while one was open for 2% of the time, Pallas kernels for 0%

profile of v7, /device:TPU:1, one launch (start us, length us, event | category | flops | bytes accessed | tf_op | source)
XLA Modules:
  0.0 94.8 jit_solution(17731032567262576225)
XLA Ops:
  0.0 0.7 and_select_fusion
  0.7 1.4 %copy.10.a_ref = s32[128,1]{1,0:T(8,128)} copy(s32[128,1]{0,1:T(1,128)} %bitcast.11) | data formatting | bytes 1024 | tf_op jit(solution)/shard_map/reshape | solution.py:39
  2.1 0.1 iota_compare_fusion.2
  2.1 0.2 reduce_window_sum.11
  2.3 0.2 select_reduce_fusion.1
  2.5 0.7 multiply_add_fusion
  3.2 1.8 %shard_map.37 = bf16[128,1152]{1,0:T(8,128)(2,1)} custom-call(bf16[128,1024]{1,0:T(8,128)(2,1)} %x_ref.1, s32[128,1]{1,0:T(8,128)} %copy.10.a_ref), custom_call_target="tpu_custom_call" | custom-call | tf_op jit(solution)/shard_map/pallas_call | solution.py:37
  5.0 1.3 %convolution_convert_fusion = bf16[128,2,1152]{2,0,1:T(8,128)(2,1)S(1)} fusion(bf16[128,1152]{1,0:T(8,128)(2,1)} %shard_map.37, pred[2,128]{1,0:T(4,128)(4,1)S(1)} %iota_compare_fusion.6, pred[128,128]{1,0:T(8,128)(4,1)S(1)} %get-tuple-element.13), kind=kOutput, calls=%fused_computation | convolution fusion | flops 75825152 | bytes 901376 | tf_op jit(solution)/shard_map/tkr,rw->tkw/dot_general | solution.py:43
  6.2 1.4 %copy.11 = bf16[128,2,1152]{2,1,0:T(2,128)(2,1)} copy(bf16[128,2,1152]{2,0,1:T(8,128)(2,1)S(1)} %convolution_convert_fusion) | data formatting | bytes 1179648 | tf_op jit(solution)/shard_map/convert_element_type | solution.py:45
  7.7 18.4 %all-to-all-start = ((bf16[128,2,1152]{2,1,0:T(2,128)(2,1)}), bf16[128,2,1152]{2,1,0:T(2,128)(2,1)S(1)}, u32[]{:S(2)}, u32[]{:S(2)}) async-start(bf16[128,2,1152]{2,1,0:T(2,128)(2,1)} %copy.11), calls=%async_computation | async-start | bytes 1179648 | tf_op jit(solution)/shard_map/all_to_all | solution.py:46
  26.1 0.8 fusion.27
  27.0 20.0 %all-to-all-done = bf16[128,2,1152]{2,1,0:T(2,128)(2,1)S(1)} async-done(((bf16[128,2,1152]{2,1,0:T(2,128)(2,1)}), bf16[128,2,1152]{2,1,0:T(2,128)(2,1)S(1)}, u32[]{:S(2)}, u32[]{:S(2)}) %all-to-all-start) | async-done | bytes 589856 | tf_op jit(solution)/shard_map/all_to_all | solution.py:46
  47.0 0.2 reshape.136
  47.2 4.4 %collective-permute-start.1 = (bf16[256,1152]{1,0:T(8,128)(2,1)S(1)}, bf16[256,1152]{1,0:T(8,128)(2,1)S(1)}, u32[]{:S(2)}, u32[]{:S(2)}) collective-permute-start(bf16[256,1152]{1,0:T(8,128)(2,1)S(1)} %reshape.136), channel_id=1, source_target_pairs={{0,3},{1,0},{2,1},{3,2},{4,7},{5,4},{6,5},{7,6},{8,11},{9,8},{10,9... | collective-permute-start | bytes 1769480 | tf_op jit(solution)/shard_map/ppermute | solution.py:57
  51.6 1.9 %collective-permute-start = (bf16[256,1152]{1,0:T(8,128)(2,1)S(1)}, bf16[256,1152]{1,0:T(8,128)(2,1)S(1)}, u32[]{:S(2)}, u32[]{:S(2)}) collective-permute-start(bf16[256,1152]{1,0:T(8,128)(2,1)S(1)} %reshape.136), channel_id=1, source_target_pairs={{0,1},{1,2},{2,3},{3,0},{4,5},{5,6},{6,7},{7,4},{8,9},{9,10},{10,1... | collective-permute-start | bytes 1769480 | tf_op jit(solution)/shard_map/ppermute | solution.py:56
  53.6 0.2 fusion.21
  53.7 0.1 select_reduce_fusion.3
  53.8 0.4 fusion
  54.2 8.0 %collective-permute-done.1 = bf16[256,1152]{1,0:T(8,128)(2,1)S(1)} collective-permute-done((bf16[256,1152]{1,0:T(8,128)(2,1)S(1)}, bf16[256,1152]{1,0:T(8,128)(2,1)S(1)}, u32[]{:S(2)}, u32[]{:S(2)}) %collective-permute-start.1) | collective-permute-done | bytes 589856 | tf_op jit(solution)/shard_map/ppermute | solution.py:57
  62.2 0.1 fusion.20
  62.3 4.9 %collective-permute-done = bf16[256,1152]{1,0:T(8,128)(2,1)S(1)} collective-permute-done((bf16[256,1152]{1,0:T(8,128)(2,1)S(1)}, bf16[256,1152]{1,0:T(8,128)(2,1)S(1)}, u32[]{:S(2)}, u32[]{:S(2)}) %collective-permute-start) | collective-permute-done | bytes 589856 | tf_op jit(solution)/shard_map/ppermute | solution.py:56
  67.2 0.2 fusion.22
  67.4 0.1 select_reduce_fusion.2
  67.5 0.4 fusion.3
  67.9 1.9 %collective-permute-start.2 = (f32[256]{0:T(256)S(1)}, f32[256]{0:T(256)S(1)}, u32[]{:S(2)}, u32[]{:S(2)}) collective-permute-start(f32[256]{0:T(256)S(1)} %fusion.3), channel_id=1, source_target_pairs={{0,3},{1,0},{2,1},{3,2},{4,7},{5,4},{6,5},{7,6},{8,11},{9,8},{10,9... | collective-permute-start | bytes 3080 | tf_op jit(solution)/shard_map/ppermute | solution.py:89
  69.8 0.4 fusion.2
  70.1 0.3 fusion.1
  70.5 1.7 %collective-permute-done.2 = f32[256]{0:T(256)S(1)} collective-permute-done((f32[256]{0:T(256)S(1)}, f32[256]{0:T(256)S(1)}, u32[]{:S(2)}, u32[]{:S(2)}) %collective-permute-start.2) | collective-permute-done | bytes 1056 | tf_op jit(solution)/shard_map/ppermute | solution.py:89
  72.2 0.1 reshape.137
  72.3 21.7 %all_to_all.17 = f32[128,1,128]{2,1,0:T(1,128)S(1)} all-to-all(f32[128,1,128]{2,1,0:T(1,128)S(1)} %bitcast.9), channel_id=1, replica_groups=mesh['dp'=128,'owner'=4] {'dp'}, dimensions={0} | all-to-all | bytes 131072 | tf_op jit(solution)/shard_map/all_to_all | solution.py:99
  94.0 0.1 broadcast_in_dim.43
  94.1 0.7 select_reduce_fusion
  (6 shorter events, 0.0 us)
Async XLA Ops:
  7.7 39.3 %all-to-all-start = ((bf16[128,2,1152]{2,1,0:T(2,128)(2,1)}), bf16[128,2,1152]{2,1,0:T(2,128)(2,1)S(1)}, u32[]{:S(2)}, u32[]{:S(2)}) async-start(bf16[128,2,1152]{2,1,0:T(2,128)(2,1)} %copy.11), calls=%async_computation | async-start | bytes 1179648 | tf_op jit(solution)/shard_map/all_to_all | solution.py:46
  47.2 15.0 %collective-permute-start.1 = (bf16[256,1152]{1,0:T(8,128)(2,1)S(1)}, bf16[256,1152]{1,0:T(8,128)(2,1)S(1)}, u32[]{:S(2)}, u32[]{:S(2)}) collective-permute-start(bf16[256,1152]{1,0:T(8,128)(2,1)S(1)} %reshape.136), channel_id=1, source_target_pairs={{0,3},{1,0},{2,1},{3,2},{4,7},{5,4},{6,5},{7,6},{8,11},{9,8},{10,9... | collective-permute-start | bytes 1769480 | tf_op jit(solution)/shard_map/ppermute | solution.py:57
  51.6 15.6 %collective-permute-start = (bf16[256,1152]{1,0:T(8,128)(2,1)S(1)}, bf16[256,1152]{1,0:T(8,128)(2,1)S(1)}, u32[]{:S(2)}, u32[]{:S(2)}) collective-permute-start(bf16[256,1152]{1,0:T(8,128)(2,1)S(1)} %reshape.136), channel_id=1, source_target_pairs={{0,1},{1,2},{2,3},{3,0},{4,5},{5,6},{6,7},{7,4},{8,9},{9,10},{10,1... | collective-permute-start | bytes 1769480 | tf_op jit(solution)/shard_map/ppermute | solution.py:56
  67.9 4.3 %collective-permute-start.2 = (f32[256]{0:T(256)S(1)}, f32[256]{0:T(256)S(1)}, u32[]{:S(2)}, u32[]{:S(2)}) collective-permute-start(f32[256]{0:T(256)S(1)} %fusion.3), channel_id=1, source_target_pairs={{0,3},{1,0},{2,1},{3,2},{4,7},{5,4},{6,5},{7,6},{8,11},{9,8},{10,9... | collective-permute-start | bytes 3080 | tf_op jit(solution)/shard_map/ppermute | solution.py:89

commit v8 on v5

--- a/solution.py
+++ b/solution.py
@@ -17,12 +17,15 @@
     here_owner = lax.axis_index("owner")
     here_dp = lax.axis_index("dp")
     values = embeddings.astype(jnp.float32)
-    unit = (values * lax.rsqrt(jnp.sum(values * values, axis=1, keepdims=True) + 1e-06)).astype(
-        jnp.bfloat16
+    gram = lax.dot_general(
+        embeddings, embeddings, (((1,), (1,)), ((), ())), preferred_element_type=jnp.float32
     )
-    target = assignment // (n_owner * CPD)
-    onehot = (target[:, None] == jnp.arange(n_dp, dtype=jnp.int32)[None, :]).astype(jnp.int32)
-    slot = jnp.sum(jnp.cumsum(onehot, axis=0) * onehot, axis=1) - 1
+    order = jnp.arange(rows, dtype=jnp.int32)
+    squares = jnp.sum(jnp.where(order[:, None] == order[None, :], gram, 0.0), axis=1)
+    unit = (values * lax.rsqrt(squares + 1e-06)[:, None]).astype(jnp.bfloat16)
+    target = lax.div(assignment, n_owner * CPD)
+    earlier = (target[:, None] == target[None, :]) & (order[None, :] < order[:, None])
+    slot = jnp.sum(earlier.astype(jnp.int32), axis=1)
     position = target * capacity + slot
     first_id = (here_dp * n_owner + here_owner) * CPD
 
@@ -79,7 +82,6 @@
     partner = partner_of(mine_ids, here_owner)
     partner_l = partner_of(ids_l, (here_owner - 1) % n_owner)
     far = best_against(rows_l, ids_l, partner_l, rows_r, ids_r, False)
-    far_back = lax.ppermute(far, "owner", to_prev)
     best = jnp.maximum(
         jnp.maximum(-1.0, best_against(mine, mine_ids, partner, mine, mine_ids, True)),
         jnp.maximum(
@@ -87,10 +89,13 @@
             best_against(mine, mine_ids, partner, rows_r, ids_r, False),
         ),
     )
-    best = jnp.maximum(best, far_back)
-    wide = jnp.pad(best.reshape(n_dp, capacity), ((0, 0), (0, LANES - capacity)))
+    wide = jnp.concatenate(
+        [best.reshape(n_dp, capacity), far.reshape(n_dp, capacity)], axis=1
+    )
+    wide = jnp.pad(wide, ((0, 0), (0, LANES - 2 * capacity)))
     returned = lax.all_to_all(wide, "dp", split_axis=0, concat_axis=0, tiled=True)
-    returned = returned[:, :capacity].reshape(slots)
+    far_here = lax.ppermute(returned[:, capacity : 2 * capacity], "owner", to_prev)
+    returned = jnp.maximum(returned[:, :capacity], far_here).reshape(slots)
     pick = position[:, None] == jnp.arange(slots, dtype=jnp.int32)[None, :]
     return jnp.sum(jnp.where(pick, returned[None, :], 0.0), axis=1)
 

time: 92.7 us -> 92.3 us (level)
  other arithmetic: 4.67 us -> 2.53 us
  waiting for transfers between devices: 34.6 us -> 36 us
  matrix products: 1.72 us -> 3 us
  blocking collectives: 21.7 us -> 20.5 us
    ppermute x1, waiting for transfers between devices: 1.67 us -> 3.07 us  [shards(): lax.ppermute(returned[:, capacity:2 * capacity], 'owner', to_prev)]
    dot_general x0 -> x1, matrix products: none -> 1.27 us  [shards(): lax.dot_general(embeddings, embeddings, (((1,), (1,)), ((), ())), preferr...]
    all_to_all x1, blocking collectives: 21.7 us -> 20.5 us  [shards(): lax.all_to_all(wide, 'dp', split_axis=0, concat_axis=0, tiled=True)]
    reduce_sum x2 -> x1, other arithmetic: 1.25 us -> 0.17 us  [shards(): slot = jnp.sum(earlier.astype(jnp.int32), axis=1)]
    convert_element_type x1, other arithmetic: 1.07 us -> 0.11 us  [shards(): unit = (values * lax.rsqrt(squares + 1e-06)[:, None]).astype(jnp.bfloat16)]
where the time goes in v8:
time: 92.3 us; the launch traced here: 91.9 us
  waiting for transfers between devices  36 us (39%)
  starting transfers between devices  26.6 us (29%)
  blocking collectives  20.5 us (22%)
  matrix products  3 us (3%)
  local copies, waits for them, and re-layouts  2.97 us (3%)
  other arithmetic  2.53 us (3%)
    all_to_all x1, blocking collectives, shards(): lax.all_to_all(wide, 'dp', split_axis=0, concat_axis=0, tiled=True)  20.5 us
    all_to_all x1, waiting for transfers between devices, shards(): lax.all_to_all(send, 'dp', split_axis=0, concat_axis=0, tiled=True)  20 us
    all_to_all x1, starting transfers between devices, shards(): lax.all_to_all(send, 'dp', split_axis=0, concat_axis=0, tiled=True)  18.4 us
    ppermute x1, waiting for transfers between devices, shards(): got_r = lax.ppermute(got, 'owner', to_prev)  8.02 us
    ppermute x1, waiting for transfers between devices, shards(): got_l = lax.ppermute(got, 'owner', to_next)  4.91 us
    ppermute x1, starting transfers between devices, shards(): got_r = lax.ppermute(got, 'owner', to_prev)  4.39 us
    ppermute x1, waiting for transfers between devices, shards(): lax.ppermute(returned[:, capacity:2 * capacity], 'owner', to_prev)  3.07 us
    ppermute x1, starting transfers between devices, shards(): got_l = lax.ppermute(got, 'owner', to_next)  1.92 us
  transfers between devices with their start and end apart: 4, of which 4 were waited for; matrix products, arithmetic and copies ran while one was open for 2% of the time, Pallas kernels for 0%

profile of v8, /device:TPU:1, one launch (start us, length us, event | category | flops | bytes accessed | tf_op | source)
XLA Modules:
  0.0 91.9 jit_solution(6075310953044125069)
XLA Ops:
  0.0 0.0 copy-start
  0.0 0.7 compare_select_fusion.1
  0.7 0.2 convert_reduce_fusion
  0.9 1.3 %fusion.4 = f32[128]{0:T(128)S(1)} fusion(bf16[128,1024]{1,0:T(8,128)(2,1)} %param.3), kind=kOutput, calls=%fused_computation.10 | convolution fusion | flops 33603456 | bytes 262656 | tf_op jit(solution)/shard_map/dot_general | solution.py:20
  2.2 0.0 copy-done
  2.2 0.1 multiply_convert_fusion
  2.3 0.1 broadcast_select_fusion
  2.4 0.3 convolution_convert_fusion
  2.8 1.4 %copy.9 = bf16[128,2,1152]{2,1,0:T(2,128)(2,1)} copy(bf16[128,2,1152]{2,0,1:T(8,128)(2,1)S(1)} %convolution_convert_fusion) | data formatting | bytes 1179648 | tf_op jit(solution)/shard_map/convert_element_type | solution.py:41
  4.2 18.4 %all-to-all-start = ((bf16[128,2,1152]{2,1,0:T(2,128)(2,1)}), bf16[128,2,1152]{2,1,0:T(2,128)(2,1)S(1)}, u32[]{:S(2)}, u32[]{:S(2)}) async-start(bf16[128,2,1152]{2,1,0:T(2,128)(2,1)} %copy.9), calls=%async_computation | async-start | bytes 1179648 | tf_op jit(solution)/shard_map/all_to_all | solution.py:42
  22.6 0.8 fusion.32
  23.5 20.0 %all-to-all-done = bf16[128,2,1152]{2,1,0:T(2,128)(2,1)S(1)} async-done(((bf16[128,2,1152]{2,1,0:T(2,128)(2,1)}), bf16[128,2,1152]{2,1,0:T(2,128)(2,1)S(1)}, u32[]{:S(2)}, u32[]{:S(2)}) %all-to-all-start) | async-done | bytes 589856 | tf_op jit(solution)/shard_map/all_to_all | solution.py:42
  43.5 0.2 reshape.149
  43.7 4.4 %collective-permute-start.1 = (bf16[256,1152]{1,0:T(8,128)(2,1)S(1)}, bf16[256,1152]{1,0:T(8,128)(2,1)S(1)}, u32[]{:S(2)}, u32[]{:S(2)}) collective-permute-start(bf16[256,1152]{1,0:T(8,128)(2,1)S(1)} %reshape.149), channel_id=1, source_target_pairs={{0,3},{1,0},{2,1},{3,2},{4,7},{5,4},{6,5},{7,6},{8,11},{9,8},{10,9... | collective-permute-start | bytes 1769480 | tf_op jit(solution)/shard_map/ppermute | solution.py:53
  48.1 1.9 %collective-permute-start = (bf16[256,1152]{1,0:T(8,128)(2,1)S(1)}, bf16[256,1152]{1,0:T(8,128)(2,1)S(1)}, u32[]{:S(2)}, u32[]{:S(2)}) collective-permute-start(bf16[256,1152]{1,0:T(8,128)(2,1)S(1)} %reshape.149), channel_id=1, source_target_pairs={{0,1},{1,2},{2,3},{3,0},{4,5},{5,6},{6,7},{7,4},{8,9},{9,10},{10,1... | collective-permute-start | bytes 1769480 | tf_op jit(solution)/shard_map/ppermute | solution.py:52
  50.1 0.2 fusion.23
  50.2 0.1 select_reduce_fusion.2
  50.3 0.4 fusion
  50.7 8.0 %collective-permute-done.1 = bf16[256,1152]{1,0:T(8,128)(2,1)S(1)} collective-permute-done((bf16[256,1152]{1,0:T(8,128)(2,1)S(1)}, bf16[256,1152]{1,0:T(8,128)(2,1)S(1)}, u32[]{:S(2)}, u32[]{:S(2)}) %collective-permute-start.1) | collective-permute-done | bytes 589856 | tf_op jit(solution)/shard_map/ppermute | solution.py:53
  58.7 0.1 fusion.22
  58.8 4.9 %collective-permute-done = bf16[256,1152]{1,0:T(8,128)(2,1)S(1)} collective-permute-done((bf16[256,1152]{1,0:T(8,128)(2,1)S(1)}, bf16[256,1152]{1,0:T(8,128)(2,1)S(1)}, u32[]{:S(2)}, u32[]{:S(2)}) %collective-permute-start) | collective-permute-done | bytes 589856 | tf_op jit(solution)/shard_map/ppermute | solution.py:52
  63.7 0.2 fusion.24
  63.9 0.4 fusion.2
  64.3 0.4 fusion.1
  64.6 0.1 max.33
  64.8 0.1 select_reduce_fusion.1
  64.9 0.4 fusion.3
  65.2 0.1 reshape.150
  65.4 0.1 select_maximum_fusion
  65.5 20.5 %all_to_all.17 = f32[128,1,128]{2,1,0:T(1,128)S(1)} all-to-all(f32[128,1,128]{2,1,0:T(1,128)S(1)} %bitcast.11), channel_id=1, replica_groups=mesh['dp'=128,'owner'=4] {'dp'}, dimensions={0} | all-to-all | bytes 131072 | tf_op jit(solution)/shard_map/all_to_all | solution.py:96
  86.0 0.1 slice.39
  86.1 1.9 %collective-permute-start.2 = (f32[128,2]{1,0:T(8,128)S(1)}, f32[128,2]{1,0:T(8,128)S(1)}, u32[]{:S(2)}, u32[]{:S(2)}) collective-permute-start(f32[128,2]{1,0:T(8,128)S(1)} %slice.39), channel_id=1, source_target_pairs={{0,3},{1,0},{2,1},{3,2},{4,7},{5,4},{6,5},{7,6},{8,11},{9,8},{10,9... | collective-permute-start | bytes 3080 | tf_op jit(solution)/shard_map/ppermute | solution.py:97
  88.0 3.1 %collective-permute-done.2 = f32[128,2]{1,0:T(8,128)S(1)} collective-permute-done((f32[128,2]{1,0:T(8,128)S(1)}, f32[128,2]{1,0:T(8,128)S(1)}, u32[]{:S(2)}, u32[]{:S(2)}) %collective-permute-start.2) | collective-permute-done | bytes 1056 | tf_op jit(solution)/shard_map/ppermute | solution.py:97
  91.1 0.1 broadcast_in_dim.71
  91.2 0.7 select_reduce_fusion
  (10 shorter events, 0.1 us)
Async XLA Ops:
  0.0 2.2 %copy-start = (bf16[128,1024]{1,0:T(8,128)(2,1)S(1)}, bf16[128,1024]{1,0:T(8,128)(2,1)}, u32[]{:S(2)}) copy-start(bf16[128,1024]{1,0:T(8,128)(2,1)} %param.3) | copy-start | bytes 786436
  4.2 39.3 %all-to-all-start = ((bf16[128,2,1152]{2,1,0:T(2,128)(2,1)}), bf16[128,2,1152]{2,1,0:T(2,128)(2,1)S(1)}, u32[]{:S(2)}, u32[]{:S(2)}) async-start(bf16[128,2,1152]{2,1,0:T(2,128)(2,1)} %copy.9), calls=%async_computation | async-start | bytes 1179648 | tf_op jit(solution)/shard_map/all_to_all | solution.py:42
  43.7 15.0 %collective-permute-start.1 = (bf16[256,1152]{1,0:T(8,128)(2,1)S(1)}, bf16[256,1152]{1,0:T(8,128)(2,1)S(1)}, u32[]{:S(2)}, u32[]{:S(2)}) collective-permute-start(bf16[256,1152]{1,0:T(8,128)(2,1)S(1)} %reshape.149), channel_id=1, source_target_pairs={{0,3},{1,0},{2,1},{3,2},{4,7},{5,4},{6,5},{7,6},{8,11},{9,8},{10,9... | collective-permute-start | bytes 1769480 | tf_op jit(solution)/shard_map/ppermute | solution.py:53
  48.1 15.6 %collective-permute-start = (bf16[256,1152]{1,0:T(8,128)(2,1)S(1)}, bf16[256,1152]{1,0:T(8,128)(2,1)S(1)}, u32[]{:S(2)}, u32[]{:S(2)}) collective-permute-start(bf16[256,1152]{1,0:T(8,128)(2,1)S(1)} %reshape.149), channel_id=1, source_target_pairs={{0,1},{1,2},{2,3},{3,0},{4,5},{5,6},{6,7},{7,4},{8,9},{9,10},{10,1... | collective-permute-start | bytes 1769480 | tf_op jit(solution)/shard_map/ppermute | solution.py:52
  86.1 5.0 %collective-permute-start.2 = (f32[128,2]{1,0:T(8,128)S(1)}, f32[128,2]{1,0:T(8,128)S(1)}, u32[]{:S(2)}, u32[]{:S(2)}) collective-permute-start(f32[128,2]{1,0:T(8,128)S(1)} %slice.39), channel_id=1, source_target_pairs={{0,3},{1,0},{2,1},{3,2},{4,7},{5,4},{6,5},{7,6},{8,11},{9,8},{10,9... | collective-permute-start | bytes 3080 | tf_op jit(solution)/shard_map/ppermute | solution.py:97

commit v9 on v8

--- a/solution.py
+++ b/solution.py
@@ -82,6 +82,7 @@
     partner = partner_of(mine_ids, here_owner)
     partner_l = partner_of(ids_l, (here_owner - 1) % n_owner)
     far = best_against(rows_l, ids_l, partner_l, rows_r, ids_r, False)
+    far_back = lax.ppermute(far, "owner", to_prev)
     best = jnp.maximum(
         jnp.maximum(-1.0, best_against(mine, mine_ids, partner, mine, mine_ids, True)),
         jnp.maximum(
@@ -89,13 +90,10 @@
             best_against(mine, mine_ids, partner, rows_r, ids_r, False),
         ),
     )
-    wide = jnp.concatenate(
-        [best.reshape(n_dp, capacity), far.reshape(n_dp, capacity)], axis=1
-    )
-    wide = jnp.pad(wide, ((0, 0), (0, LANES - 2 * capacity)))
+    best = jnp.maximum(best, far_back)
+    wide = jnp.pad(best.reshape(n_dp, capacity), ((0, 0), (0, LANES - capacity)))
     returned = lax.all_to_all(wide, "dp", split_axis=0, concat_axis=0, tiled=True)
-    far_here = lax.ppermute(returned[:, capacity : 2 * capacity], "owner", to_prev)
-    returned = jnp.maximum(returned[:, :capacity], far_here).reshape(slots)
+    returned = returned[:, :capacity].reshape(slots)
     pick = position[:, None] == jnp.arange(slots, dtype=jnp.int32)[None, :]
     return jnp.sum(jnp.where(pick, returned[None, :], 0.0), axis=1)
 

time: 92.3 us -> 92.5 us (level)
  blocking collectives: 20.5 us -> 0 us
  starting transfers between devices: 26.6 us -> 37 us
  waiting for transfers between devices: 36 us -> 46.2 us
    all_to_all x1 -> x0, blocking collectives: 20.5 us -> none  [shards(): lax.all_to_all(wide, 'dp', split_axis=0, concat_axis=0, tiled=True)]
    all_to_all x0 -> x1, waiting for transfers between devices: none -> 11.5 us  [shards(): lax.all_to_all(wide, 'dp', split_axis=0, concat_axis=0, tiled=True)]
    all_to_all x0 -> x1, starting transfers between devices: none -> 10.3 us  [shards(): lax.all_to_all(wide, 'dp', split_axis=0, concat_axis=0, tiled=True)]
    ppermute x1, waiting for transfers between devices: 3.07 us -> 1.67 us  [shards(): far_back = lax.ppermute(far, 'owner', to_prev)]
  transfers between devices with their start and end apart: 4 -> 5, of which waited for: 4 -> 5; matrix products, arithmetic and copies ran while one was open for 2% -> 2% of each run, Pallas kernels for 0% -> 0%
where the time goes in v9:
time: 92.5 us; the launch traced here: 92.2 us
  waiting for transfers between devices  46.2 us (50%)
  starting transfers between devices  37 us (40%)
  local copies, waits for them, and re-layouts  3.38 us (4%)
  matrix products  3 us (3%)
  other arithmetic  2.44 us (3%)
    all_to_all x1, waiting for transfers between devices, shards(): lax.all_to_all(send, 'dp', split_axis=0, concat_axis=0, tiled=True)  20 us
    all_to_all x1, starting transfers between devices, shards(): lax.all_to_all(send, 'dp', split_axis=0, concat_axis=0, tiled=True)  18.4 us
    all_to_all x1, waiting for transfers between devices, shards(): lax.all_to_all(wide, 'dp', split_axis=0, concat_axis=0, tiled=True)  11.5 us
    all_to_all x1, starting transfers between devices, shards(): lax.all_to_all(wide, 'dp', split_axis=0, concat_axis=0, tiled=True)  10.3 us
    ppermute x1, waiting for transfers between devices, shards(): got_r = lax.ppermute(got, 'owner', to_prev)  8.02 us
    ppermute x1, waiting for transfers between devices, shards(): got_l = lax.ppermute(got, 'owner', to_next)  4.91 us
    ppermute x1, starting transfers between devices, shards(): got_r = lax.ppermute(got, 'owner', to_prev)  4.39 us
    ppermute x1, starting transfers between devices, shards(): got_l = lax.ppermute(got, 'owner', to_next)  1.92 us
  transfers between devices with their start and end apart: 5, of which 5 were waited for; matrix products, arithmetic and copies ran while one was open for 2% of the time, Pallas kernels for 0%

profile of v9, /device:TPU:1, one launch (start us, length us, event | category | flops | bytes accessed | tf_op | source)
XLA Modules:
  0.0 92.2 jit_solution(14613840762902002774)
XLA Ops:
  0.0 0.0 copy-start
  0.0 0.7 compare_select_fusion.1
  0.7 0.2 convert_reduce_fusion
  0.9 1.3 %fusion.4 = f32[128]{0:T(128)S(1)} fusion(bf16[128,1024]{1,0:T(8,128)(2,1)} %param.3), kind=kOutput, calls=%fused_computation.10 | convolution fusion | flops 33603456 | bytes 262656 | tf_op jit(solution)/shard_map/dot_general | solution.py:20
  2.2 0.0 copy-done
  2.2 0.1 multiply_convert_fusion
  2.4 0.1 broadcast_select_fusion
  2.4 0.3 convolution_convert_fusion
  2.8 1.4 %copy.7 = bf16[128,2,1152]{2,1,0:T(2,128)(2,1)} copy(bf16[128,2,1152]{2,0,1:T(8,128)(2,1)S(1)} %convolution_convert_fusion) | data formatting | bytes 1179648 | tf_op jit(solution)/shard_map/convert_element_type | solution.py:41
  4.2 18.4 %all-to-all-start = ((bf16[128,2,1152]{2,1,0:T(2,128)(2,1)}), bf16[128,2,1152]{2,1,0:T(2,128)(2,1)S(1)}, u32[]{:S(2)}, u32[]{:S(2)}) async-start(bf16[128,2,1152]{2,1,0:T(2,128)(2,1)} %copy.7), calls=%async_computation | async-start | bytes 1179648 | tf_op jit(solution)/shard_map/all_to_all | solution.py:42
  22.6 0.8 fusion.32
  23.5 20.0 %all-to-all-done = bf16[128,2,1152]{2,1,0:T(2,128)(2,1)S(1)} async-done(((bf16[128,2,1152]{2,1,0:T(2,128)(2,1)}), bf16[128,2,1152]{2,1,0:T(2,128)(2,1)S(1)}, u32[]{:S(2)}, u32[]{:S(2)}) %all-to-all-start) | async-done | bytes 589856 | tf_op jit(solution)/shard_map/all_to_all | solution.py:42
  43.5 0.2 reshape.141
  43.7 4.4 %collective-permute-start.1 = (bf16[256,1152]{1,0:T(8,128)(2,1)S(1)}, bf16[256,1152]{1,0:T(8,128)(2,1)S(1)}, u32[]{:S(2)}, u32[]{:S(2)}) collective-permute-start(bf16[256,1152]{1,0:T(8,128)(2,1)S(1)} %reshape.141), channel_id=1, source_target_pairs={{0,3},{1,0},{2,1},{3,2},{4,7},{5,4},{6,5},{7,6},{8,11},{9,8},{10,9... | collective-permute-start | bytes 1769480 | tf_op jit(solution)/shard_map/ppermute | solution.py:53
  48.1 1.9 %collective-permute-start = (bf16[256,1152]{1,0:T(8,128)(2,1)S(1)}, bf16[256,1152]{1,0:T(8,128)(2,1)S(1)}, u32[]{:S(2)}, u32[]{:S(2)}) collective-permute-start(bf16[256,1152]{1,0:T(8,128)(2,1)S(1)} %reshape.141), channel_id=1, source_target_pairs={{0,1},{1,2},{2,3},{3,0},{4,5},{5,6},{6,7},{7,4},{8,9},{9,10},{10,1... | collective-permute-start | bytes 1769480 | tf_op jit(solution)/shard_map/ppermute | solution.py:52
  50.1 0.2 fusion.23
  50.2 0.1 select_reduce_fusion.2
  50.3 0.4 fusion
  50.7 8.0 %collective-permute-done.1 = bf16[256,1152]{1,0:T(8,128)(2,1)S(1)} collective-permute-done((bf16[256,1152]{1,0:T(8,128)(2,1)S(1)}, bf16[256,1152]{1,0:T(8,128)(2,1)S(1)}, u32[]{:S(2)}, u32[]{:S(2)}) %collective-permute-start.1) | collective-permute-done | bytes 589856 | tf_op jit(solution)/shard_map/ppermute | solution.py:53
  58.7 0.1 fusion.22
  58.8 4.9 %collective-permute-done = bf16[256,1152]{1,0:T(8,128)(2,1)S(1)} collective-permute-done((bf16[256,1152]{1,0:T(8,128)(2,1)S(1)}, bf16[256,1152]{1,0:T(8,128)(2,1)S(1)}, u32[]{:S(2)}, u32[]{:S(2)}) %collective-permute-start) | collective-permute-done | bytes 589856 | tf_op jit(solution)/shard_map/ppermute | solution.py:52
  63.7 0.2 fusion.24
  63.9 0.1 select_reduce_fusion.1
  64.0 0.3 fusion.3
  64.3 1.9 %collective-permute-start.2 = (f32[256]{0:T(256)S(1)}, f32[256]{0:T(256)S(1)}, u32[]{:S(2)}, u32[]{:S(2)}) collective-permute-start(f32[256]{0:T(256)S(1)} %fusion.3), channel_id=1, source_target_pairs={{0,3},{1,0},{2,1},{3,2},{4,7},{5,4},{6,5},{7,6},{8,11},{9,8},{10,9... | collective-permute-start | bytes 3080 | tf_op jit(solution)/shard_map/ppermute | solution.py:85
  66.3 0.4 fusion.2
  66.6 0.4 fusion.1
  67.0 1.7 %collective-permute-done.2 = f32[256]{0:T(256)S(1)} collective-permute-done((f32[256]{0:T(256)S(1)}, f32[256]{0:T(256)S(1)}, u32[]{:S(2)}, u32[]{:S(2)}) %collective-permute-start.2) | collective-permute-done | bytes 1056 | tf_op jit(solution)/shard_map/ppermute | solution.py:85
  68.7 0.1 reshape.142
  68.8 0.6 pad.4
  69.4 10.3 %all-to-all-start.1 = ((f32[128,1,128]{2,1,0:T(1,128)}), f32[128,1,128]{2,1,0:T(1,128)S(1)}, u32[]{:S(2)}, u32[]{:S(2)}) async-start(f32[128,1,128]{2,1,0:T(1,128)} %bitcast.2), calls=%async_computation.1 | async-start | bytes 131072 | tf_op jit(solution)/shard_map/all_to_all | solution.py:95
  79.8 11.5 %all-to-all-done.1 = f32[128,1,128]{2,1,0:T(1,128)S(1)} async-done(((f32[128,1,128]{2,1,0:T(1,128)}), f32[128,1,128]{2,1,0:T(1,128)S(1)}, u32[]{:S(2)}, u32[]{:S(2)}) %all-to-all-start.1) | async-done | bytes 65568 | tf_op jit(solution)/shard_map/all_to_all | solution.py:95
  91.3 0.1 broadcast_in_dim.71
  91.5 0.7 select_reduce_fusion
  (9 shorter events, 0.1 us)
Async XLA Ops:
  0.0 2.2 %copy-start = (bf16[128,1024]{1,0:T(8,128)(2,1)S(1)}, bf16[128,1024]{1,0:T(8,128)(2,1)}, u32[]{:S(2)}) copy-start(bf16[128,1024]{1,0:T(8,128)(2,1)} %param.3) | copy-start | bytes 786436
  4.2 39.3 %all-to-all-start = ((bf16[128,2,1152]{2,1,0:T(2,128)(2,1)}), bf16[128,2,1152]{2,1,0:T(2,128)(2,1)S(1)}, u32[]{:S(2)}, u32[]{:S(2)}) async-start(bf16[128,2,1152]{2,1,0:T(2,128)(2,1)} %copy.7), calls=%async_computation | async-start | bytes 1179648 | tf_op jit(solution)/shard_map/all_to_all | solution.py:42
  43.7 15.0 %collective-permute-start.1 = (bf16[256,1152]{1,0:T(8,128)(2,1)S(1)}, bf16[256,1152]{1,0:T(8,128)(2,1)S(1)}, u32[]{:S(2)}, u32[]{:S(2)}) collective-permute-start(bf16[256,1152]{1,0:T(8,128)(2,1)S(1)} %reshape.141), channel_id=1, source_target_pairs={{0,3},{1,0},{2,1},{3,2},{4,7},{5,4},{6,5},{7,6},{8,11},{9,8},{10,9... | collective-permute-start | bytes 1769480 | tf_op jit(solution)/shard_map/ppermute | solution.py:53
  48.1 15.6 %collective-permute-start = (bf16[256,1152]{1,0:T(8,128)(2,1)S(1)}, bf16[256,1152]{1,0:T(8,128)(2,1)S(1)}, u32[]{:S(2)}, u32[]{:S(2)}) collective-permute-start(bf16[256,1152]{1,0:T(8,128)(2,1)S(1)} %reshape.141), channel_id=1, source_target_pairs={{0,1},{1,2},{2,3},{3,0},{4,5},{5,6},{6,7},{7,4},{8,9},{9,10},{10,1... | collective-permute-start | bytes 1769480 | tf_op jit(solution)/shard_map/ppermute | solution.py:52
  64.3 4.3 %collective-permute-start.2 = (f32[256]{0:T(256)S(1)}, f32[256]{0:T(256)S(1)}, u32[]{:S(2)}, u32[]{:S(2)}) collective-permute-start(f32[256]{0:T(256)S(1)} %fusion.3), channel_id=1, source_target_pairs={{0,3},{1,0},{2,1},{3,2},{4,7},{5,4},{6,5},{7,6},{8,11},{9,8},{10,9... | collective-permute-start | bytes 3080 | tf_op jit(solution)/shard_map/ppermute | solution.py:85
  69.4 21.9 %all-to-all-start.1 = ((f32[128,1,128]{2,1,0:T(1,128)}), f32[128,1,128]{2,1,0:T(1,128)S(1)}, u32[]{:S(2)}, u32[]{:S(2)}) async-start(f32[128,1,128]{2,1,0:T(1,128)} %bitcast.2), calls=%async_computation.1 | async-start | bytes 131072 | tf_op jit(solution)/shard_map/all_to_all | solution.py:95

commit v10 on v9

--- a/solution.py
+++ b/solution.py
@@ -14,6 +14,7 @@
     assert n_owner == 4
     capacity = 2 * rows // n_dp
     slots = capacity * n_dp
+    assert slots <= width
     here_owner = lax.axis_index("owner")
     here_dp = lax.axis_index("dp")
     values = embeddings.astype(jnp.float32)
@@ -49,16 +50,18 @@
 
     to_next = [(i, (i + 1) % n_owner) for i in range(n_owner)]
     to_prev = [(i, (i - 1) % n_owner) for i in range(n_owner)]
-    got_l = lax.ppermute(got, "owner", to_next)
-    got_r = lax.ppermute(got, "owner", to_prev)
+    code_rows = jnp.pad(got[:, width].reshape(1, slots), ((0, 15), (0, width - slots)))
+    block = jnp.concatenate([mine, code_rows], axis=0)
+    got_l = lax.ppermute(block, "owner", to_next)
+    got_r = lax.ppermute(block, "owner", to_prev)
 
     def ids_of(block, owner_index):
-        c1 = block[:, width].astype(jnp.int32)
+        c1 = block[slots, :slots].astype(jnp.int32)
         return jnp.where(c1 > 0, (here_dp * n_owner + owner_index) * CPD + c1 - 1, -1)
 
-    rows_l = got_l[:, :width]
+    rows_l = got_l[:slots]
     ids_l = ids_of(got_l, (here_owner - 1) % n_owner)
-    rows_r = got_r[:, :width]
+    rows_r = got_r[:slots]
     ids_r = ids_of(got_r, (here_owner + 1) % n_owner)
 
     def partner_of(ids, owner_index):

time: 92.5 us -> 92 us (level)
  transfers between devices with their start and end apart: 5 -> 5, of which waited for: 5 -> 4; matrix products, arithmetic and copies ran while one was open for 2% -> 2% of each run, Pallas kernels for 0% -> 0%
where the time goes in v10:
time: 92 us; the launch traced here: 91.6 us
  waiting for transfers between devices  45.6 us (50%)
  starting transfers between devices  37 us (40%)
  local copies, waits for them, and re-layouts  3.56 us (4%)
  matrix products  3.02 us (3%)
  other arithmetic  2.25 us (2%)
    all_to_all x1, waiting for transfers between devices, shards(): lax.all_to_all(send, 'dp', split_axis=0, concat_axis=0, tiled=True)  20 us
    all_to_all x1, starting transfers between devices, shards(): lax.all_to_all(send, 'dp', split_axis=0, concat_axis=0, tiled=True)  18.4 us
    ppermute x1, waiting for transfers between devices, shards(): got_l = lax.ppermute(block, 'owner', to_next)  12.4 us
    all_to_all x1, waiting for transfers between devices, shards(): lax.all_to_all(wide, 'dp', split_axis=0, concat_axis=0, tiled=True)  11.5 us
    all_to_all x1, starting transfers between devices, shards(): lax.all_to_all(wide, 'dp', split_axis=0, concat_axis=0, tiled=True)  10.3 us
    ppermute x1, starting transfers between devices, shards(): got_r = lax.ppermute(block, 'owner', to_prev)  4.39 us
    ppermute x1, starting transfers between devices, shards(): far_back = lax.ppermute(far, 'owner', to_prev)  1.92 us
    ppermute x1, starting transfers between devices, shards(): got_l = lax.ppermute(block, 'owner', to_next)  1.92 us
  transfers between devices with their start and end apart: 5, of which 4 were waited for; matrix products, arithmetic and copies ran while one was open for 2% of the time, Pallas kernels for 0%

profile of v10, /device:TPU:1, one launch (start us, length us, event | category | flops | bytes accessed | tf_op | source)
XLA Modules:
  0.0 91.6 jit_solution(17880828818418103237)
XLA Ops:
  0.0 0.0 copy-start
  0.0 0.7 compare_select_fusion.3
  0.7 0.2 convert_reduce_fusion
  0.9 1.3 %fusion.5 = f32[128]{0:T(128)S(1)} fusion(bf16[128,1024]{1,0:T(8,128)(2,1)} %param.3), kind=kOutput, calls=%fused_computation.12 | convolution fusion | flops 33603456 | bytes 262656 | tf_op jit(solution)/shard_map/dot_general | solution.py:21
  2.2 0.0 copy-done
  2.2 0.1 multiply_convert_fusion
  2.4 0.1 broadcast_select_fusion
  2.4 0.3 convolution_convert_fusion
  2.8 1.4 %copy.7 = bf16[128,2,1152]{2,1,0:T(2,128)(2,1)} copy(bf16[128,2,1152]{2,0,1:T(8,128)(2,1)S(1)} %convolution_convert_fusion) | data formatting | bytes 1179648 | tf_op jit(solution)/shard_map/convert_element_type | solution.py:42
  4.2 18.4 %all-to-all-start = ((bf16[128,2,1152]{2,1,0:T(2,128)(2,1)}), bf16[128,2,1152]{2,1,0:T(2,128)(2,1)S(1)}, u32[]{:S(2)}, u32[]{:S(2)}) async-start(bf16[128,2,1152]{2,1,0:T(2,128)(2,1)} %copy.7), calls=%async_computation | async-start | bytes 1179648 | tf_op jit(solution)/shard_map/all_to_all | solution.py:43
  22.6 0.8 fusion.28
  23.5 20.0 %all-to-all-done = bf16[128,2,1152]{2,1,0:T(2,128)(2,1)S(1)} async-done(((bf16[128,2,1152]{2,1,0:T(2,128)(2,1)}), bf16[128,2,1152]{2,1,0:T(2,128)(2,1)S(1)}, u32[]{:S(2)}, u32[]{:S(2)}) %all-to-all-start) | async-done | bytes 589856 | tf_op jit(solution)/shard_map/all_to_all | solution.py:43
  43.5 0.2 reshape.120
  43.7 0.1 slice_reduce_fusion
  43.9 0.1 slice.30
  44.0 4.4 %collective-permute-start.1 = (bf16[272,1024]{1,0:T(8,128)(2,1)S(1)}, bf16[272,1024]{1,0:T(8,128)(2,1)S(1)}, u32[]{:S(2)}, u32[]{:S(2)}) collective-permute-start(bf16[272,1024]{1,0:T(8,128)(2,1)S(1)} %fusion.6), channel_id=1, source_target_pairs={{0,3},{1,0},{2,1},{3,2},{4,7},{5,4},{6,5},{7,6},{8,11},{9,8},{10,9... | collective-permute-start | bytes 1671176 | tf_op jit(solution)/shard_map/ppermute | solution.py:56
  48.4 1.9 %collective-permute-start = (bf16[272,1024]{1,0:T(8,128)(2,1)S(1)}, bf16[272,1024]{1,0:T(8,128)(2,1)S(1)}, u32[]{:S(2)}, u32[]{:S(2)}) collective-permute-start(bf16[272,1024]{1,0:T(8,128)(2,1)S(1)} %fusion.6), channel_id=1, source_target_pairs={{0,1},{1,2},{2,3},{3,0},{4,5},{5,6},{6,7},{7,4},{8,9},{9,10},{10,1... | collective-permute-start | bytes 1671176 | tf_op jit(solution)/shard_map/ppermute | solution.py:55
  50.3 0.2 fusion.17
  50.5 0.1 select_reduce_fusion.2
  50.6 0.4 fusion
  50.9 12.4 %collective-permute-done = bf16[272,1024]{1,0:T(8,128)(2,1)S(1)} collective-permute-done((bf16[272,1024]{1,0:T(8,128)(2,1)S(1)}, bf16[272,1024]{1,0:T(8,128)(2,1)S(1)}, u32[]{:S(2)}, u32[]{:S(2)}) %collective-permute-start) | collective-permute-done | bytes 557088 | tf_op jit(solution)/shard_map/ppermute | solution.py:55
  63.3 0.1 select_reduce_fusion.1
  63.4 0.0 collective-permute-done.1
  63.4 0.4 fusion.3
  63.8 1.9 %collective-permute-start.2 = (f32[256]{0:T(256)S(1)}, f32[256]{0:T(256)S(1)}, u32[]{:S(2)}, u32[]{:S(2)}) collective-permute-start(f32[256]{0:T(256)S(1)} %fusion.3), channel_id=1, source_target_pairs={{0,3},{1,0},{2,1},{3,2},{4,7},{5,4},{6,5},{7,6},{8,11},{9,8},{10,9... | collective-permute-start | bytes 3080 | tf_op jit(solution)/shard_map/ppermute | solution.py:88
  65.7 0.4 fusion.2
  66.1 0.4 fusion.1
  66.4 1.7 %collective-permute-done.2 = f32[256]{0:T(256)S(1)} collective-permute-done((f32[256]{0:T(256)S(1)}, f32[256]{0:T(256)S(1)}, u32[]{:S(2)}, u32[]{:S(2)}) %collective-permute-start.2) | collective-permute-done | bytes 1056 | tf_op jit(solution)/shard_map/ppermute | solution.py:88
  68.1 0.1 reshape.121
  68.3 0.6 pad.9
  68.9 10.3 %all-to-all-start.1 = ((f32[128,1,128]{2,1,0:T(1,128)}), f32[128,1,128]{2,1,0:T(1,128)S(1)}, u32[]{:S(2)}, u32[]{:S(2)}) async-start(f32[128,1,128]{2,1,0:T(1,128)} %bitcast.4), calls=%async_computation.1 | async-start | bytes 131072 | tf_op jit(solution)/shard_map/all_to_all | solution.py:98
  79.3 11.5 %all-to-all-done.1 = f32[128,1,128]{2,1,0:T(1,128)S(1)} async-done(((f32[128,1,128]{2,1,0:T(1,128)}), f32[128,1,128]{2,1,0:T(1,128)S(1)}, u32[]{:S(2)}, u32[]{:S(2)}) %all-to-all-start.1) | async-done | bytes 65568 | tf_op jit(solution)/shard_map/all_to_all | solution.py:98
  90.8 0.1 broadcast_in_dim.71
  90.9 0.7 select_reduce_fusion
  (12 shorter events, 0.2 us)
Async XLA Ops:
  0.0 2.2 %copy-start = (bf16[128,1024]{1,0:T(8,128)(2,1)S(1)}, bf16[128,1024]{1,0:T(8,128)(2,1)}, u32[]{:S(2)}) copy-start(bf16[128,1024]{1,0:T(8,128)(2,1)} %param.3) | copy-start | bytes 786436
  4.2 39.3 %all-to-all-start = ((bf16[128,2,1152]{2,1,0:T(2,128)(2,1)}), bf16[128,2,1152]{2,1,0:T(2,128)(2,1)S(1)}, u32[]{:S(2)}, u32[]{:S(2)}) async-start(bf16[128,2,1152]{2,1,0:T(2,128)(2,1)} %copy.7), calls=%async_computation | async-start | bytes 1179648 | tf_op jit(solution)/shard_map/all_to_all | solution.py:43
  44.0 19.4 %collective-permute-start.1 = (bf16[272,1024]{1,0:T(8,128)(2,1)S(1)}, bf16[272,1024]{1,0:T(8,128)(2,1)S(1)}, u32[]{:S(2)}, u32[]{:S(2)}) collective-permute-start(bf16[272,1024]{1,0:T(8,128)(2,1)S(1)} %fusion.6), channel_id=1, source_target_pairs={{0,3},{1,0},{2,1},{3,2},{4,7},{5,4},{6,5},{7,6},{8,11},{9,8},{10,9... | collective-permute-start | bytes 1671176 | tf_op jit(solution)/shard_map/ppermute | solution.py:56
  48.4 14.9 %collective-permute-start = (bf16[272,1024]{1,0:T(8,128)(2,1)S(1)}, bf16[272,1024]{1,0:T(8,128)(2,1)S(1)}, u32[]{:S(2)}, u32[]{:S(2)}) collective-permute-start(bf16[272,1024]{1,0:T(8,128)(2,1)S(1)} %fusion.6), channel_id=1, source_target_pairs={{0,1},{1,2},{2,3},{3,0},{4,5},{5,6},{6,7},{7,4},{8,9},{9,10},{10,1... | collective-permute-start | bytes 1671176 | tf_op jit(solution)/shard_map/ppermute | solution.py:55
  63.8 4.3 %collective-permute-start.2 = (f32[256]{0:T(256)S(1)}, f32[256]{0:T(256)S(1)}, u32[]{:S(2)}, u32[]{:S(2)}) collective-permute-start(f32[256]{0:T(256)S(1)} %fusion.3), channel_id=1, source_target_pairs={{0,3},{1,0},{2,1},{3,2},{4,7},{5,4},{6,5},{7,6},{8,11},{9,8},{10,9... | collective-permute-start | bytes 3080 | tf_op jit(solution)/shard_map/ppermute | solution.py:88
  68.9 21.9 %all-to-all-start.1 = ((f32[128,1,128]{2,1,0:T(1,128)}), f32[128,1,128]{2,1,0:T(1,128)S(1)}, u32[]{:S(2)}, u32[]{:S(2)}) async-start(f32[128,1,128]{2,1,0:T(1,128)} %bitcast.4), calls=%async_computation.1 | async-start | bytes 131072 | tf_op jit(solution)/shard_map/all_to_all | solution.py:98

commit v11 on v10

--- a/solution.py
+++ b/solution.py
@@ -40,16 +40,21 @@
     send = jnp.einsum(
         "tkr,rw->tkw", place.astype(jnp.bfloat16), packed, preferred_element_type=jnp.float32
     ).astype(jnp.bfloat16)
+    to_next = [(i, (i + 1) % n_owner) for i in range(n_owner)]
+    to_prev = [(i, (i - 1) % n_owner) for i in range(n_owner)]
+    warm = (
+        lax.ppermute(assignment[:8], "owner", to_next),
+        lax.ppermute(assignment[:8], "owner", to_prev),
+    )
     got = lax.all_to_all(send, "dp", split_axis=0, concat_axis=0, tiled=True).reshape(
         slots, width + LANES
     )
+    first_id = jnp.where(warm[0][0] + warm[1][0] < 0, 0, first_id)
 
     mine = got[:, :width]
     c1 = got[:, width].astype(jnp.int32)
     mine_ids = jnp.where(c1 > 0, first_id + c1 - 1, -1)
 
-    to_next = [(i, (i + 1) % n_owner) for i in range(n_owner)]
-    to_prev = [(i, (i - 1) % n_owner) for i in range(n_owner)]
     code_rows = jnp.pad(got[:, width].reshape(1, slots), ((0, 15), (0, width - slots)))
     block = jnp.concatenate([mine, code_rows], axis=0)
     got_l = lax.ppermute(block, "owner", to_next)

time: 92 us -> 92.2 us (level)
  starting transfers between devices: 37 us -> 43.6 us
  waiting for transfers between devices: 45.6 us -> 39 us
    all_to_all x1, waiting for transfers between devices: 20 us -> 13.2 us  [shards(): lax.all_to_all(send, 'dp', split_axis=0, concat_axis=0, tiled=True)]
    ppermute x0 -> x2, starting transfers between devices: none -> 6.49 us  [the longest x1 3.38 us: shards(): lax.ppermute(assignment[:8], 'owner', to_prev)]
  transfers between devices with their start and end apart: 5 -> 7, of which waited for: 4 -> 5; matrix products, arithmetic and copies ran while one was open for 2% -> 2% of each run, Pallas kernels for 0% -> 0%
where the time goes in v11:
time: 92.2 us; the launch traced here: 91.8 us
  starting transfers between devices  43.6 us (47%)
  waiting for transfers between devices  39 us (42%)
  local copies, waits for them, and re-layouts  3.56 us (4%)
  matrix products  3.02 us (3%)
  other arithmetic  2.26 us (2%)
    all_to_all x1, starting transfers between devices, shards(): lax.all_to_all(send, 'dp', split_axis=0, concat_axis=0, tiled=True)  18.6 us
    all_to_all x1, waiting for transfers between devices, shards(): lax.all_to_all(send, 'dp', split_axis=0, concat_axis=0, tiled=True)  13.2 us
    ppermute x1, waiting for transfers between devices, shards(): got_l = lax.ppermute(block, 'owner', to_next)  12.4 us
    all_to_all x1, waiting for transfers between devices, shards(): lax.all_to_all(wide, 'dp', split_axis=0, concat_axis=0, tiled=True)  11.5 us
    all_to_all x1, starting transfers between devices, shards(): lax.all_to_all(wide, 'dp', split_axis=0, concat_axis=0, tiled=True)  10.3 us
    ppermute x1, starting transfers between devices, shards(): got_r = lax.ppermute(block, 'owner', to_prev)  4.39 us
    ppermute x1, starting transfers between devices, shards(): lax.ppermute(assignment[:8], 'owner', to_prev)  3.38 us
    ppermute x1, starting transfers between devices, shards(): lax.ppermute(assignment[:8], 'owner', to_next)  3.12 us
  transfers between devices with their start and end apart: 7, of which 5 were waited for; matrix products, arithmetic and copies ran while one was open for 2% of the time, Pallas kernels for 0%

profile of v11, /device:TPU:1, one launch (start us, length us, event | category | flops | bytes accessed | tf_op | source)
XLA Modules:
  0.0 91.8 jit_solution(295411485758137835)
XLA Ops:
  0.0 0.0 copy-start
  0.0 0.7 compare_select_fusion.3
  0.7 0.2 convert_reduce_fusion
  0.9 1.3 %fusion.5 = f32[128]{0:T(128)S(1)} fusion(bf16[128,1024]{1,0:T(8,128)(2,1)} %param.3), kind=kOutput, calls=%fused_computation.12 | convolution fusion | flops 33603456 | bytes 262656 | tf_op jit(solution)/shard_map/dot_general | solution.py:21
  2.2 0.0 copy-done
  2.2 0.1 multiply_convert_fusion
  2.4 0.1 broadcast_select_fusion
  2.4 0.3 convolution_convert_fusion
  2.8 1.4 %copy.7 = bf16[128,2,1152]{2,1,0:T(2,128)(2,1)} copy(bf16[128,2,1152]{2,0,1:T(8,128)(2,1)S(1)} %convolution_convert_fusion) | data formatting | bytes 1179648 | tf_op jit(solution)/shard_map/convert_element_type | solution.py:42
  4.2 0.0 copy-start.1
  4.2 18.6 %all-to-all-start = ((bf16[128,2,1152]{2,1,0:T(2,128)(2,1)}), bf16[128,2,1152]{2,1,0:T(2,128)(2,1)S(1)}, u32[]{:S(2)}, u32[]{:S(2)}) async-start(bf16[128,2,1152]{2,1,0:T(2,128)(2,1)} %copy.7), calls=%async_computation | async-start | bytes 1179648 | tf_op jit(solution)/shard_map/all_to_all | solution.py:49
  22.7 0.0 copy-done.1
  22.7 3.1 %collective-permute-start = (s32[8]{0:T(128)S(1)}, s32[8]{0:T(128)S(1)}, u32[]{:S(2)}, u32[]{:S(2)}) collective-permute-start(s32[8]{0:T(128)S(1)} %bitcast.22), channel_id=1, source_target_pairs={{0,1},{1,2},{2,3},{3,0},{4,5},{5,6},{6,7},{7,4},{8,9},{9,10},{10,1... | collective-permute-start | bytes 104 | tf_op jit(solution)/shard_map/ppermute | solution.py:46
  25.9 3.4 %collective-permute-start.1 = (s32[8]{0:T(128)S(1)}, s32[8]{0:T(128)S(1)}, u32[]{:S(2)}, u32[]{:S(2)}) collective-permute-start(s32[8]{0:T(128)S(1)} %bitcast.23), channel_id=1, source_target_pairs={{0,3},{1,0},{2,1},{3,2},{4,7},{5,4},{6,5},{7,6},{8,11},{9,8},{10,9... | collective-permute-start | bytes 104 | tf_op jit(solution)/shard_map/ppermute | solution.py:47
  29.3 0.8 fusion.28
  30.1 0.0 collective-permute-done
  30.1 0.3 collective-permute-done.1
  30.5 13.2 %all-to-all-done = bf16[128,2,1152]{2,1,0:T(2,128)(2,1)S(1)} async-done(((bf16[128,2,1152]{2,1,0:T(2,128)(2,1)}), bf16[128,2,1152]{2,1,0:T(2,128)(2,1)S(1)}, u32[]{:S(2)}, u32[]{:S(2)}) %all-to-all-start) | async-done | bytes 589856 | tf_op jit(solution)/shard_map/all_to_all | solution.py:49
  43.6 0.2 reshape.123
  43.9 0.1 slice_reduce_fusion
  44.0 0.1 slice.43
  44.1 4.4 %collective-permute-start.3 = (bf16[272,1024]{1,0:T(8,128)(2,1)S(1)}, bf16[272,1024]{1,0:T(8,128)(2,1)S(1)}, u32[]{:S(2)}, u32[]{:S(2)}) collective-permute-start(bf16[272,1024]{1,0:T(8,128)(2,1)S(1)} %fusion.6), channel_id=1, source_target_pairs={{0,3},{1,0},{2,1},{3,2},{4,7},{5,4},{6,5},{7,6},{8,11},{9,8},{10,9... | collective-permute-start | bytes 1671176 | tf_op jit(solution)/shard_map/ppermute | solution.py:61
  48.5 1.9 %collective-permute-start.2 = (bf16[272,1024]{1,0:T(8,128)(2,1)S(1)}, bf16[272,1024]{1,0:T(8,128)(2,1)S(1)}, u32[]{:S(2)}, u32[]{:S(2)}) collective-permute-start(bf16[272,1024]{1,0:T(8,128)(2,1)S(1)} %fusion.6), channel_id=1, source_target_pairs={{0,1},{1,2},{2,3},{3,0},{4,5},{5,6},{6,7},{7,4},{8,9},{9,10},{10,1... | collective-permute-start | bytes 1671176 | tf_op jit(solution)/shard_map/ppermute | solution.py:60
  50.4 0.2 fusion.17
  50.6 0.1 select_reduce_fusion.2
  50.7 0.4 fusion
  51.1 12.4 %collective-permute-done.2 = bf16[272,1024]{1,0:T(8,128)(2,1)S(1)} collective-permute-done((bf16[272,1024]{1,0:T(8,128)(2,1)S(1)}, bf16[272,1024]{1,0:T(8,128)(2,1)S(1)}, u32[]{:S(2)}, u32[]{:S(2)}) %collective-permute-start.2) | collective-permute-done | bytes 557088 | tf_op jit(solution)/shard_map/ppermute | solution.py:60
  63.5 0.1 select_reduce_fusion.1
  63.5 0.0 collective-permute-done.3
  63.6 0.4 fusion.3
  63.9 1.9 %collective-permute-start.4 = (f32[256]{0:T(256)S(1)}, f32[256]{0:T(256)S(1)}, u32[]{:S(2)}, u32[]{:S(2)}) collective-permute-start(f32[256]{0:T(256)S(1)} %fusion.3), channel_id=1, source_target_pairs={{0,3},{1,0},{2,1},{3,2},{4,7},{5,4},{6,5},{7,6},{8,11},{9,8},{10,9... | collective-permute-start | bytes 3080 | tf_op jit(solution)/shard_map/ppermute | solution.py:93
  65.9 0.4 fusion.2
  66.2 0.4 fusion.1
  66.6 1.7 %collective-permute-done.4 = f32[256]{0:T(256)S(1)} collective-permute-done((f32[256]{0:T(256)S(1)}, f32[256]{0:T(256)S(1)}, u32[]{:S(2)}, u32[]{:S(2)}) %collective-permute-start.4) | collective-permute-done | bytes 1056 | tf_op jit(solution)/shard_map/ppermute | solution.py:93
  68.3 0.1 reshape.124
  68.4 0.6 pad.9
  69.0 10.3 %all-to-all-start.1 = ((f32[128,1,128]{2,1,0:T(1,128)}), f32[128,1,128]{2,1,0:T(1,128)S(1)}, u32[]{:S(2)}, u32[]{:S(2)}) async-start(f32[128,1,128]{2,1,0:T(1,128)} %bitcast.5), calls=%async_computation.1 | async-start | bytes 131072 | tf_op jit(solution)/shard_map/all_to_all | solution.py:103
  79.4 11.5 %all-to-all-done.1 = f32[128,1,128]{2,1,0:T(1,128)S(1)} async-done(((f32[128,1,128]{2,1,0:T(1,128)}), f32[128,1,128]{2,1,0:T(1,128)S(1)}, u32[]{:S(2)}, u32[]{:S(2)}) %all-to-all-start.1) | async-done | bytes 65568 | tf_op jit(solution)/shard_map/all_to_all | solution.py:103
  90.9 0.1 broadcast_in_dim.71
  91.1 0.7 select_reduce_fusion
  (12 shorter events, 0.2 us)
Async XLA Ops:
  0.0 2.2 %copy-start = (bf16[128,1024]{1,0:T(8,128)(2,1)S(1)}, bf16[128,1024]{1,0:T(8,128)(2,1)}, u32[]{:S(2)}) copy-start(bf16[128,1024]{1,0:T(8,128)(2,1)} %param.3) | copy-start | bytes 786436
  4.2 18.6 %copy-start.1 = (s32[128]{0:T(128)S(1)}, s32[128]{0:T(128)}, u32[]{:S(2)}) copy-start(s32[128]{0:T(128)} %param.4) | copy-start | bytes 1540
  4.2 39.5 %all-to-all-start = ((bf16[128,2,1152]{2,1,0:T(2,128)(2,1)}), bf16[128,2,1152]{2,1,0:T(2,128)(2,1)S(1)}, u32[]{:S(2)}, u32[]{:S(2)}) async-start(bf16[128,2,1152]{2,1,0:T(2,128)(2,1)} %copy.7), calls=%async_computation | async-start | bytes 1179648 | tf_op jit(solution)/shard_map/all_to_all | solution.py:49
  22.7 7.4 %collective-permute-start = (s32[8]{0:T(128)S(1)}, s32[8]{0:T(128)S(1)}, u32[]{:S(2)}, u32[]{:S(2)}) collective-permute-start(s32[8]{0:T(128)S(1)} %bitcast.22), channel_id=1, source_target_pairs={{0,1},{1,2},{2,3},{3,0},{4,5},{5,6},{6,7},{7,4},{8,9},{9,10},{10,1... | collective-permute-start | bytes 104 | tf_op jit(solution)/shard_map/ppermute | solution.py:46
  25.9 4.6 %collective-permute-start.1 = (s32[8]{0:T(128)S(1)}, s32[8]{0:T(128)S(1)}, u32[]{:S(2)}, u32[]{:S(2)}) collective-permute-start(s32[8]{0:T(128)S(1)} %bitcast.23), channel_id=1, source_target_pairs={{0,3},{1,0},{2,1},{3,2},{4,7},{5,4},{6,5},{7,6},{8,11},{9,8},{10,9... | collective-permute-start | bytes 104 | tf_op jit(solution)/shard_map/ppermute | solution.py:47
  44.1 19.4 %collective-permute-start.3 = (bf16[272,1024]{1,0:T(8,128)(2,1)S(1)}, bf16[272,1024]{1,0:T(8,128)(2,1)S(1)}, u32[]{:S(2)}, u32[]{:S(2)}) collective-permute-start(bf16[272,1024]{1,0:T(8,128)(2,1)S(1)} %fusion.6), channel_id=1, source_target_pairs={{0,3},{1,0},{2,1},{3,2},{4,7},{5,4},{6,5},{7,6},{8,11},{9,8},{10,9... | collective-permute-start | bytes 1671176 | tf_op jit(solution)/shard_map/ppermute | solution.py:61
  48.5 14.9 %collective-permute-start.2 = (bf16[272,1024]{1,0:T(8,128)(2,1)S(1)}, bf16[272,1024]{1,0:T(8,128)(2,1)S(1)}, u32[]{:S(2)}, u32[]{:S(2)}) collective-permute-start(bf16[272,1024]{1,0:T(8,128)(2,1)S(1)} %fusion.6), channel_id=1, source_target_pairs={{0,1},{1,2},{2,3},{3,0},{4,5},{5,6},{6,7},{7,4},{8,9},{9,10},{10,1... | collective-permute-start | bytes 1671176 | tf_op jit(solution)/shard_map/ppermute | solution.py:60
  63.9 4.3 %collective-permute-start.4 = (f32[256]{0:T(256)S(1)}, f32[256]{0:T(256)S(1)}, u32[]{:S(2)}, u32[]{:S(2)}) collective-permute-start(f32[256]{0:T(256)S(1)} %fusion.3), channel_id=1, source_target_pairs={{0,3},{1,0},{2,1},{3,2},{4,7},{5,4},{6,5},{7,6},{8,11},{9,8},{10,9... | collective-permute-start | bytes 3080 | tf_op jit(solution)/shard_map/ppermute | solution.py:93
  69.0 21.9 %all-to-all-start.1 = ((f32[128,1,128]{2,1,0:T(1,128)}), f32[128,1,128]{2,1,0:T(1,128)S(1)}, u32[]{:S(2)}, u32[]{:S(2)}) async-start(f32[128,1,128]{2,1,0:T(1,128)} %bitcast.5), calls=%async_computation.1 | async-start | bytes 131072 | tf_op jit(solution)/shard_map/all_to_all | solution.py:103

commit v12 on v10

--- a/solution.py
+++ b/solution.py
@@ -97,8 +97,8 @@
     wide = jnp.pad(best.reshape(n_dp, capacity), ((0, 0), (0, LANES - capacity)))
     returned = lax.all_to_all(wide, "dp", split_axis=0, concat_axis=0, tiled=True)
     returned = returned[:, :capacity].reshape(slots)
-    pick = position[:, None] == jnp.arange(slots, dtype=jnp.int32)[None, :]
-    return jnp.sum(jnp.where(pick, returned[None, :], 0.0), axis=1)
+    pick = (position[:, None] == jnp.arange(slots, dtype=jnp.int32)[None, :]).astype(jnp.float32)
+    return jnp.dot(pick, returned, precision=lax.Precision.HIGHEST)
 
 
 def solution(mesh):

time: 92 us -> 92.1 us (level)
  no operation moved by 1% of the time
where the time goes in v12:
time: 92.1 us; the launch traced here: 91.7 us
  waiting for transfers between devices  45.6 us (50%)
  starting transfers between devices  37 us (40%)
  matrix products  3.79 us (4%)
  local copies, waits for them, and re-layouts  3.56 us (4%)
  other arithmetic  1.55 us (2%)
    all_to_all x1, waiting for transfers between devices, shards(): lax.all_to_all(send, 'dp', split_axis=0, concat_axis=0, tiled=True)  20 us
    all_to_all x1, starting transfers between devices, shards(): lax.all_to_all(send, 'dp', split_axis=0, concat_axis=0, tiled=True)  18.4 us
    ppermute x1, waiting for transfers between devices, shards(): got_l = lax.ppermute(block, 'owner', to_next)  12.4 us
    all_to_all x1, waiting for transfers between devices, shards(): lax.all_to_all(wide, 'dp', split_axis=0, concat_axis=0, tiled=True)  11.5 us
    all_to_all x1, starting transfers between devices, shards(): lax.all_to_all(wide, 'dp', split_axis=0, concat_axis=0, tiled=True)  10.3 us
    ppermute x1, starting transfers between devices, shards(): got_r = lax.ppermute(block, 'owner', to_prev)  4.39 us
    ppermute x1, starting transfers between devices, shards(): far_back = lax.ppermute(far, 'owner', to_prev)  1.92 us
    ppermute x1, starting transfers between devices, shards(): got_l = lax.ppermute(block, 'owner', to_next)  1.92 us
  transfers between devices with their start and end apart: 5, of which 4 were waited for; matrix products, arithmetic and copies ran while one was open for 2% of the time, Pallas kernels for 0%

profile of v12, /device:TPU:1, one launch (start us, length us, event | category | flops | bytes accessed | tf_op | source)
XLA Modules:
  0.0 91.7 jit_solution(18320986544809857683)
XLA Ops:
  0.0 0.0 copy-start
  0.0 0.7 compare_select_fusion.3
  0.7 0.2 convert_reduce_fusion
  0.9 1.3 %fusion.5 = f32[128]{0:T(128)S(1)} fusion(bf16[128,1024]{1,0:T(8,128)(2,1)} %param.3), kind=kOutput, calls=%fused_computation.12 | convolution fusion | flops 33603456 | bytes 262656 | tf_op jit(solution)/shard_map/dot_general | solution.py:21
  2.2 0.0 copy-done
  2.2 0.1 multiply_convert_fusion
  2.4 0.1 broadcast_select_fusion
  2.4 0.3 convolution_convert_fusion
  2.8 1.4 %copy.7 = bf16[128,2,1152]{2,1,0:T(2,128)(2,1)} copy(bf16[128,2,1152]{2,0,1:T(8,128)(2,1)S(1)} %convolution_convert_fusion) | data formatting | bytes 1179648 | tf_op jit(solution)/shard_map/convert_element_type | solution.py:42
  4.2 18.4 %all-to-all-start = ((bf16[128,2,1152]{2,1,0:T(2,128)(2,1)}), bf16[128,2,1152]{2,1,0:T(2,128)(2,1)S(1)}, u32[]{:S(2)}, u32[]{:S(2)}) async-start(bf16[128,2,1152]{2,1,0:T(2,128)(2,1)} %copy.7), calls=%async_computation | async-start | bytes 1179648 | tf_op jit(solution)/shard_map/all_to_all | solution.py:43
  22.6 0.8 fusion.29
  23.5 20.0 %all-to-all-done = bf16[128,2,1152]{2,1,0:T(2,128)(2,1)S(1)} async-done(((bf16[128,2,1152]{2,1,0:T(2,128)(2,1)}), bf16[128,2,1152]{2,1,0:T(2,128)(2,1)S(1)}, u32[]{:S(2)}, u32[]{:S(2)}) %all-to-all-start) | async-done | bytes 589856 | tf_op jit(solution)/shard_map/all_to_all | solution.py:43
  43.5 0.2 reshape.122
  43.7 0.1 slice_reduce_fusion
  43.9 0.1 slice.30
  44.0 4.4 %collective-permute-start.1 = (bf16[272,1024]{1,0:T(8,128)(2,1)S(1)}, bf16[272,1024]{1,0:T(8,128)(2,1)S(1)}, u32[]{:S(2)}, u32[]{:S(2)}) collective-permute-start(bf16[272,1024]{1,0:T(8,128)(2,1)S(1)} %fusion.6), channel_id=1, source_target_pairs={{0,3},{1,0},{2,1},{3,2},{4,7},{5,4},{6,5},{7,6},{8,11},{9,8},{10,9... | collective-permute-start | bytes 1671176 | tf_op jit(solution)/shard_map/ppermute | solution.py:56
  48.4 1.9 %collective-permute-start = (bf16[272,1024]{1,0:T(8,128)(2,1)S(1)}, bf16[272,1024]{1,0:T(8,128)(2,1)S(1)}, u32[]{:S(2)}, u32[]{:S(2)}) collective-permute-start(bf16[272,1024]{1,0:T(8,128)(2,1)S(1)} %fusion.6), channel_id=1, source_target_pairs={{0,1},{1,2},{2,3},{3,0},{4,5},{5,6},{6,7},{7,4},{8,9},{9,10},{10,1... | collective-permute-start | bytes 1671176 | tf_op jit(solution)/shard_map/ppermute | solution.py:55
  50.3 0.2 fusion.17
  50.5 0.1 select_reduce_fusion.1
  50.6 0.4 fusion
  50.9 12.4 %collective-permute-done = bf16[272,1024]{1,0:T(8,128)(2,1)S(1)} collective-permute-done((bf16[272,1024]{1,0:T(8,128)(2,1)S(1)}, bf16[272,1024]{1,0:T(8,128)(2,1)S(1)}, u32[]{:S(2)}, u32[]{:S(2)}) %collective-permute-start) | collective-permute-done | bytes 557088 | tf_op jit(solution)/shard_map/ppermute | solution.py:55
  63.3 0.1 select_reduce_fusion
  63.4 0.0 collective-permute-done.1
  63.4 0.4 fusion.3
  63.8 1.9 %collective-permute-start.2 = (f32[256]{0:T(256)S(1)}, f32[256]{0:T(256)S(1)}, u32[]{:S(2)}, u32[]{:S(2)}) collective-permute-start(f32[256]{0:T(256)S(1)} %fusion.3), channel_id=1, source_target_pairs={{0,3},{1,0},{2,1},{3,2},{4,7},{5,4},{6,5},{7,6},{8,11},{9,8},{10,9... | collective-permute-start | bytes 3080 | tf_op jit(solution)/shard_map/ppermute | solution.py:88
  65.7 0.4 fusion.2
  66.1 0.4 fusion.1
  66.4 1.7 %collective-permute-done.2 = f32[256]{0:T(256)S(1)} collective-permute-done((f32[256]{0:T(256)S(1)}, f32[256]{0:T(256)S(1)}, u32[]{:S(2)}, u32[]{:S(2)}) %collective-permute-start.2) | collective-permute-done | bytes 1056 | tf_op jit(solution)/shard_map/ppermute | solution.py:88
  68.1 0.1 reshape.123
  68.3 0.6 pad.9
  68.9 10.3 %all-to-all-start.1 = ((f32[128,1,128]{2,1,0:T(1,128)}), f32[128,1,128]{2,1,0:T(1,128)S(1)}, u32[]{:S(2)}, u32[]{:S(2)}) async-start(f32[128,1,128]{2,1,0:T(1,128)} %bitcast.4), calls=%async_computation.1 | async-start | bytes 131072 | tf_op jit(solution)/shard_map/all_to_all | solution.py:98
  79.3 11.5 %all-to-all-done.1 = f32[128,1,128]{2,1,0:T(1,128)S(1)} async-done(((f32[128,1,128]{2,1,0:T(1,128)}), f32[128,1,128]{2,1,0:T(1,128)S(1)}, u32[]{:S(2)}, u32[]{:S(2)}) %all-to-all-start.1) | async-done | bytes 65568 | tf_op jit(solution)/shard_map/all_to_all | solution.py:98
  90.8 0.1 reshape.126
  90.9 0.8 convolution_bitcast_fusion
  (12 shorter events, 0.2 us)
Async XLA Ops:
  0.0 2.2 %copy-start = (bf16[128,1024]{1,0:T(8,128)(2,1)S(1)}, bf16[128,1024]{1,0:T(8,128)(2,1)}, u32[]{:S(2)}) copy-start(bf16[128,1024]{1,0:T(8,128)(2,1)} %param.3) | copy-start | bytes 786436
  4.2 39.3 %all-to-all-start = ((bf16[128,2,1152]{2,1,0:T(2,128)(2,1)}), bf16[128,2,1152]{2,1,0:T(2,128)(2,1)S(1)}, u32[]{:S(2)}, u32[]{:S(2)}) async-start(bf16[128,2,1152]{2,1,0:T(2,128)(2,1)} %copy.7), calls=%async_computation | async-start | bytes 1179648 | tf_op jit(solution)/shard_map/all_to_all | solution.py:43
  44.0 19.4 %collective-permute-start.1 = (bf16[272,1024]{1,0:T(8,128)(2,1)S(1)}, bf16[272,1024]{1,0:T(8,128)(2,1)S(1)}, u32[]{:S(2)}, u32[]{:S(2)}) collective-permute-start(bf16[272,1024]{1,0:T(8,128)(2,1)S(1)} %fusion.6), channel_id=1, source_target_pairs={{0,3},{1,0},{2,1},{3,2},{4,7},{5,4},{6,5},{7,6},{8,11},{9,8},{10,9... | collective-permute-start | bytes 1671176 | tf_op jit(solution)/shard_map/ppermute | solution.py:56
  48.4 14.9 %collective-permute-start = (bf16[272,1024]{1,0:T(8,128)(2,1)S(1)}, bf16[272,1024]{1,0:T(8,128)(2,1)S(1)}, u32[]{:S(2)}, u32[]{:S(2)}) collective-permute-start(bf16[272,1024]{1,0:T(8,128)(2,1)S(1)} %fusion.6), channel_id=1, source_target_pairs={{0,1},{1,2},{2,3},{3,0},{4,5},{5,6},{6,7},{7,4},{8,9},{9,10},{10,1... | collective-permute-start | bytes 1671176 | tf_op jit(solution)/shard_map/ppermute | solution.py:55
  63.8 4.3 %collective-permute-start.2 = (f32[256]{0:T(256)S(1)}, f32[256]{0:T(256)S(1)}, u32[]{:S(2)}, u32[]{:S(2)}) collective-permute-start(f32[256]{0:T(256)S(1)} %fusion.3), channel_id=1, source_target_pairs={{0,3},{1,0},{2,1},{3,2},{4,7},{5,4},{6,5},{7,6},{8,11},{9,8},{10,9... | collective-permute-start | bytes 3080 | tf_op jit(solution)/shard_map/ppermute | solution.py:88
  68.9 21.9 %all-to-all-start.1 = ((f32[128,1,128]{2,1,0:T(1,128)}), f32[128,1,128]{2,1,0:T(1,128)S(1)}, u32[]{:S(2)}, u32[]{:S(2)}) async-start(f32[128,1,128]{2,1,0:T(1,128)} %bitcast.4), calls=%async_computation.1 | async-start | bytes 131072 | tf_op jit(solution)/shard_map/all_to_all | solution.py:98

commit v13 on v12

--- a/solution.py
+++ b/solution.py
@@ -14,7 +14,7 @@
     assert n_owner == 4
     capacity = 2 * rows // n_dp
     slots = capacity * n_dp
-    assert slots <= width
+    assert slots <= width and rows <= LANES
     here_owner = lax.axis_index("owner")
     here_dp = lax.axis_index("dp")
     values = embeddings.astype(jnp.float32)
@@ -32,7 +32,12 @@
 
     code = (assignment % CPD + 1).astype(jnp.bfloat16)
     lane = jnp.arange(LANES, dtype=jnp.int32)
-    extra = jnp.where(lane[None, :] == 0, code[:, None], jnp.zeros((), jnp.bfloat16))
+    row_index = jnp.arange(rows, dtype=jnp.int32).astype(jnp.bfloat16)
+    extra = jnp.where(
+        lane[None, :] == 0,
+        code[:, None],
+        jnp.where(lane[None, :] == 1, row_index[:, None], jnp.zeros((), jnp.bfloat16)),
+    )
     packed = jnp.concatenate([unit, extra], axis=1)
     place = (target[None, None, :] == jnp.arange(n_dp, dtype=jnp.int32)[:, None, None]) & (
         slot[None, None, :] == jnp.arange(capacity, dtype=jnp.int32)[None, :, None]
@@ -94,11 +99,12 @@
         ),
     )
     best = jnp.maximum(best, far_back)
-    wide = jnp.pad(best.reshape(n_dp, capacity), ((0, 0), (0, LANES - capacity)))
+    source_row = got[:, width + 1].astype(jnp.int32).reshape(n_dp, capacity, 1)
+    filled = (c1 > 0).reshape(n_dp, capacity, 1)
+    at_row = filled & (source_row == jnp.arange(LANES, dtype=jnp.int32)[None, None, :])
+    wide = jnp.max(jnp.where(at_row, best.reshape(n_dp, capacity, 1), -2.0), axis=1)
     returned = lax.all_to_all(wide, "dp", split_axis=0, concat_axis=0, tiled=True)
-    returned = returned[:, :capacity].reshape(slots)
-    pick = (position[:, None] == jnp.arange(slots, dtype=jnp.int32)[None, :]).astype(jnp.float32)
-    return jnp.dot(pick, returned, precision=lax.Precision.HIGHEST)
+    return jnp.max(returned[:, :rows], axis=0)
 
 
 def solution(mesh):

time: 92.1 us -> 91.2 us (level)
  blocking collectives: 0 us -> 21.7 us
  waiting for transfers between devices: 45.6 us -> 33.4 us
  starting transfers between devices: 37 us -> 26.6 us
  other arithmetic: 1.55 us -> 2.63 us
    all_to_all x0 -> x1, blocking collectives: none -> 21.7 us  [shards(): lax.all_to_all(wide, 'dp', split_axis=0, concat_axis=0, tiled=True)]
    all_to_all x1 -> x0, waiting for transfers between devices: 11.5 us -> none  [shards(): lax.all_to_all(wide, 'dp', split_axis=0, concat_axis=0, tiled=True)]
    all_to_all x1 -> x0, starting transfers between devices: 10.3 us -> none  [shards(): lax.all_to_all(wide, 'dp', split_axis=0, concat_axis=0, tiled=True)]
  transfers between devices with their start and end apart: 5 -> 4, of which waited for: 4 -> 3; matrix products, arithmetic and copies ran while one was open for 2% -> 3% of each run, Pallas kernels for 0% -> 0%
where the time goes in v13:
time: 91.2 us; the launch traced here: 90.9 us
  waiting for transfers between devices  33.4 us (37%)
  starting transfers between devices  26.6 us (29%)
  blocking collectives  21.7 us (24%)
  local copies, waits for them, and re-layouts  3.3 us (4%)
  matrix products  3.03 us (3%)
  other arithmetic  2.63 us (3%)
    all_to_all x1, blocking collectives, shards(): lax.all_to_all(wide, 'dp', split_axis=0, concat_axis=0, tiled=True)  21.7 us
    all_to_all x1, waiting for transfers between devices, shards(): lax.all_to_all(send, 'dp', split_axis=0, concat_axis=0, tiled=True)  20 us
    all_to_all x1, starting transfers between devices, shards(): lax.all_to_all(send, 'dp', split_axis=0, concat_axis=0, tiled=True)  18.4 us
    ppermute x1, waiting for transfers between devices, shards(): got_l = lax.ppermute(block, 'owner', to_next)  11.7 us
    ppermute x1, starting transfers between devices, shards(): got_r = lax.ppermute(block, 'owner', to_prev)  4.39 us
    ppermute x1, starting transfers between devices, shards(): far_back = lax.ppermute(far, 'owner', to_prev)  1.92 us
    ppermute x1, starting transfers between devices, shards(): got_l = lax.ppermute(block, 'owner', to_next)  1.92 us
  transfers between devices with their start and end apart: 4, of which 3 were waited for; matrix products, arithmetic and copies ran while one was open for 3% of the time, Pallas kernels for 0%

profile of v13, /device:TPU:1, one launch (start us, length us, event | category | flops | bytes accessed | tf_op | source)
XLA Modules:
  0.0 90.9 jit_solution(10760132635585272815)
XLA Ops:
  0.0 0.0 copy-start
  0.0 0.7 compare_select_fusion.3
  0.7 0.2 convert_reduce_fusion.1
  0.9 1.3 %fusion.5 = f32[128]{0:T(128)S(1)} fusion(bf16[128,1024]{1,0:T(8,128)(2,1)} %param.3), kind=kOutput, calls=%fused_computation.12 | convolution fusion | flops 33603456 | bytes 262656 | tf_op jit(solution)/shard_map/dot_general | solution.py:21
  2.2 0.0 copy-done
  2.2 0.1 multiply_convert_fusion
  2.3 0.1 select_select_fusion
  2.5 0.3 convolution_convert_fusion
  2.8 1.4 %copy.6 = bf16[128,2,1152]{2,1,0:T(2,128)(2,1)} copy(bf16[128,2,1152]{2,0,1:T(8,128)(2,1)S(1)} %convolution_convert_fusion) | data formatting | bytes 1179648 | tf_op jit(solution)/shard_map/convert_element_type | solution.py:47
  4.2 18.4 %all-to-all-start = ((bf16[128,2,1152]{2,1,0:T(2,128)(2,1)}), bf16[128,2,1152]{2,1,0:T(2,128)(2,1)S(1)}, u32[]{:S(2)}, u32[]{:S(2)}) async-start(bf16[128,2,1152]{2,1,0:T(2,128)(2,1)} %copy.6), calls=%async_computation | async-start | bytes 1179648 | tf_op jit(solution)/shard_map/all_to_all | solution.py:48
  22.7 0.8 fusion.30
  23.5 20.0 %all-to-all-done = bf16[128,2,1152]{2,1,0:T(2,128)(2,1)S(1)} async-done(((bf16[128,2,1152]{2,1,0:T(2,128)(2,1)}), bf16[128,2,1152]{2,1,0:T(2,128)(2,1)S(1)}, u32[]{:S(2)}, u32[]{:S(2)}) %all-to-all-start) | async-done | bytes 589856 | tf_op jit(solution)/shard_map/all_to_all | solution.py:48
  43.5 0.2 reshape.144
  43.8 0.1 slice_reduce_fusion
  43.9 0.1 slice.31
  44.0 4.4 %collective-permute-start.1 = (bf16[272,1024]{1,0:T(8,128)(2,1)S(1)}, bf16[272,1024]{1,0:T(8,128)(2,1)S(1)}, u32[]{:S(2)}, u32[]{:S(2)}) collective-permute-start(bf16[272,1024]{1,0:T(8,128)(2,1)S(1)} %fusion.6), channel_id=1, source_target_pairs={{0,3},{1,0},{2,1},{3,2},{4,7},{5,4},{6,5},{7,6},{8,11},{9,8},{10,9... | collective-permute-start | bytes 1671176 | tf_op jit(solution)/shard_map/ppermute | solution.py:61
  48.4 1.9 %collective-permute-start = (bf16[272,1024]{1,0:T(8,128)(2,1)S(1)}, bf16[272,1024]{1,0:T(8,128)(2,1)S(1)}, u32[]{:S(2)}, u32[]{:S(2)}) collective-permute-start(bf16[272,1024]{1,0:T(8,128)(2,1)S(1)} %fusion.6), channel_id=1, source_target_pairs={{0,1},{1,2},{2,3},{3,0},{4,5},{5,6},{6,7},{7,4},{8,9},{9,10},{10,1... | collective-permute-start | bytes 1671176 | tf_op jit(solution)/shard_map/ppermute | solution.py:60
  50.3 0.2 convert_reduce_fusion
  50.6 0.1 fusion.20
  50.7 0.1 reshape.145
  50.8 0.1 copy.8
  50.9 0.2 gt.40
  51.1 0.1 copy.7
  51.1 0.1 select_reduce_fusion.2
  51.2 0.4 fusion
  51.6 11.7 %collective-permute-done = bf16[272,1024]{1,0:T(8,128)(2,1)S(1)} collective-permute-done((bf16[272,1024]{1,0:T(8,128)(2,1)S(1)}, bf16[272,1024]{1,0:T(8,128)(2,1)S(1)}, u32[]{:S(2)}, u32[]{:S(2)}) %collective-permute-start) | collective-permute-done | bytes 557088 | tf_op jit(solution)/shard_map/ppermute | solution.py:60
  63.3 0.1 select_reduce_fusion.1
  63.4 0.0 collective-permute-done.1
  63.5 0.4 fusion.3
  63.8 1.9 %collective-permute-start.2 = (f32[256]{0:T(256)S(1)}, f32[256]{0:T(256)S(1)}, u32[]{:S(2)}, u32[]{:S(2)}) collective-permute-start(f32[256]{0:T(256)S(1)} %fusion.3), channel_id=1, source_target_pairs={{0,3},{1,0},{2,1},{3,2},{4,7},{5,4},{6,5},{7,6},{8,11},{9,8},{10,9... | collective-permute-start | bytes 3080 | tf_op jit(solution)/shard_map/ppermute | solution.py:93
  65.7 0.4 fusion.2
  66.1 0.4 fusion.1
  66.5 1.7 %collective-permute-done.2 = f32[256]{0:T(256)S(1)} collective-permute-done((f32[256]{0:T(256)S(1)}, f32[256]{0:T(256)S(1)}, u32[]{:S(2)}, u32[]{:S(2)}) %collective-permute-start.2) | collective-permute-done | bytes 1056 | tf_op jit(solution)/shard_map/ppermute | solution.py:93
  68.1 0.1 broadcast_in_dim.137
  68.3 0.1 copy.9
  68.3 0.2 select_reduce_fusion
  68.5 21.7 %all_to_all.14 = f32[128,1,128]{2,1,0:T(1,128)S(1)} all-to-all(f32[128,1,128]{2,1,0:T(1,128)S(1)} %bitcast.10), channel_id=1, replica_groups=mesh['dp'=128,'owner'=4] {'dp'}, dimensions={0} | all-to-all | bytes 131072 | tf_op jit(solution)/shard_map/all_to_all | solution.py:106
  90.2 0.7 reduce_max.59
  (11 shorter events, 0.2 us)
Async XLA Ops:
  0.0 2.2 %copy-start = (bf16[128,1024]{1,0:T(8,128)(2,1)S(1)}, bf16[128,1024]{1,0:T(8,128)(2,1)}, u32[]{:S(2)}) copy-start(bf16[128,1024]{1,0:T(8,128)(2,1)} %param.3) | copy-start | bytes 786436
  4.2 39.3 %all-to-all-start = ((bf16[128,2,1152]{2,1,0:T(2,128)(2,1)}), bf16[128,2,1152]{2,1,0:T(2,128)(2,1)S(1)}, u32[]{:S(2)}, u32[]{:S(2)}) async-start(bf16[128,2,1152]{2,1,0:T(2,128)(2,1)} %copy.6), calls=%async_computation | async-start | bytes 1179648 | tf_op jit(solution)/shard_map/all_to_all | solution.py:48
  44.0 19.4 %collective-permute-start.1 = (bf16[272,1024]{1,0:T(8,128)(2,1)S(1)}, bf16[272,1024]{1,0:T(8,128)(2,1)S(1)}, u32[]{:S(2)}, u32[]{:S(2)}) collective-permute-start(bf16[272,1024]{1,0:T(8,128)(2,1)S(1)} %fusion.6), channel_id=1, source_target_pairs={{0,3},{1,0},{2,1},{3,2},{4,7},{5,4},{6,5},{7,6},{8,11},{9,8},{10,9... | collective-permute-start | bytes 1671176 | tf_op jit(solution)/shard_map/ppermute | solution.py:61
  48.4 14.9 %collective-permute-start = (bf16[272,1024]{1,0:T(8,128)(2,1)S(1)}, bf16[272,1024]{1,0:T(8,128)(2,1)S(1)}, u32[]{:S(2)}, u32[]{:S(2)}) collective-permute-start(bf16[272,1024]{1,0:T(8,128)(2,1)S(1)} %fusion.6), channel_id=1, source_target_pairs={{0,1},{1,2},{2,3},{3,0},{4,5},{5,6},{6,7},{7,4},{8,9},{9,10},{10,1... | collective-permute-start | bytes 1671176 | tf_op jit(solution)/shard_map/ppermute | solution.py:60
  63.8 4.3 %collective-permute-start.2 = (f32[256]{0:T(256)S(1)}, f32[256]{0:T(256)S(1)}, u32[]{:S(2)}, u32[]{:S(2)}) collective-permute-start(f32[256]{0:T(256)S(1)} %fusion.3), channel_id=1, source_target_pairs={{0,3},{1,0},{2,1},{3,2},{4,7},{5,4},{6,5},{7,6},{8,11},{9,8},{10,9... | collective-permute-start | bytes 3080 | tf_op jit(solution)/shard_map/ppermute | solution.py:93

commit v14 on v13

--- a/solution.py
+++ b/solution.py
@@ -4,6 +4,7 @@
 from jax.sharding import PartitionSpec as P
 
 CPD = 16
+assert CPD & (CPD - 1) == 0
 LANES = 128
 
 
@@ -24,13 +25,15 @@
     order = jnp.arange(rows, dtype=jnp.int32)
     squares = jnp.sum(jnp.where(order[:, None] == order[None, :], gram, 0.0), axis=1)
     unit = (values * lax.rsqrt(squares + 1e-06)[:, None]).astype(jnp.bfloat16)
-    target = lax.div(assignment, n_owner * CPD)
+    group = n_owner * CPD
+    assert group & (group - 1) == 0
+    target = lax.shift_right_logical(assignment, group.bit_length() - 1)
     earlier = (target[:, None] == target[None, :]) & (order[None, :] < order[:, None])
     slot = jnp.sum(earlier.astype(jnp.int32), axis=1)
     position = target * capacity + slot
     first_id = (here_dp * n_owner + here_owner) * CPD
 
-    code = (assignment % CPD + 1).astype(jnp.bfloat16)
+    code = (jnp.bitwise_and(assignment, CPD - 1) + 1).astype(jnp.bfloat16)
     lane = jnp.arange(LANES, dtype=jnp.int32)
     row_index = jnp.arange(rows, dtype=jnp.int32).astype(jnp.bfloat16)
     extra = jnp.where(

time: 91.2 us -> 91.2 us (level)
  no operation moved by 1% of the time
where the time goes in v14:
time: 91.2 us; the launch traced here: 90.9 us
  waiting for transfers between devices  33.4 us (37%)
  starting transfers between devices  26.6 us (29%)
  blocking collectives  21.7 us (24%)
  local copies, waits for them, and re-layouts  3.3 us (4%)
  matrix products  3.03 us (3%)
  other arithmetic  2.62 us (3%)
    all_to_all x1, blocking collectives, shards(): lax.all_to_all(wide, 'dp', split_axis=0, concat_axis=0, tiled=True)  21.7 us
    all_to_all x1, waiting for transfers between devices, shards(): lax.all_to_all(send, 'dp', split_axis=0, concat_axis=0, tiled=True)  20 us
    all_to_all x1, starting transfers between devices, shards(): lax.all_to_all(send, 'dp', split_axis=0, concat_axis=0, tiled=True)  18.4 us
    ppermute x1, waiting for transfers between devices, shards(): got_l = lax.ppermute(block, 'owner', to_next)  11.7 us
    ppermute x1, starting transfers between devices, shards(): got_r = lax.ppermute(block, 'owner', to_prev)  4.39 us
    ppermute x1, starting transfers between devices, shards(): got_l = lax.ppermute(block, 'owner', to_next)  1.92 us
    ppermute x1, starting transfers between devices, shards(): far_back = lax.ppermute(far, 'owner', to_prev)  1.92 us
  transfers between devices with their start and end apart: 4, of which 3 were waited for; matrix products, arithmetic and copies ran while one was open for 3% of the time, Pallas kernels for 0%

profile of v14, /device:TPU:1, one launch (start us, length us, event | category | flops | bytes accessed | tf_op | source)
XLA Modules:
  0.0 90.9 jit_solution(43403383719605518)
XLA Ops:
  0.0 0.0 copy-start
  0.0 0.7 broadcast_shift-right-logical_fusion
  0.7 0.2 convert_reduce_fusion.1
  0.9 1.3 %fusion.5 = f32[128]{0:T(128)S(1)} fusion(bf16[128,1024]{1,0:T(8,128)(2,1)} %param.3), kind=kOutput, calls=%fused_computation.12 | convolution fusion | flops 33603456 | bytes 262656 | tf_op jit(solution)/shard_map/dot_general | solution.py:22
  2.2 0.0 copy-done
  2.2 0.1 multiply_convert_fusion
  2.3 0.1 select_select_fusion
  2.5 0.3 convolution_convert_fusion
  2.8 1.4 %copy.6 = bf16[128,2,1152]{2,1,0:T(2,128)(2,1)} copy(bf16[128,2,1152]{2,0,1:T(8,128)(2,1)S(1)} %convolution_convert_fusion) | data formatting | bytes 1179648 | tf_op jit(solution)/shard_map/convert_element_type | solution.py:50
  4.2 18.4 %all-to-all-start = ((bf16[128,2,1152]{2,1,0:T(2,128)(2,1)}), bf16[128,2,1152]{2,1,0:T(2,128)(2,1)S(1)}, u32[]{:S(2)}, u32[]{:S(2)}) async-start(bf16[128,2,1152]{2,1,0:T(2,128)(2,1)} %copy.6), calls=%async_computation | async-start | bytes 1179648 | tf_op jit(solution)/shard_map/all_to_all | solution.py:51
  22.6 0.8 fusion.28
  23.5 20.0 %all-to-all-done = bf16[128,2,1152]{2,1,0:T(2,128)(2,1)S(1)} async-done(((bf16[128,2,1152]{2,1,0:T(2,128)(2,1)}), bf16[128,2,1152]{2,1,0:T(2,128)(2,1)S(1)}, u32[]{:S(2)}, u32[]{:S(2)}) %all-to-all-start) | async-done | bytes 589856 | tf_op jit(solution)/shard_map/all_to_all | solution.py:51
  43.5 0.2 reshape.144
  43.8 0.1 slice_reduce_fusion
  43.9 0.1 slice.31
  44.0 4.4 %collective-permute-start.1 = (bf16[272,1024]{1,0:T(8,128)(2,1)S(1)}, bf16[272,1024]{1,0:T(8,128)(2,1)S(1)}, u32[]{:S(2)}, u32[]{:S(2)}) collective-permute-start(bf16[272,1024]{1,0:T(8,128)(2,1)S(1)} %fusion.6), channel_id=1, source_target_pairs={{0,3},{1,0},{2,1},{3,2},{4,7},{5,4},{6,5},{7,6},{8,11},{9,8},{10,9... | collective-permute-start | bytes 1671176 | tf_op jit(solution)/shard_map/ppermute | solution.py:64
  48.4 1.9 %collective-permute-start = (bf16[272,1024]{1,0:T(8,128)(2,1)S(1)}, bf16[272,1024]{1,0:T(8,128)(2,1)S(1)}, u32[]{:S(2)}, u32[]{:S(2)}) collective-permute-start(bf16[272,1024]{1,0:T(8,128)(2,1)S(1)} %fusion.6), channel_id=1, source_target_pairs={{0,1},{1,2},{2,3},{3,0},{4,5},{5,6},{6,7},{7,4},{8,9},{9,10},{10,1... | collective-permute-start | bytes 1671176 | tf_op jit(solution)/shard_map/ppermute | solution.py:63
  50.3 0.2 convert_reduce_fusion
  50.5 0.1 fusion.20
  50.7 0.1 reshape.145
  50.8 0.1 copy.8
  50.9 0.2 gt.40
  51.1 0.1 copy.7
  51.1 0.1 select_reduce_fusion.2
  51.2 0.4 fusion
  51.6 11.7 %collective-permute-done = bf16[272,1024]{1,0:T(8,128)(2,1)S(1)} collective-permute-done((bf16[272,1024]{1,0:T(8,128)(2,1)S(1)}, bf16[272,1024]{1,0:T(8,128)(2,1)S(1)}, u32[]{:S(2)}, u32[]{:S(2)}) %collective-permute-start) | collective-permute-done | bytes 557088 | tf_op jit(solution)/shard_map/ppermute | solution.py:63
  63.3 0.1 select_reduce_fusion.1
  63.4 0.0 collective-permute-done.1
  63.4 0.4 fusion.3
  63.8 1.9 %collective-permute-start.2 = (f32[256]{0:T(256)S(1)}, f32[256]{0:T(256)S(1)}, u32[]{:S(2)}, u32[]{:S(2)}) collective-permute-start(f32[256]{0:T(256)S(1)} %fusion.3), channel_id=1, source_target_pairs={{0,3},{1,0},{2,1},{3,2},{4,7},{5,4},{6,5},{7,6},{8,11},{9,8},{10,9... | collective-permute-start | bytes 3080 | tf_op jit(solution)/shard_map/ppermute | solution.py:96
  65.7 0.4 fusion.2
  66.1 0.4 fusion.1
  66.5 1.7 %collective-permute-done.2 = f32[256]{0:T(256)S(1)} collective-permute-done((f32[256]{0:T(256)S(1)}, f32[256]{0:T(256)S(1)}, u32[]{:S(2)}, u32[]{:S(2)}) %collective-permute-start.2) | collective-permute-done | bytes 1056 | tf_op jit(solution)/shard_map/ppermute | solution.py:96
  68.1 0.1 broadcast_in_dim.137
  68.3 0.1 copy.9
  68.3 0.2 select_reduce_fusion
  68.5 21.7 %all_to_all.14 = f32[128,1,128]{2,1,0:T(1,128)S(1)} all-to-all(f32[128,1,128]{2,1,0:T(1,128)S(1)} %bitcast.10), channel_id=1, replica_groups=mesh['dp'=128,'owner'=4] {'dp'}, dimensions={0} | all-to-all | bytes 131072 | tf_op jit(solution)/shard_map/all_to_all | solution.py:109
  90.2 0.7 reduce_max.59
  (11 shorter events, 0.2 us)
Async XLA Ops:
  0.0 2.2 %copy-start = (bf16[128,1024]{1,0:T(8,128)(2,1)S(1)}, bf16[128,1024]{1,0:T(8,128)(2,1)}, u32[]{:S(2)}) copy-start(bf16[128,1024]{1,0:T(8,128)(2,1)} %param.3) | copy-start | bytes 786436
  4.2 39.3 %all-to-all-start = ((bf16[128,2,1152]{2,1,0:T(2,128)(2,1)}), bf16[128,2,1152]{2,1,0:T(2,128)(2,1)S(1)}, u32[]{:S(2)}, u32[]{:S(2)}) async-start(bf16[128,2,1152]{2,1,0:T(2,128)(2,1)} %copy.6), calls=%async_computation | async-start | bytes 1179648 | tf_op jit(solution)/shard_map/all_to_all | solution.py:51
  44.0 19.4 %collective-permute-start.1 = (bf16[272,1024]{1,0:T(8,128)(2,1)S(1)}, bf16[272,1024]{1,0:T(8,128)(2,1)S(1)}, u32[]{:S(2)}, u32[]{:S(2)}) collective-permute-start(bf16[272,1024]{1,0:T(8,128)(2,1)S(1)} %fusion.6), channel_id=1, source_target_pairs={{0,3},{1,0},{2,1},{3,2},{4,7},{5,4},{6,5},{7,6},{8,11},{9,8},{10,9... | collective-permute-start | bytes 1671176 | tf_op jit(solution)/shard_map/ppermute | solution.py:64
  48.4 14.9 %collective-permute-start = (bf16[272,1024]{1,0:T(8,128)(2,1)S(1)}, bf16[272,1024]{1,0:T(8,128)(2,1)S(1)}, u32[]{:S(2)}, u32[]{:S(2)}) collective-permute-start(bf16[272,1024]{1,0:T(8,128)(2,1)S(1)} %fusion.6), channel_id=1, source_target_pairs={{0,1},{1,2},{2,3},{3,0},{4,5},{5,6},{6,7},{7,4},{8,9},{9,10},{10,1... | collective-permute-start | bytes 1671176 | tf_op jit(solution)/shard_map/ppermute | solution.py:63
  63.8 4.3 %collective-permute-start.2 = (f32[256]{0:T(256)S(1)}, f32[256]{0:T(256)S(1)}, u32[]{:S(2)}, u32[]{:S(2)}) collective-permute-start(f32[256]{0:T(256)S(1)} %fusion.3), channel_id=1, source_target_pairs={{0,3},{1,0},{2,1},{3,2},{4,7},{5,4},{6,5},{7,6},{8,11},{9,8},{10,9... | collective-permute-start | bytes 3080 | tf_op jit(solution)/shard_map/ppermute | solution.py:96
